TPU v7x, 512 devices: a whole 4x4x16 slice. The times are simulated.
512 devices in a mesh: gx: 32 (over z, core), gy: 4 (over y), gz: 4 (over x).
Axes of the slice: x: 4, y: 4, z: 16, core: 2. Of those that a mesh axis runs over, the one named last changes fastest.
Arguments:
- saturation: float32 [64, 512, 512], P('gz', 'gx', 'gy'), may hold values from 0.05 to 0.95
- retention: float32 [64, 512, 512], P('gz', 'gx', 'gy'), may hold values from 0 to 1
- gravity: float32 [64, 512, 512], P('gz', 'gx', 'gy'), may hold values from 0.02 to 0.2
- cell_map: int32 [4, 32768, 128], P('gz', ('gx', 'gy')), may hold values from 0 to 1023
- owner_id: int32 [4, 16384, 1], P('gz', ('gx', 'gy')), may hold values from 0 to 127; in each aligned block of 128 rows (0 to 127, 128 to 255, ..., all dimensions but the last counted through in order) at most 2 rows name the same one
- stream_dir: int32 [4, 8192], P('gz', ('gx', 'gy')), may hold values 0 or 1
- node_weight: float32 [4, 16384, 128], P('gz', ('gx', 'gy')), may hold values from 0.25 to 4
- flight: float32 [4, 16384, 128], P('gz', ('gx', 'gy')), may hold values from 0.1 to 0.45
Outputs:
- final_sat: float32 [64, 512, 512], P('gz', 'gx', 'gy')
- streamline_sat: float32 [4, 16384, 128], P('gz', ('gx', 'gy'))
Inputs may be any that keep to these rules, and one draw needn't show every extreme that they name: `owner_id`: among the 128 segments of one device no owner is named more than 2 times; some owner exactly 2 times.
All inputs are finite; a program needn't handle non-finite values. No bound on the sum of `stream_dir` on one device may be relied on, other than what follows from the above.
Results may differ from a plain program's by a relative error of at most 0.00005.
Values sent between devices are 32-bit elements; how exact they have to be, the bound alone decides.
No kernel may reach another device: no remote copies, remote signals or barrier semaphores. Data moves between devices by JAX's collectives and lax.ppermute only.
A program may use at most 64 MiB of HBM per device.

v0:
```python
import math

import jax
import jax.numpy as jnp
from jax import lax
from jax.sharding import PartitionSpec as P

BL_STEPS = 8


def from_behind(block, axis, distance):
    devices = range(lax.axis_size(axis))
    route = [(i - distance, i) for i in devices if i - distance in devices]
    return lax.ppermute(block, axis, route)


def frac_flow(values):
    return values * values / (values * values + (1.0 - values) * (1.0 - values))


def transport(node_sat, increments, reversed_flag):
    flipped = reversed_flag[..., None] == 1
    state = jnp.where(flipped, node_sat[..., ::-1], node_sat)
    ratio = jnp.where(flipped, increments[..., ::-1], increments)
    inlet = jnp.ones(state.shape[:-1] + (1,), jnp.float32)
    for iteration in range(BL_STEPS):
        flows = frac_flow(state)
        upstream = jnp.concatenate([inlet, flows[..., :-1]], axis=-1)
        state = state - ratio * (flows - upstream)
    return jnp.where(flipped, state[..., ::-1], state)


def slot_rows(owners, groups, capacity):
    onehot = (owners[:, None] == jnp.arange(groups, dtype=jnp.int32)[None, :]).astype(jnp.int32)
    before = jnp.cumsum(onehot, axis=0) - onehot
    return owners * capacity + jnp.sum(before * onehot, axis=1)


def descend(carried, layer):
    keep, drop = layer
    inflow = keep * carried
    return (inflow + drop, inflow)


def column_hot(cell_ids):
    lanes = lax.broadcasted_iota(jnp.int32, (128, cell_ids.shape[0]), 0)
    return (cell_ids[None, :] % 128 == lanes).astype(jnp.float32)


def row_hot(cell_ids, map_rows):
    levels = lax.broadcasted_iota(jnp.int32, (map_rows, cell_ids.shape[0]), 0)
    return (cell_ids[None, :] // 128 == levels).astype(jnp.float32)


def on_device(saturation, retention, gravity, cell_map, owner_id, stream_dir, node_weight, flight):
    layers, rows_x, rows_y = saturation.shape
    size_x = lax.axis_size("gx")
    size_y = lax.axis_size("gy")
    groups = size_x * size_y
    seg_len = cell_map.shape[2]
    capacity = cell_map.shape[1] // groups
    flat = saturation.reshape(-1)
    cell_count = flat.shape[0]
    map_rows = min(cell_count // 128, max(8, capacity * seg_len // 32))
    local_map = cell_map[0]
    node_total = local_map.shape[0] * seg_len
    block_width = math.gcd(node_total, 2048)
    block_count = node_total // block_width
    block_ids = local_map.reshape(block_count, block_width)
    cell_table = flat[: map_rows * 128].reshape(map_rows, 128)

    def pick_block(cell_ids):
        by_rows = jnp.dot(
            cell_table,
            column_hot(cell_ids),
            precision=lax.Precision.HIGHEST,
            preferred_element_type=jnp.float32,
        )
        return jnp.sum(by_rows * row_hot(cell_ids, map_rows), axis=0)

    offered = lax.map(pick_block, block_ids).reshape(local_map.shape)
    arrived = lax.all_to_all(offered, ("gx", "gy"), split_axis=0, concat_axis=0, tiled=True)
    burden = gravity * saturation * (1.0 - saturation)
    zero_plane = jnp.zeros((rows_x, rows_y), jnp.float32)
    local_end, _ = lax.scan(descend, zero_plane, (retention, burden))
    through = jnp.prod(retention, axis=0)

    def relay(counter, entering):
        return from_behind(through * entering + local_end, "gz", 1)

    entering = lax.fori_loop(0, lax.axis_size("gz") - 1, relay, zero_plane)
    _, inflow = lax.scan(descend, entering, (retention, burden))
    owners = owner_id[0, :, 0]
    rows = slot_rows(owners, groups, capacity)
    node_in = arrived[rows]
    seg_dev = node_in.shape[0]
    updated = transport(
        node_in.reshape(seg_dev // 2, 2 * seg_len),
        flight[0].reshape(seg_dev // 2, 2 * seg_len),
        stream_dir[0],
    )
    updated = updated.reshape(seg_dev, seg_len)
    weights = node_weight[0]
    package = (
        jnp.zeros((groups * capacity, 2, seg_len), jnp.float32)
        .at[rows]
        .set(jnp.stack([weights * updated, weights], axis=1))
    )
    returned = lax.all_to_all(package, ("gx", "gy"), split_axis=0, concat_axis=0, tiled=True)
    weighted_sat = returned[:, 0, :].reshape(block_count, block_width)
    weight_only = returned[:, 1, :].reshape(block_count, block_width)

    def add_block(totals, block):
        cell_ids, upper, lower = block
        levels = row_hot(cell_ids, map_rows)
        stacked = jnp.concatenate([levels * upper[None, :], levels * lower[None, :]], axis=0)
        added = lax.dot_general(
            stacked,
            column_hot(cell_ids),
            (((1,), (1,)), ((), ())),
            precision=lax.Precision.HIGHEST,
            preferred_element_type=jnp.float32,
        )
        return (totals + added, None)

    sums, _ = lax.scan(
        add_block,
        jnp.zeros((2 * map_rows, 128), jnp.float32),
        (block_ids, weighted_sat, weight_only),
    )
    padding = jnp.zeros((cell_count - map_rows * 128,), jnp.float32)
    numerator = jnp.concatenate([sums[:map_rows].reshape(-1), padding])
    denominator = jnp.concatenate([sums[map_rows:].reshape(-1), padding])
    mixed = ((flat + numerator) / (1.0 + denominator)).reshape(layers, rows_x, rows_y)
    final_sat = mixed + inflow - burden
    return (final_sat, updated[None])


def solution(mesh):
    return jax.shard_map(
        on_device,
        mesh=mesh,
        in_specs=(
            P("gz", "gx", "gy"),
            P("gz", "gx", "gy"),
            P("gz", "gx", "gy"),
            P("gz", ("gx", "gy"), None),
            P("gz", ("gx", "gy"), None),
            P("gz", ("gx", "gy")),
            P("gz", ("gx", "gy"), None),
            P("gz", ("gx", "gy"), None),
        ),
        out_specs=(P("gz", "gx", "gy"), P("gz", ("gx", "gy"), None)),
        check_vma=False,
    )
```

profile of v0, /device:TPU:1, one launch (start us, length us, event | category | flops | bytes accessed | tf_op | source)
XLA Modules:
  0.0 111.6 jit_solution(316056352617969704)
XLA Ops:
  0.7 1.0 reshape_squeeze.12
  1.6 12.0 %while.58 = (s32[]{:T(128)}, f32[16,2048]{1,0:T(8,128)S(1)}, s32[16,2048]{1,0:T(8,128)S(1)}, f32[8,128]{1,0:T(8,128)S(1)}, s32[]{:T(128)}, /*index=5*/s32[]{:T(128)}) while((s32[]{:T(128)}, f32[16,2048]{1,0:T(8,128)S(1)}, s32[16,2048]{1,0:T(8,128)S(1)}, f32[8,128]{1,0:T(8,128)S(1)}, s32[]{:T(128)}, /*index=5*/s32[]{:T(128)}) %tuple.117), condition=%wide.region_4.5_spmd, body=%wide.region_2.4_spmd.sunk | while | flops 25516032 | bytes 86093 | solution.py:81
  1.7 0.4 fusion.18
  2.5 0.4 fusion.18
  5.5 0.4 fusion.18
  13.7 0.8 all_to_all.11
  14.5 20.6 %all-to-all-start = ((f32[128,2,128]{2,1,0:T(2,128)}), f32[128,2,128]{2,1,0:T(2,128)S(1)}, u32[]{:S(2)}, u32[]{:S(2)}) async-start(f32[128,2,128]{2,1,0:T(2,128)} %all_to_all.11), calls=%async_computation | async-start | bytes 262144 | tf_op jit(solution)/shard_map/all_to_all | solution.py:82
  35.1 0.6 copy-done.5
  36.1 0.7 copy-done.4
  37.0 0.7 copy-done.3
  37.7 0.9 copy-done.1
  38.6 0.5 while.62
  39.2 0.6 copy-done.6
  39.8 13.3 %all-to-all-done = f32[128,2,128]{2,1,0:T(2,128)S(1)} async-done(((f32[128,2,128]{2,1,0:T(2,128)}), f32[128,2,128]{2,1,0:T(2,128)S(1)}, u32[]{:S(2)}, u32[]{:S(2)}) %all-to-all-start) | async-done | bytes 131104 | tf_op jit(solution)/shard_map/all_to_all | solution.py:82
  53.1 0.6 gather_fusion
  55.3 0.8 copy-done.2
  56.3 0.8 broadcast_in_dim.45
  57.0 12.4 %scatter_fusion = f32[256,2,128]{2,1,0:T(2,128)} fusion(f32[256,2,128]{2,1,0:T(2,128)} %broadcast_in_dim.45, s32[128]{0:T(128)S(1)} %fusion.11, f32[128,2,128]{2,1,0:T(2,128)S(1)} %copy.10), kind=kCustom, calls=%fused_computation.1 | custom fusion | bytes 393728 | tf_op jit(solution)/shard_map/scatter | solution.py:107
  69.5 5.3 %all-to-all-start.1 = ((f32[256,2,128]{2,1,0:T(2,128)}), f32[256,2,128]{2,1,0:T(2,128)S(1)}, u32[]{:S(2)}, u32[]{:S(2)}) async-start(f32[256,2,128]{2,1,0:T(2,128)} %scatter_fusion), calls=%async_computation.1 | async-start | bytes 524288 | tf_op jit(solution)/shard_map/all_to_all | solution.py:109
  74.7 13.3 %while.59 = (s32[]{:T(128)}, f32[16,128]{1,0:T(8,128)S(1)}, f32[16,128]{1,0:T(8,128)S(1)}, f32[16,128]{1,0:T(8,128)S(1)}, s32[]{:T(128)}) while((s32[]{:T(128)}, f32[16,128]{1,0:T(8,128)S(1)}, f32[16,128]{1,0:T(8,128)S(1)}, f32[16,128]{1,0:T(8,128)S(1)}, s32[]{:T(128)}) %tuple.126), condition=%wide.region_12.13_spmd, body=%wide.region_11.12_spmd.sunk | while | flops 4098 | bytes 65637 | solution.py:91
  74.8 3.1 %collective-permute-start = (f32[16,128]{1,0:T(8,128)S(1)}, f32[16,128]{1,0:T(8,128)S(1)}, u32[]{:S(2)}, u32[]{:S(2)}) collective-permute-start(f32[16,128]{1,0:T(8,128)S(1)} %multiply_add_fusion.2), channel_id=1, source_target_pairs={{0,1},{1,2},{2,3},{4,5},{5,6},{6,7},{8,9},{9,10},{10,11},{12,13},{... | collective-permute-start | bytes 24584 | tf_op jit(solution)/shard_map/while/body/eval_jaxpr/ppermute | solution.py:14
  77.9 0.8 collective-permute-done
  78.7 3.9 %collective-permute-start = (f32[16,128]{1,0:T(8,128)S(1)}, f32[16,128]{1,0:T(8,128)S(1)}, u32[]{:S(2)}, u32[]{:S(2)}) collective-permute-start(f32[16,128]{1,0:T(8,128)S(1)} %multiply_add_fusion.2), channel_id=1, source_target_pairs={{0,1},{1,2},{2,3},{4,5},{5,6},{6,7},{8,9},{9,10},{10,11},{12,13},{... | collective-permute-start | bytes 24584 | tf_op jit(solution)/shard_map/while/body/eval_jaxpr/ppermute | solution.py:14
  82.6 0.8 collective-permute-done
  83.4 3.9 %collective-permute-start = (f32[16,128]{1,0:T(8,128)S(1)}, f32[16,128]{1,0:T(8,128)S(1)}, u32[]{:S(2)}, u32[]{:S(2)}) collective-permute-start(f32[16,128]{1,0:T(8,128)S(1)} %multiply_add_fusion.2), channel_id=1, source_target_pairs={{0,1},{1,2},{2,3},{4,5},{5,6},{6,7},{8,9},{9,10},{10,11},{12,13},{... | collective-permute-start | bytes 24584 | tf_op jit(solution)/shard_map/while/body/eval_jaxpr/ppermute | solution.py:14
  87.3 0.8 collective-permute-done
  88.1 0.8 while.60
  88.8 0.6 broadcast_in_dim_reshape.3
  89.5 8.5 %all-to-all-done.1 = f32[256,2,128]{2,1,0:T(2,128)S(1)} async-done(((f32[256,2,128]{2,1,0:T(2,128)}), f32[256,2,128]{2,1,0:T(2,128)S(1)}, u32[]{:S(2)}, u32[]{:S(2)}) %all-to-all-start.1) | async-done | bytes 262176 | tf_op jit(solution)/shard_map/all_to_all | solution.py:109
  98.0 0.7 slice_reduce_fusion
  98.7 12.2 %while.61 = (s32[]{:T(128)}, f32[16,128]{1,0:T(8,128)S(1)}, s32[16,2048]{1,0:T(8,128)S(1)}, f32[16,2048]{1,0:T(8,128)S(1)}, f32[16,2048]{1,0:T(8,128)S(1)}, /*index=5*/s32[]{:T(128)}, s32[]{:T(128)}) while((s32[]{:T(128)}, f32[16,128]{1,0:T(8,128)S(1)}, s32[16,2048]{1,0:T(8,128)S(1)}, f32[16,2048]{1,0:T(8,128)S(1)}, ...), condition=%wide.region_7.8_spmd.clone, body=%wide.region_6.7_spmd.clone.sunk | while | flops 50720768 | bytes 385119 | solution.py:126
  98.9 0.6 convolution_add_fusion.2
  99.6 0.6 convolution_add_fusion.2
  100.4 0.6 convolution_add_fusion.2
  101.2 0.6 convolution_add_fusion.2
  101.9 0.6 convolution_add_fusion.2
  102.7 0.6 convolution_add_fusion.2
  103.4 0.6 convolution_add_fusion.2
  104.2 0.6 convolution_add_fusion.2
  105.0 0.6 convolution_add_fusion.2
  105.7 0.6 convolution_add_fusion.2
  106.5 0.6 convolution_add_fusion.2
  107.2 0.6 convolution_add_fusion.2
  108.0 0.6 convolution_add_fusion.2
  108.8 0.6 convolution_add_fusion.2
  109.5 0.6 convolution_add_fusion.2
  110.3 0.6 convolution_add_fusion.2
  110.9 0.7 add_subtract_fusion
  (221 shorter events, 14.5 us)
Async XLA Ops:
  0.6 1.0 copy-start
  14.5 38.7 %all-to-all-start = ((f32[128,2,128]{2,1,0:T(2,128)}), f32[128,2,128]{2,1,0:T(2,128)S(1)}, u32[]{:S(2)}, u32[]{:S(2)}) async-start(f32[128,2,128]{2,1,0:T(2,128)} %all_to_all.11), calls=%async_computation | async-start | bytes 262144 | tf_op jit(solution)/shard_map/all_to_all | solution.py:82
  35.0 0.7 copy-start.5
  36.0 0.8 copy-start.4
  36.8 0.9 copy-start.3
  37.7 0.9 copy-start.1
  39.1 0.7 copy-start.6
  55.3 0.8 copy-start.2
  69.5 28.5 %all-to-all-start.1 = ((f32[256,2,128]{2,1,0:T(2,128)}), f32[256,2,128]{2,1,0:T(2,128)S(1)}, u32[]{:S(2)}, u32[]{:S(2)}) async-start(f32[256,2,128]{2,1,0:T(2,128)} %scatter_fusion), calls=%async_computation.1 | async-start | bytes 524288 | tf_op jit(solution)/shard_map/all_to_all | solution.py:109
  74.8 3.9 %collective-permute-start = (f32[16,128]{1,0:T(8,128)S(1)}, f32[16,128]{1,0:T(8,128)S(1)}, u32[]{:S(2)}, u32[]{:S(2)}) collective-permute-start(f32[16,128]{1,0:T(8,128)S(1)} %multiply_add_fusion.2), channel_id=1, source_target_pairs={{0,1},{1,2},{2,3},{4,5},{5,6},{6,7},{8,9},{9,10},{10,11},{12,13},{... | collective-permute-start | bytes 24584 | tf_op jit(solution)/shard_map/while/body/eval_jaxpr/ppermute | solution.py:14
  78.7 4.7 %collective-permute-start = (f32[16,128]{1,0:T(8,128)S(1)}, f32[16,128]{1,0:T(8,128)S(1)}, u32[]{:S(2)}, u32[]{:S(2)}) collective-permute-start(f32[16,128]{1,0:T(8,128)S(1)} %multiply_add_fusion.2), channel_id=1, source_target_pairs={{0,1},{1,2},{2,3},{4,5},{5,6},{6,7},{8,9},{9,10},{10,11},{12,13},{... | collective-permute-start | bytes 24584 | tf_op jit(solution)/shard_map/while/body/eval_jaxpr/ppermute | solution.py:14
  83.4 4.7 %collective-permute-start = (f32[16,128]{1,0:T(8,128)S(1)}, f32[16,128]{1,0:T(8,128)S(1)}, u32[]{:S(2)}, u32[]{:S(2)}) collective-permute-start(f32[16,128]{1,0:T(8,128)S(1)} %multiply_add_fusion.2), channel_id=1, source_target_pairs={{0,1},{1,2},{2,3},{4,5},{5,6},{6,7},{8,9},{9,10},{10,11},{12,13},{... | collective-permute-start | bytes 24584 | tf_op jit(solution)/shard_map/while/body/eval_jaxpr/ppermute | solution.py:14
where the time goes:
time: 112 us
  starting transfers between devices  36.8 us (33%)
  local copies, waits for them, and re-layouts  25.6 us (23%)
  waiting for transfers between devices  24.2 us (22%)
  matrix products  16.5 us (15%)
  other arithmetic  5.18 us (5%)
  loops' own time  2.46 us (2%)
    all_to_all x1, starting transfers between devices, on_device(): lax.all_to_all(offered, ('gx', 'gy'), split_axis=0, concat_axis=0, tiled=...  20.6 us
    all_to_all x1, waiting for transfers between devices, on_device(): lax.all_to_all(offered, ('gx', 'gy'), split_axis=0, concat_axis=0, tiled=...  13.3 us
    scatter x1, local copies, waits for them, and re-layouts, on_device(): package = jnp.zeros((groups * capacity, 2, seg_len), jnp.float32).at[rows...  12.4 us
    ppermute x3, starting transfers between devices, from_behind(): return lax.ppermute(block, axis, route)  10.9 us
    dot_general x16, matrix products, add_block(): lax.dot_general(stacked, column_hot(cell_ids), (((1,), (1,)), ((), ())),...  9.55 us
    all_to_all x1, waiting for transfers between devices, on_device(): lax.all_to_all(package, ('gx', 'gy'), split_axis=0, concat_axis=0, tiled=...  8.5 us
    dot_general x16, matrix products, pick_block(): jnp.dot(cell_table, column_hot(cell_ids), precision=lax.Precision.HIGHEST...  6.99 us
    all_to_all x1, starting transfers between devices, on_device(): lax.all_to_all(package, ('gx', 'gy'), split_axis=0, concat_axis=0, tiled=...  5.28 us
  transfers between devices with their start and end apart: 5, of which 5 were waited for; matrix products, arithmetic and copies ran while one was open for 2% of the time, Pallas kernels for 0%

commit v1 on v0

--- a/solution.py
+++ b/solution.py
@@ -3,6 +3,8 @@
 import jax
 import jax.numpy as jnp
 from jax import lax
+from jax.experimental import pallas as pl
+from jax.experimental.pallas import tpu as pltpu
 from jax.sharding import PartitionSpec as P
 
 BL_STEPS = 8
@@ -50,6 +52,91 @@
 def row_hot(cell_ids, map_rows):
     levels = lax.broadcasted_iota(jnp.int32, (map_rows, cell_ids.shape[0]), 0)
     return (cell_ids[None, :] // 128 == levels).astype(jnp.float32)
+
+
+def gather_kernel(table_ref, ids_ref, out_ref):
+    map_rows = table_ref.shape[0]
+    tiles = ids_ref.shape[0] // 8
+    table = table_ref[...]
+    spread = [jnp.broadcast_to(table[r : r + 1, :], (8, 128)) for r in range(map_rows)]
+
+    def body(i, carry):
+        start = pl.multiple_of(i * 8, 8)
+        ids = ids_ref[pl.ds(start, 8), :]
+        lane = jnp.bitwise_and(ids, 127)
+        level = jnp.right_shift(ids, 7)
+        picked = jnp.zeros((8, 128), jnp.float32)
+        for r in range(map_rows):
+            got = jnp.take_along_axis(spread[r], lane, axis=1, mode="promise_in_bounds")
+            picked = jnp.where(level == r, got, picked)
+        out_ref[pl.ds(start, 8), :] = picked
+        return carry
+
+    lax.fori_loop(0, tiles, body, 0, unroll=4)
+
+
+def gather_cells(cell_table, local_map):
+    return pl.pallas_call(
+        gather_kernel,
+        out_shape=jax.ShapeDtypeStruct(local_map.shape, jnp.float32),
+        in_specs=[pl.BlockSpec(memory_space=pltpu.VMEM)] * 2,
+        out_specs=pl.BlockSpec(memory_space=pltpu.VMEM),
+    )(cell_table, local_map)
+
+
+def scatter_kernel(ids_ref, upper_ref, lower_ref, out_ref):
+    map_rows = out_ref.shape[0] // 2
+    tiles = ids_ref.shape[0] // 8
+    lanes = lax.broadcasted_iota(jnp.int32, (128, 128), 0)
+    levels = lax.broadcasted_iota(jnp.int32, (map_rows, 128), 0)
+
+    def pieces(values):
+        high = values.astype(jnp.bfloat16)
+        rest = values - high.astype(jnp.float32)
+        middle = rest.astype(jnp.bfloat16)
+        low = (rest - middle.astype(jnp.float32)).astype(jnp.bfloat16)
+        return [high, middle, low]
+
+    def body(i, totals):
+        start = pl.multiple_of(i * 8, 8)
+        ids = ids_ref[pl.ds(start, 8), :]
+        upper = upper_ref[pl.ds(start, 8), :]
+        lower = lower_ref[pl.ds(start, 8), :]
+        hots, parts = [], []
+        for j in range(8):
+            cell = ids[j : j + 1, :]
+            hots.append((jnp.bitwise_and(cell, 127) == lanes).astype(jnp.bfloat16))
+            on_level = jnp.right_shift(cell, 7) == levels
+            rows = jnp.concatenate(
+                [
+                    jnp.where(on_level, upper[j : j + 1, :], 0.0),
+                    jnp.where(on_level, lower[j : j + 1, :], 0.0),
+                ],
+                axis=0,
+            )
+            parts.append(jnp.concatenate(pieces(rows), axis=0))
+        added = lax.dot_general(
+            jnp.concatenate(parts, axis=1),
+            jnp.concatenate(hots, axis=1),
+            (((1,), (1,)), ((), ())),
+            preferred_element_type=jnp.float32,
+        )
+        return totals + added
+
+    totals = lax.fori_loop(
+        0, tiles, body, jnp.zeros((6 * map_rows, 128), jnp.float32), unroll=2
+    )
+    span = 2 * map_rows
+    out_ref[...] = (totals[:span] + totals[span : 2 * span]) + totals[2 * span :]
+
+
+def scatter_cells(local_map, upper, lower, map_rows):
+    return pl.pallas_call(
+        scatter_kernel,
+        out_shape=jax.ShapeDtypeStruct((2 * map_rows, 128), jnp.float32),
+        in_specs=[pl.BlockSpec(memory_space=pltpu.VMEM)] * 3,
+        out_specs=pl.BlockSpec(memory_space=pltpu.VMEM),
+    )(local_map, upper, lower)
 
 
 def on_device(saturation, retention, gravity, cell_map, owner_id, stream_dir, node_weight, flight):
@@ -69,26 +156,20 @@
     block_ids = local_map.reshape(block_count, block_width)
     cell_table = flat[: map_rows * 128].reshape(map_rows, 128)
 
-    def pick_block(cell_ids):
-        by_rows = jnp.dot(
-            cell_table,
-            column_hot(cell_ids),
-            precision=lax.Precision.HIGHEST,
-            preferred_element_type=jnp.float32,
-        )
-        return jnp.sum(by_rows * row_hot(cell_ids, map_rows), axis=0)
-
-    offered = lax.map(pick_block, block_ids).reshape(local_map.shape)
+    offered = gather_cells(cell_table, local_map)
     arrived = lax.all_to_all(offered, ("gx", "gy"), split_axis=0, concat_axis=0, tiled=True)
     burden = gravity * saturation * (1.0 - saturation)
     zero_plane = jnp.zeros((rows_x, rows_y), jnp.float32)
     local_end, _ = lax.scan(descend, zero_plane, (retention, burden))
     through = jnp.prod(retention, axis=0)
 
-    def relay(counter, entering):
-        return from_behind(through * entering + local_end, "gz", 1)
-
-    entering = lax.fori_loop(0, lax.axis_size("gz") - 1, relay, zero_plane)
+    depth_size = lax.axis_size("gz")
+    pair = jnp.stack([through, local_end])
+    behind = [from_behind(pair, "gz", d) for d in range(1, depth_size)]
+    entering = zero_plane
+    for d in range(depth_size - 1, 0, -1):
+        above = behind[d - 1]
+        entering = above[0] * entering + above[1]
     _, inflow = lax.scan(descend, entering, (retention, burden))
     owners = owner_id[0, :, 0]
     rows = slot_rows(owners, groups, capacity)
@@ -101,33 +182,14 @@
     )
     updated = updated.reshape(seg_dev, seg_len)
     weights = node_weight[0]
-    package = (
-        jnp.zeros((groups * capacity, 2, seg_len), jnp.float32)
-        .at[rows]
-        .set(jnp.stack([weights * updated, weights], axis=1))
-    )
+    slots = groups * capacity
+    filled = rows[None, :] == jnp.arange(slots, dtype=jnp.int32)[:, None]
+    source = jnp.sum(jnp.where(filled, jnp.arange(seg_dev, dtype=jnp.int32)[None, :], 0), axis=1)
+    used = jnp.any(filled, axis=1)
+    stacked = jnp.stack([weights * updated, weights], axis=1)
+    package = jnp.where(used[:, None, None], stacked[source], 0.0)
     returned = lax.all_to_all(package, ("gx", "gy"), split_axis=0, concat_axis=0, tiled=True)
-    weighted_sat = returned[:, 0, :].reshape(block_count, block_width)
-    weight_only = returned[:, 1, :].reshape(block_count, block_width)
-
-    def add_block(totals, block):
-        cell_ids, upper, lower = block
-        levels = row_hot(cell_ids, map_rows)
-        stacked = jnp.concatenate([levels * upper[None, :], levels * lower[None, :]], axis=0)
-        added = lax.dot_general(
-            stacked,
-            column_hot(cell_ids),
-            (((1,), (1,)), ((), ())),
-            precision=lax.Precision.HIGHEST,
-            preferred_element_type=jnp.float32,
-        )
-        return (totals + added, None)
-
-    sums, _ = lax.scan(
-        add_block,
-        jnp.zeros((2 * map_rows, 128), jnp.float32),
-        (block_ids, weighted_sat, weight_only),
-    )
+    sums = scatter_cells(local_map, returned[:, 0, :], returned[:, 1, :], map_rows)
     padding = jnp.zeros((cell_count - map_rows * 128,), jnp.float32)
     numerator = jnp.concatenate([sums[:map_rows].reshape(-1), padding])
     denominator = jnp.concatenate([sums[map_rows:].reshape(-1), padding])

time: 112 us -> 96.5 us (0.86)
  local copies, waits for them, and re-layouts: 25.6 us -> 7.13 us
  matrix products: 16.5 us -> 0 us
  waiting for transfers between devices: 24.2 us -> 37.6 us
  Pallas kernels: 0 us -> 9.02 us
  loops' own time: 2.46 us -> 0.83 us
  starting transfers between devices: 36.8 us -> 35.3 us
    dot_general x32 -> x0, matrix products: 16.5 us -> none  [the longest x16 9.55 us: add_block(): lax.dot_general(stacked, column_hot(cell_ids), (((1,), (1,)), ((), ())),...]
    all_to_all x1, waiting for transfers between devices: 8.5 us -> 21.7 us  [on_device(): lax.all_to_all(package, ('gx', 'gy'), split_axis=0, concat_axis=0, tiled=...]
    scatter x1 -> x0, local copies, waits for them, and re-layouts: 12.4 us -> none  [on_device(): package = jnp.zeros((groups * capacity, 2, seg_len), jnp.float32).at[rows...]
    pallas_call x0 -> x2, Pallas kernels: none -> 9.02 us  [the longest x1 6.4 us: scatter_cells(): pl.pallas_call(scatter_kernel, out_shape=jax.ShapeDtypeStruct((2 * map_ro...]
    dynamic_update_slice x16 -> x0, local copies, waits for them, and re-layouts: 3.28 us -> none  [on_device(): offered = lax.map(pick_block, block_ids).reshape(local_map.shape)]
    all_to_all x1, waiting for transfers between devices: 13.3 us -> 15.8 us  [on_device(): lax.all_to_all(offered, ('gx', 'gy'), split_axis=0, concat_axis=0, tiled=...]
    ppermute x3, waiting for transfers between devices: 2.31 us -> 0.01 us  [from_behind(): return lax.ppermute(block, axis, route)]
    unnamed x14 -> x12, local copies, waits for them, and re-layouts: 4.38 us -> 2.07 us
  transfers between devices with their start and end apart: 5 -> 5, of which waited for: 5 -> 2; matrix products, arithmetic and copies ran while one was open for 2% -> 3% of each run, Pallas kernels for 0% -> 3%
where the time goes in v1:
time: 96.5 us; the launch traced here: 96 us
  waiting for transfers between devices  37.6 us (39%)
  starting transfers between devices  35.3 us (37%)
  Pallas kernels  9.02 us (9%)
  local copies, waits for them, and re-layouts  7.13 us (7%)
  other arithmetic  5.24 us (5%)
    all_to_all x1, waiting for transfers between devices, on_device(): lax.all_to_all(package, ('gx', 'gy'), split_axis=0, concat_axis=0, tiled=...  21.7 us
    all_to_all x1, starting transfers between devices, on_device(): lax.all_to_all(offered, ('gx', 'gy'), split_axis=0, concat_axis=0, tiled=...  20.3 us
    all_to_all x1, waiting for transfers between devices, on_device(): lax.all_to_all(offered, ('gx', 'gy'), split_axis=0, concat_axis=0, tiled=...  15.8 us
    ppermute x3, starting transfers between devices, from_behind(): return lax.ppermute(block, axis, route)  9.71 us
    pallas_call x1, Pallas kernels, scatter_cells(): pl.pallas_call(scatter_kernel, out_shape=jax.ShapeDtypeStruct((2 * map_ro...  6.4 us
    all_to_all x1, starting transfers between devices, on_device(): lax.all_to_all(package, ('gx', 'gy'), split_axis=0, concat_axis=0, tiled=...  5.29 us
    pallas_call x1, Pallas kernels, gather_cells(): pl.pallas_call(gather_kernel, out_shape=jax.ShapeDtypeStruct(local_map.sh...  2.62 us
    unnamed x12, local copies, waits for them, and re-layouts  2.07 us
  transfers between devices with their start and end apart: 5, of which 2 were waited for; matrix products, arithmetic and copies ran while one was open for 3% of the time, Pallas kernels for 3%

profile of v1, /device:TPU:1, one launch (start us, length us, event | category | flops | bytes accessed | tf_op | source)
XLA Modules:
  0.0 96.0 jit_solution(2125140049655712103)
XLA Ops:
  0.6 0.0 copy-start.1
  0.7 1.0 %subtract_multiply_fusion = f32[16,16,128]{2,1,0:T(8,128)S(1)} fusion(f32[16,16,128]{2,1,0:T(8,128)} %param.12, f32[16,16,128]{2,1,0:T(8,128)} %param.14), kind=kLoop, calls=%fused_computation.10 | loop fusion | flops 98304 | bytes 393216 | tf_op jit(solution)/shard_map/mul | solution.py:161
  1.7 0.5 while.24
  2.2 0.0 copy-start
  2.3 4.1 %collective-permute-start = (f32[2,16,128]{2,1,0:T(8,128)S(1)}, f32[2,16,128]{2,1,0:T(8,128)S(1)}, u32[]{:S(2)}, u32[]{:S(2)}) collective-permute-start(f32[2,16,128]{2,1,0:T(8,128)S(1)} %pad_maximum_fusion.1), channel_id=1, source_target_pairs={{0,1},{1,2},{2,3},{4,5},{5,6},{6,7},{8,9},{9,10},{10,11},{12,13},{... | collective-permute-start | bytes 49160 | tf_op jit(solution)/shard_map/ppermute | solution.py:16
  6.3 4.4 %collective-permute-start.1 = (f32[2,16,128]{2,1,0:T(8,128)S(1)}, f32[2,16,128]{2,1,0:T(8,128)S(1)}, u32[]{:S(2)}, u32[]{:S(2)}) collective-permute-start(f32[2,16,128]{2,1,0:T(8,128)S(1)} %pad_maximum_fusion.1), channel_id=1, source_target_pairs={{0,2},{1,3},{4,6},{5,7},{8,10},{9,11},{12,14},{13,15},{16,18},{17,... | collective-permute-start | bytes 49160 | tf_op jit(solution)/shard_map/ppermute | solution.py:16
  10.7 1.3 %collective-permute-start.2 = (f32[2,16,128]{2,1,0:T(8,128)S(1)}, f32[2,16,128]{2,1,0:T(8,128)S(1)}, u32[]{:S(2)}, u32[]{:S(2)}) collective-permute-start(f32[2,16,128]{2,1,0:T(8,128)S(1)} %pad_maximum_fusion.1), channel_id=1, source_target_pairs={{0,3},{4,7},{8,11},{12,15},{16,19},{20,23},{24,27},{28,31},{32,35}... | collective-permute-start | bytes 49160 | tf_op jit(solution)/shard_map/ppermute | solution.py:16
  12.0 0.6 slice.84.table_ref
  12.6 2.6 %shard_map.95 = f32[256,128]{1,0:T(8,128)} custom-call(f32[8,128]{1,0:T(8,128)} %slice.84.table_ref, s32[256,128]{1,0:T(8,128)} %bitcast.80), custom_call_target="tpu_custom_call" | custom-call | tf_op jit(solution)/shard_map/pallas_call | solution.py:79
  15.2 20.3 %all-to-all-start = ((f32[128,2,128]{2,1,0:T(2,128)}), f32[128,2,128]{2,1,0:T(2,128)S(1)}, u32[]{:S(2)}, u32[]{:S(2)}) async-start(f32[128,2,128]{2,1,0:T(2,128)} %bitcast.82), calls=%async_computation | async-start | bytes 262144 | tf_op jit(solution)/shard_map/all_to_all | solution.py:160
  35.6 0.6 copy-done.4
  36.2 0.1 fusion.1
  36.3 0.2 reduce_window_sum.11
  36.5 0.2 select_reduce_fusion.1
  36.7 0.1 select_reduce_fusion
  36.8 0.1 fusion
  36.9 0.0 copy-start.5
  36.9 0.6 copy-done.5
  37.6 0.2 rev.10
  37.8 15.8 %all-to-all-done = f32[128,2,128]{2,1,0:T(2,128)S(1)} async-done(((f32[128,2,128]{2,1,0:T(2,128)}), f32[128,2,128]{2,1,0:T(2,128)S(1)}, u32[]{:S(2)}, u32[]{:S(2)}) %all-to-all-start) | async-done | bytes 131104 | tf_op jit(solution)/shard_map/all_to_all | solution.py:160
  53.7 0.6 gather_fusion
  54.3 0.2 rev.9
  54.5 0.1 add_divide_fusion.8
  54.6 0.1 add_divide_fusion.7
  54.7 0.1 add_divide_fusion.6
  54.8 0.1 add_divide_fusion.5
  54.9 0.1 add_divide_fusion.4
  55.1 0.1 add_divide_fusion.3
  55.2 0.1 add_divide_fusion.2
  55.3 0.1 add_divide_fusion.1
  55.4 0.1 multiply_subtract_fusion
  55.5 0.2 rev.11
  55.7 0.1 broadcast_select_fusion.1
  55.8 0.0 copy-start.2
  55.8 0.1 reshape.111
  55.9 0.8 copy-done.2
  56.6 0.1 mul.170
  56.7 0.1 pad_maximum_fusion
  56.8 1.0 %gather_fusion.1 = f32[256,2,128]{2,1,0:T(2,128)S(1)} fusion(f32[128,2,128]{2,1,0:T(2,128)S(1)} %pad_maximum_fusion, s32[1024]{0:T(1024)S(1)} %pad_clamp_fusion), kind=kCustom, calls=%fused_computation.1 | custom fusion | bytes 525312 | tf_op jit(solution)/shard_map/gather | solution.py:190
  57.8 1.0 %broadcast_select_fusion = f32[256,2,128]{2,1,0:T(2,128)} fusion(f32[256,2,128]{2,1,0:T(2,128)S(1)} %gather_fusion.1, pred[256]{0:T(512)(128)(4,1)S(1)} %fusion), kind=kLoop, calls=%fused_computation.7 | loop fusion | flops 65536 | bytes 524544 | tf_op jit(solution)/shard_map/jit(_where)/select_n | solution.py:190
  58.9 5.3 %all-to-all-start.1 = ((f32[256,2,128]{2,1,0:T(2,128)}), f32[256,2,128]{2,1,0:T(2,128)S(1)}, u32[]{:S(2)}, u32[]{:S(2)}) async-start(f32[256,2,128]{2,1,0:T(2,128)} %broadcast_select_fusion), calls=%async_computation.1 | async-start | bytes 524288 | tf_op jit(solution)/shard_map/all_to_all | solution.py:191
  64.1 0.8 while.23
  65.0 0.6 broadcast_in_dim_reshape.3
  65.6 21.7 %all-to-all-done.1 = f32[256,2,128]{2,1,0:T(2,128)S(1)} async-done(((f32[256,2,128]{2,1,0:T(2,128)}), f32[256,2,128]{2,1,0:T(2,128)S(1)}, u32[]{:S(2)}, u32[]{:S(2)}) %all-to-all-start.1) | async-done | bytes 262176 | tf_op jit(solution)/shard_map/all_to_all | solution.py:191
  87.3 0.9 fusion.6
  88.2 6.4 %shard_map.96 = f32[16,128]{1,0:T(8,128)} custom-call(s32[256,128]{1,0:T(8,128)} %bitcast.81, f32[256,128]{1,0:T(8,128)} %bitcast.84, f32[256,128]{1,0:T(8,128)} %bitcast.83), custom_call_target="tpu_custom_call" | custom-call | tf_op jit(solution)/shard_map/pallas_call | solution.py:134
  94.6 0.7 slice_bitcast_fusion.1
  95.3 0.7 add_subtract_fusion
  (70 shorter events, 0.7 us)
Async XLA Ops:
  0.6 1.0 %copy-start.1 = (f32[16,16,128]{2,1,0:T(8,128)S(1)}, f32[16,16,128]{2,1,0:T(8,128)}, u32[]{:S(2)}) copy-start(f32[16,16,128]{2,1,0:T(8,128)} %param.13) | copy-start | bytes 393220
  2.2 9.8 %copy-start = (f32[16,16,128]{2,1,0:T(8,128)S(1)}, f32[16,16,128]{2,1,0:T(8,128)}, u32[]{:S(2)}) copy-start(f32[16,16,128]{2,1,0:T(8,128)} %param.12) | copy-start | bytes 393220
  2.3 35.5 %collective-permute-start = (f32[2,16,128]{2,1,0:T(8,128)S(1)}, f32[2,16,128]{2,1,0:T(8,128)S(1)}, u32[]{:S(2)}, u32[]{:S(2)}) collective-permute-start(f32[2,16,128]{2,1,0:T(8,128)S(1)} %pad_maximum_fusion.1), channel_id=1, source_target_pairs={{0,1},{1,2},{2,3},{4,5},{5,6},{6,7},{8,9},{9,10},{10,11},{12,13},{... | collective-permute-start | bytes 49160 | tf_op jit(solution)/shard_map/ppermute | solution.py:16
  6.3 31.5 %collective-permute-start.1 = (f32[2,16,128]{2,1,0:T(8,128)S(1)}, f32[2,16,128]{2,1,0:T(8,128)S(1)}, u32[]{:S(2)}, u32[]{:S(2)}) collective-permute-start(f32[2,16,128]{2,1,0:T(8,128)S(1)} %pad_maximum_fusion.1), channel_id=1, source_target_pairs={{0,2},{1,3},{4,6},{5,7},{8,10},{9,11},{12,14},{13,15},{16,18},{17,... | collective-permute-start | bytes 49160 | tf_op jit(solution)/shard_map/ppermute | solution.py:16
  10.7 27.1 %collective-permute-start.2 = (f32[2,16,128]{2,1,0:T(8,128)S(1)}, f32[2,16,128]{2,1,0:T(8,128)S(1)}, u32[]{:S(2)}, u32[]{:S(2)}) collective-permute-start(f32[2,16,128]{2,1,0:T(8,128)S(1)} %pad_maximum_fusion.1), channel_id=1, source_target_pairs={{0,3},{4,7},{8,11},{12,15},{16,19},{20,23},{24,27},{28,31},{32,35}... | collective-permute-start | bytes 49160 | tf_op jit(solution)/shard_map/ppermute | solution.py:16
  15.2 38.4 %all-to-all-start = ((f32[128,2,128]{2,1,0:T(2,128)}), f32[128,2,128]{2,1,0:T(2,128)S(1)}, u32[]{:S(2)}, u32[]{:S(2)}) async-start(f32[128,2,128]{2,1,0:T(2,128)} %bitcast.82), calls=%async_computation | async-start | bytes 262144 | tf_op jit(solution)/shard_map/all_to_all | solution.py:160
  35.5 0.7 copy-start.4
  36.5 1.1 %copy-start.3 = (f32[1,128,128]{2,1,0:T(8,128)S(1)}, f32[1,128,128]{2,1,0:T(8,128)}, u32[]{:S(2)}) copy-start(f32[1,128,128]{2,1,0:T(8,128)} %param.19) | copy-start | bytes 196612
  36.9 0.7 copy-start.5
  55.8 0.8 copy-start.2
  58.9 28.5 %all-to-all-start.1 = ((f32[256,2,128]{2,1,0:T(2,128)}), f32[256,2,128]{2,1,0:T(2,128)S(1)}, u32[]{:S(2)}, u32[]{:S(2)}) async-start(f32[256,2,128]{2,1,0:T(2,128)} %broadcast_select_fusion), calls=%async_computation.1 | async-start | bytes 524288 | tf_op jit(solution)/shard_map/all_to_all | solution.py:191

commit v2 on v1

--- a/solution.py
+++ b/solution.py
@@ -1,5 +1,3 @@
-import math
-
 import jax
 import jax.numpy as jnp
 from jax import lax
@@ -7,6 +5,7 @@
 from jax.experimental.pallas import tpu as pltpu
 from jax.sharding import PartitionSpec as P
 
+
 BL_STEPS = 8
 
 
@@ -25,7 +24,7 @@
     state = jnp.where(flipped, node_sat[..., ::-1], node_sat)
     ratio = jnp.where(flipped, increments[..., ::-1], increments)
     inlet = jnp.ones(state.shape[:-1] + (1,), jnp.float32)
-    for iteration in range(BL_STEPS):
+    for _ in range(BL_STEPS):
         flows = frac_flow(state)
         upstream = jnp.concatenate([inlet, flows[..., :-1]], axis=-1)
         state = state - ratio * (flows - upstream)
@@ -42,16 +41,6 @@
     keep, drop = layer
     inflow = keep * carried
     return (inflow + drop, inflow)
-
-
-def column_hot(cell_ids):
-    lanes = lax.broadcasted_iota(jnp.int32, (128, cell_ids.shape[0]), 0)
-    return (cell_ids[None, :] % 128 == lanes).astype(jnp.float32)
-
-
-def row_hot(cell_ids, map_rows):
-    levels = lax.broadcasted_iota(jnp.int32, (map_rows, cell_ids.shape[0]), 0)
-    return (cell_ids[None, :] // 128 == levels).astype(jnp.float32)
 
 
 def gather_kernel(table_ref, ids_ref, out_ref):
@@ -139,6 +128,22 @@
     )(local_map, upper, lower)
 
 
+def segregation(saturation, retention, gravity):
+    burden = gravity * saturation * (1.0 - saturation)
+    zero_plane = jnp.zeros(saturation.shape[1:], jnp.float32)
+    local_end, _ = lax.scan(descend, zero_plane, (retention, burden))
+    through = jnp.prod(retention, axis=0)
+    depth_size = lax.axis_size("gz")
+    pair = jnp.stack([through, local_end])
+    behind = [from_behind(pair, "gz", d) for d in range(1, depth_size)]
+    entering = zero_plane
+    for d in range(depth_size - 1, 0, -1):
+        above = behind[d - 1]
+        entering = above[0] * entering + above[1]
+    _, inflow = lax.scan(descend, entering, (retention, burden))
+    return inflow, burden
+
+
 def on_device(saturation, retention, gravity, cell_map, owner_id, stream_dir, node_weight, flight):
     layers, rows_x, rows_y = saturation.shape
     size_x = lax.axis_size("gx")
@@ -150,27 +155,10 @@
     cell_count = flat.shape[0]
     map_rows = min(cell_count // 128, max(8, capacity * seg_len // 32))
     local_map = cell_map[0]
-    node_total = local_map.shape[0] * seg_len
-    block_width = math.gcd(node_total, 2048)
-    block_count = node_total // block_width
-    block_ids = local_map.reshape(block_count, block_width)
     cell_table = flat[: map_rows * 128].reshape(map_rows, 128)
 
     offered = gather_cells(cell_table, local_map)
     arrived = lax.all_to_all(offered, ("gx", "gy"), split_axis=0, concat_axis=0, tiled=True)
-    burden = gravity * saturation * (1.0 - saturation)
-    zero_plane = jnp.zeros((rows_x, rows_y), jnp.float32)
-    local_end, _ = lax.scan(descend, zero_plane, (retention, burden))
-    through = jnp.prod(retention, axis=0)
-
-    depth_size = lax.axis_size("gz")
-    pair = jnp.stack([through, local_end])
-    behind = [from_behind(pair, "gz", d) for d in range(1, depth_size)]
-    entering = zero_plane
-    for d in range(depth_size - 1, 0, -1):
-        above = behind[d - 1]
-        entering = above[0] * entering + above[1]
-    _, inflow = lax.scan(descend, entering, (retention, burden))
     owners = owner_id[0, :, 0]
     rows = slot_rows(owners, groups, capacity)
     node_in = arrived[rows]
@@ -189,6 +177,8 @@
     stacked = jnp.stack([weights * updated, weights], axis=1)
     package = jnp.where(used[:, None, None], stacked[source], 0.0)
     returned = lax.all_to_all(package, ("gx", "gy"), split_axis=0, concat_axis=0, tiled=True)
+    package, retention, gravity = lax.optimization_barrier((package, retention, gravity))
+    inflow, burden = segregation(saturation, retention, gravity)
     sums = scatter_cells(local_map, returned[:, 0, :], returned[:, 1, :], map_rows)
     padding = jnp.zeros((cell_count - map_rows * 128,), jnp.float32)
     numerator = jnp.concatenate([sums[:map_rows].reshape(-1), padding])

time: 96.5 us -> 97 us (level)
  local copies, waits for them, and re-layouts: 7.13 us -> 9.22 us
  other arithmetic: 5.24 us -> 4.24 us
  starting transfers between devices: 35.3 us -> 34.3 us
    ppermute x3, starting transfers between devices: 9.71 us -> 8.16 us  [from_behind(): return lax.ppermute(block, axis, route)]
    unnamed x12 -> x14, local copies, waits for them, and re-layouts: 2.07 us -> 3.48 us
    mul x1, other arithmetic: 1.02 us -> 0.02 us  [segregation(): burden = gravity * saturation * (1.0 - saturation)]
  transfers between devices with their start and end apart: 5 -> 5, of which waited for: 2 -> 2; matrix products, arithmetic and copies ran while one was open for 3% -> 2% of each run, Pallas kernels for 3% -> 0%
where the time goes in v2:
time: 97 us; the launch traced here: 96.5 us
  waiting for transfers between devices  37.9 us (39%)
  starting transfers between devices  34.3 us (35%)
  local copies, waits for them, and re-layouts  9.22 us (10%)
  Pallas kernels  9.02 us (9%)
  other arithmetic  4.24 us (4%)
    all_to_all x1, waiting for transfers between devices, on_device(): lax.all_to_all(package, ('gx', 'gy'), split_axis=0, concat_axis=0, tiled=...  22.6 us
    all_to_all x1, starting transfers between devices, on_device(): lax.all_to_all(offered, ('gx', 'gy'), split_axis=0, concat_axis=0, tiled=...  20.6 us
    all_to_all x1, waiting for transfers between devices, on_device(): lax.all_to_all(offered, ('gx', 'gy'), split_axis=0, concat_axis=0, tiled=...  15.3 us
    ppermute x3, starting transfers between devices, from_behind(): return lax.ppermute(block, axis, route)  8.16 us
    pallas_call x1, Pallas kernels, scatter_cells(): pl.pallas_call(scatter_kernel, out_shape=jax.ShapeDtypeStruct((2 * map_ro...  6.4 us
    all_to_all x1, starting transfers between devices, on_device(): lax.all_to_all(package, ('gx', 'gy'), split_axis=0, concat_axis=0, tiled=...  5.61 us
    unnamed x14, local copies, waits for them, and re-layouts  3.48 us
    pallas_call x1, Pallas kernels, gather_cells(): pl.pallas_call(gather_kernel, out_shape=jax.ShapeDtypeStruct(local_map.sh...  2.62 us
  transfers between devices with their start and end apart: 5, of which 2 were waited for; matrix products, arithmetic and copies ran while one was open for 2% of the time, Pallas kernels for 0%

profile of v2, /device:TPU:1, one launch (start us, length us, event | category | flops | bytes accessed | tf_op | source)
XLA Modules:
  0.0 96.5 jit_solution(10837333792172820805)
XLA Ops:
  0.6 1.3 %slice.84.table_ref = f32[8,128]{1,0:T(8,128)} slice(f32[256,128]{1,0:T(8,128)} %bitcast.78), slice={[0:8], [0:128]} | slice | bytes 8192 | tf_op jit(solution)/shard_map/slice | solution.py:158
  1.9 2.6 %shard_map.95 = f32[256,128]{1,0:T(8,128)} custom-call(f32[8,128]{1,0:T(8,128)} %slice.84.table_ref, s32[256,128]{1,0:T(8,128)} %bitcast.80), custom_call_target="tpu_custom_call" | custom-call | tf_op jit(solution)/shard_map/pallas_call | solution.py:68
  4.5 20.6 %all-to-all-start = ((f32[128,2,128]{2,1,0:T(2,128)}), f32[128,2,128]{2,1,0:T(2,128)S(1)}, u32[]{:S(2)}, u32[]{:S(2)}) async-start(f32[128,2,128]{2,1,0:T(2,128)} %bitcast.82), calls=%async_computation | async-start | bytes 262144 | tf_op jit(solution)/shard_map/all_to_all | solution.py:161
  25.1 0.0 copy-start.5
  25.1 0.6 copy-done.5
  25.8 0.1 fusion.1
  25.8 0.2 reduce_window_sum.11
  26.0 0.2 select_reduce_fusion.1
  26.2 0.6 copy-done.4
  26.9 0.2 rev.10
  27.1 0.1 select_reduce_fusion
  27.2 0.0 copy-start.6
  27.2 0.1 fusion
  27.3 0.5 copy-done.6
  27.9 15.3 %all-to-all-done = f32[128,2,128]{2,1,0:T(2,128)S(1)} async-done(((f32[128,2,128]{2,1,0:T(2,128)}), f32[128,2,128]{2,1,0:T(2,128)S(1)}, u32[]{:S(2)}, u32[]{:S(2)}) %all-to-all-start) | async-done | bytes 131104 | tf_op jit(solution)/shard_map/all_to_all | solution.py:161
  43.2 0.6 gather_fusion
  43.9 0.2 rev.9
  44.1 0.1 add_divide_fusion.8
  44.2 0.1 add_divide_fusion.7
  44.3 0.1 add_divide_fusion.6
  44.4 0.1 add_divide_fusion.5
  44.5 0.1 add_divide_fusion.4
  44.6 0.1 add_divide_fusion.3
  44.7 0.1 add_divide_fusion.2
  44.9 0.1 add_divide_fusion.1
  45.0 0.1 multiply_subtract_fusion
  45.1 0.2 rev.11
  45.3 0.1 broadcast_select_fusion.1
  45.3 0.0 copy-start.2
  45.3 0.1 reshape.111
  45.4 0.8 copy-done.2
  46.2 0.1 mul.170
  46.2 0.1 pad_maximum_fusion
  46.4 1.0 %gather_fusion.1 = f32[256,2,128]{2,1,0:T(2,128)S(1)} fusion(f32[128,2,128]{2,1,0:T(2,128)S(1)} %pad_maximum_fusion, s32[1024]{0:T(1024)S(1)} %pad_clamp_fusion), kind=kCustom, calls=%fused_computation.1 | custom fusion | bytes 525312 | tf_op jit(solution)/shard_map/gather | solution.py:178
  47.4 1.0 %broadcast_select_fusion = f32[256,2,128]{2,1,0:T(2,128)} fusion(f32[256,2,128]{2,1,0:T(2,128)S(1)} %gather_fusion.1, pred[256]{0:T(512)(128)(4,1)S(1)} %fusion), kind=kLoop, calls=%fused_computation.7 | loop fusion | flops 65536 | bytes 524544 | tf_op jit(solution)/shard_map/jit(_where)/select_n | solution.py:178
  48.5 0.9 copy-done.1
  49.4 0.5 while.24
  49.9 4.4 %collective-permute-start.2 = (f32[2,16,128]{2,1,0:T(8,128)S(1)}, f32[2,16,128]{2,1,0:T(8,128)S(1)}, u32[]{:S(2)}, u32[]{:S(2)}) collective-permute-start(f32[2,16,128]{2,1,0:T(8,128)S(1)} %pad_maximum_fusion.1), channel_id=1, source_target_pairs={{0,3},{4,7},{8,11},{12,15},{16,19},{20,23},{24,27},{28,31},{32,35}... | collective-permute-start | bytes 49160 | tf_op jit(solution)/shard_map/ppermute | solution.py:15
  54.3 1.3 %collective-permute-start.1 = (f32[2,16,128]{2,1,0:T(8,128)S(1)}, f32[2,16,128]{2,1,0:T(8,128)S(1)}, u32[]{:S(2)}, u32[]{:S(2)}) collective-permute-start(f32[2,16,128]{2,1,0:T(8,128)S(1)} %pad_maximum_fusion.1), channel_id=1, source_target_pairs={{0,2},{1,3},{4,6},{5,7},{8,10},{9,11},{12,14},{13,15},{16,18},{17,... | collective-permute-start | bytes 49160 | tf_op jit(solution)/shard_map/ppermute | solution.py:15
  55.6 2.5 %collective-permute-start = (f32[2,16,128]{2,1,0:T(8,128)S(1)}, f32[2,16,128]{2,1,0:T(8,128)S(1)}, u32[]{:S(2)}, u32[]{:S(2)}) collective-permute-start(f32[2,16,128]{2,1,0:T(8,128)S(1)} %pad_maximum_fusion.1), channel_id=1, source_target_pairs={{0,1},{1,2},{2,3},{4,5},{5,6},{6,7},{8,9},{9,10},{10,11},{12,13},{... | collective-permute-start | bytes 49160 | tf_op jit(solution)/shard_map/ppermute | solution.py:15
  58.1 0.6 broadcast_in_dim_reshape.3
  58.7 5.6 %all-to-all-start.1 = ((f32[256,2,128]{2,1,0:T(2,128)}), f32[256,2,128]{2,1,0:T(2,128)S(1)}, u32[]{:S(2)}, u32[]{:S(2)}) async-start(f32[256,2,128]{2,1,0:T(2,128)} %broadcast_select_fusion), calls=%async_computation.1 | async-start | bytes 524288 | tf_op jit(solution)/shard_map/all_to_all | solution.py:179
  64.4 0.8 while.23
  65.2 22.6 %all-to-all-done.1 = f32[256,2,128]{2,1,0:T(2,128)S(1)} async-done(((f32[256,2,128]{2,1,0:T(2,128)}), f32[256,2,128]{2,1,0:T(2,128)S(1)}, u32[]{:S(2)}, u32[]{:S(2)}) %all-to-all-start.1) | async-done | bytes 262176 | tf_op jit(solution)/shard_map/all_to_all | solution.py:179
  87.8 0.9 fusion.6
  88.7 6.4 %shard_map.96 = f32[16,128]{1,0:T(8,128)} custom-call(s32[256,128]{1,0:T(8,128)} %bitcast.81, f32[256,128]{1,0:T(8,128)} %bitcast.84, f32[256,128]{1,0:T(8,128)} %bitcast.83), custom_call_target="tpu_custom_call" | custom-call | tf_op jit(solution)/shard_map/pallas_call | solution.py:123
  95.1 0.7 slice_bitcast_fusion.1
  95.8 0.7 add_subtract_fusion
  (72 shorter events, 0.7 us)
Async XLA Ops:
  4.5 38.7 %all-to-all-start = ((f32[128,2,128]{2,1,0:T(2,128)}), f32[128,2,128]{2,1,0:T(2,128)S(1)}, u32[]{:S(2)}, u32[]{:S(2)}) async-start(f32[128,2,128]{2,1,0:T(2,128)} %bitcast.82), calls=%async_computation | async-start | bytes 262144 | tf_op jit(solution)/shard_map/all_to_all | solution.py:161
  25.1 0.7 copy-start.5
  26.0 0.8 copy-start.4
  27.2 0.7 copy-start.6
  45.3 0.8 copy-start.2
  47.4 1.1 %copy-start = (f32[16,16,128]{2,1,0:T(8,128)S(1)}, f32[16,16,128]{2,1,0:T(8,128)}, u32[]{:S(2)}) copy-start(f32[16,16,128]{2,1,0:T(8,128)} %param.12) | copy-start | bytes 393220
  47.4 1.1 %copy-start.3 = (f32[16,16,128]{2,1,0:T(8,128)S(1)}, f32[16,16,128]{2,1,0:T(8,128)}, u32[]{:S(2)}) copy-start(f32[16,16,128]{2,1,0:T(8,128)} %param.14) | copy-start | bytes 393220
  48.4 0.9 copy-start.1
  49.9 14.4 %collective-permute-start.2 = (f32[2,16,128]{2,1,0:T(8,128)S(1)}, f32[2,16,128]{2,1,0:T(8,128)S(1)}, u32[]{:S(2)}, u32[]{:S(2)}) collective-permute-start(f32[2,16,128]{2,1,0:T(8,128)S(1)} %pad_maximum_fusion.1), channel_id=1, source_target_pairs={{0,3},{4,7},{8,11},{12,15},{16,19},{20,23},{24,27},{28,31},{32,35}... | collective-permute-start | bytes 49160 | tf_op jit(solution)/shard_map/ppermute | solution.py:15
  54.3 10.1 %collective-permute-start.1 = (f32[2,16,128]{2,1,0:T(8,128)S(1)}, f32[2,16,128]{2,1,0:T(8,128)S(1)}, u32[]{:S(2)}, u32[]{:S(2)}) collective-permute-start(f32[2,16,128]{2,1,0:T(8,128)S(1)} %pad_maximum_fusion.1), channel_id=1, source_target_pairs={{0,2},{1,3},{4,6},{5,7},{8,10},{9,11},{12,14},{13,15},{16,18},{17,... | collective-permute-start | bytes 49160 | tf_op jit(solution)/shard_map/ppermute | solution.py:15
  55.6 8.8 %collective-permute-start = (f32[2,16,128]{2,1,0:T(8,128)S(1)}, f32[2,16,128]{2,1,0:T(8,128)S(1)}, u32[]{:S(2)}, u32[]{:S(2)}) collective-permute-start(f32[2,16,128]{2,1,0:T(8,128)S(1)} %pad_maximum_fusion.1), channel_id=1, source_target_pairs={{0,1},{1,2},{2,3},{4,5},{5,6},{6,7},{8,9},{9,10},{10,11},{12,13},{... | collective-permute-start | bytes 49160 | tf_op jit(solution)/shard_map/ppermute | solution.py:15
  58.7 29.0 %all-to-all-start.1 = ((f32[256,2,128]{2,1,0:T(2,128)}), f32[256,2,128]{2,1,0:T(2,128)S(1)}, u32[]{:S(2)}, u32[]{:S(2)}) async-start(f32[256,2,128]{2,1,0:T(2,128)} %broadcast_select_fusion), calls=%async_computation.1 | async-start | bytes 524288 | tf_op jit(solution)/shard_map/all_to_all | solution.py:179

commit v3 on v2

--- a/solution.py
+++ b/solution.py
@@ -44,9 +44,9 @@
 
 
 def gather_kernel(table_ref, ids_ref, out_ref):
-    map_rows = table_ref.shape[0]
+    map_rows = table_ref.shape[1]
     tiles = ids_ref.shape[0] // 8
-    table = table_ref[...]
+    table = table_ref[0]
     spread = [jnp.broadcast_to(table[r : r + 1, :], (8, 128)) for r in range(map_rows)]
 
     def body(i, carry):
@@ -61,19 +61,23 @@
         out_ref[pl.ds(start, 8), :] = picked
         return carry
 
-    lax.fori_loop(0, tiles, body, 0, unroll=4)
-
-
-def gather_cells(cell_table, local_map):
+    lax.fori_loop(0, tiles, body, 0, unroll=True)
+
+
+def gather_cells(saturation, local_map, map_rows):
     return pl.pallas_call(
         gather_kernel,
         out_shape=jax.ShapeDtypeStruct(local_map.shape, jnp.float32),
-        in_specs=[pl.BlockSpec(memory_space=pltpu.VMEM)] * 2,
-        out_specs=pl.BlockSpec(memory_space=pltpu.VMEM),
-    )(cell_table, local_map)
-
-
-def scatter_kernel(ids_ref, upper_ref, lower_ref, out_ref):
+        grid=(1,),
+        in_specs=[
+            pl.BlockSpec((1, map_rows, 128), lambda i: (0, 0, 0)),
+            pl.BlockSpec(local_map.shape, lambda i: (0, 0)),
+        ],
+        out_specs=pl.BlockSpec(local_map.shape, lambda i: (0, 0)),
+    )(saturation, local_map)
+
+
+def scatter_kernel(ids_ref, both_ref, out_ref):
     map_rows = out_ref.shape[0] // 2
     tiles = ids_ref.shape[0] // 8
     lanes = lax.broadcasted_iota(jnp.int32, (128, 128), 0)
@@ -89,8 +93,8 @@
     def body(i, totals):
         start = pl.multiple_of(i * 8, 8)
         ids = ids_ref[pl.ds(start, 8), :]
-        upper = upper_ref[pl.ds(start, 8), :]
-        lower = lower_ref[pl.ds(start, 8), :]
+        upper = both_ref[pl.ds(start, 8), pl.ds(0, 128)]
+        lower = both_ref[pl.ds(start, 8), pl.ds(128, 128)]
         hots, parts = [], []
         for j in range(8):
             cell = ids[j : j + 1, :]
@@ -113,19 +117,19 @@
         return totals + added
 
     totals = lax.fori_loop(
-        0, tiles, body, jnp.zeros((6 * map_rows, 128), jnp.float32), unroll=2
+        0, tiles, body, jnp.zeros((6 * map_rows, 128), jnp.float32), unroll=True
     )
     span = 2 * map_rows
     out_ref[...] = (totals[:span] + totals[span : 2 * span]) + totals[2 * span :]
 
 
-def scatter_cells(local_map, upper, lower, map_rows):
+def scatter_cells(local_map, both, map_rows):
     return pl.pallas_call(
         scatter_kernel,
         out_shape=jax.ShapeDtypeStruct((2 * map_rows, 128), jnp.float32),
-        in_specs=[pl.BlockSpec(memory_space=pltpu.VMEM)] * 3,
+        in_specs=[pl.BlockSpec(memory_space=pltpu.VMEM)] * 2,
         out_specs=pl.BlockSpec(memory_space=pltpu.VMEM),
-    )(local_map, upper, lower)
+    )(local_map, both)
 
 
 def segregation(saturation, retention, gravity):
@@ -155,9 +159,8 @@
     cell_count = flat.shape[0]
     map_rows = min(cell_count // 128, max(8, capacity * seg_len // 32))
     local_map = cell_map[0]
-    cell_table = flat[: map_rows * 128].reshape(map_rows, 128)
-
-    offered = gather_cells(cell_table, local_map)
+
+    offered = gather_cells(saturation, local_map, map_rows)
     arrived = lax.all_to_all(offered, ("gx", "gy"), split_axis=0, concat_axis=0, tiled=True)
     owners = owner_id[0, :, 0]
     rows = slot_rows(owners, groups, capacity)
@@ -174,12 +177,13 @@
     filled = rows[None, :] == jnp.arange(slots, dtype=jnp.int32)[:, None]
     source = jnp.sum(jnp.where(filled, jnp.arange(seg_dev, dtype=jnp.int32)[None, :], 0), axis=1)
     used = jnp.any(filled, axis=1)
-    stacked = jnp.stack([weights * updated, weights], axis=1)
-    package = jnp.where(used[:, None, None], stacked[source], 0.0)
+    joined = jnp.concatenate([weights * updated, weights], axis=1)
+    joined = jnp.concatenate([joined, jnp.zeros((1, 2 * seg_len), jnp.float32)], axis=0)
+    package = joined[jnp.where(used, source, seg_dev)]
     returned = lax.all_to_all(package, ("gx", "gy"), split_axis=0, concat_axis=0, tiled=True)
     package, retention, gravity = lax.optimization_barrier((package, retention, gravity))
     inflow, burden = segregation(saturation, retention, gravity)
-    sums = scatter_cells(local_map, returned[:, 0, :], returned[:, 1, :], map_rows)
+    sums = scatter_cells(local_map, returned, map_rows)
     padding = jnp.zeros((cell_count - map_rows * 128,), jnp.float32)
     numerator = jnp.concatenate([sums[:map_rows].reshape(-1), padding])
     denominator = jnp.concatenate([sums[map_rows:].reshape(-1), padding])

time: 97 us -> 93.1 us (0.960)
  Pallas kernels: 9.02 us -> 6.29 us
  other arithmetic: 4.24 us -> 3.03 us
    slice x2 -> x0, local copies, waits for them, and re-layouts: 2.18 us -> none  [the longest x1 1.28 us: on_device(): cell_table = flat[:map_rows * 128].reshape(map_rows, 128)]
    pallas_call x1, Pallas kernels: 6.4 us -> 4.26 us  [scatter_cells(): pl.pallas_call(scatter_kernel, out_shape=jax.ShapeDtypeStruct((2 * map_ro...]
    all_to_all x0 -> x2, local copies, waits for them, and re-layouts: none -> 1.73 us  [on_device(): lax.all_to_all(package, ('gx', 'gy'), split_axis=0, concat_axis=0, tiled=...]
    select_n x2, other arithmetic: 1.04 us -> 0.01 us  [on_device(): package = joined[jnp.where(used, source, seg_dev)]]
where the time goes in v3:
time: 93.1 us; the launch traced here: 92.7 us
  waiting for transfers between devices  38 us (41%)
  starting transfers between devices  34.9 us (37%)
  local copies, waits for them, and re-layouts  8.62 us (9%)
  Pallas kernels  6.29 us (7%)
  other arithmetic  3.03 us (3%)
  between operations  0.96 us (1%)
    all_to_all x1, waiting for transfers between devices, on_device(): lax.all_to_all(package, ('gx', 'gy'), split_axis=0, concat_axis=0, tiled=...  22.6 us
    all_to_all x1, starting transfers between devices, on_device(): lax.all_to_all(offered, ('gx', 'gy'), split_axis=0, concat_axis=0, tiled=...  20.6 us
    all_to_all x1, waiting for transfers between devices, on_device(): lax.all_to_all(offered, ('gx', 'gy'), split_axis=0, concat_axis=0, tiled=...  15.5 us
    ppermute x3, starting transfers between devices, from_behind(): return lax.ppermute(block, axis, route)  8.76 us
    all_to_all x1, starting transfers between devices, on_device(): lax.all_to_all(package, ('gx', 'gy'), split_axis=0, concat_axis=0, tiled=...  5.61 us
    pallas_call x1, Pallas kernels, scatter_cells(): pl.pallas_call(scatter_kernel, out_shape=jax.ShapeDtypeStruct((2 * map_ro...  4.26 us
    unnamed x14, local copies, waits for them, and re-layouts  3.38 us
    pallas_call x1, Pallas kernels, gather_cells(): pl.pallas_call(gather_kernel, out_shape=jax.ShapeDtypeStruct(local_map.sh...  2.03 us
  transfers between devices with their start and end apart: 5, of which 2 were waited for; matrix products, arithmetic and copies ran while one was open for 2% of the time, Pallas kernels for 0%

profile of v3, /device:TPU:1, one launch (start us, length us, event | category | flops | bytes accessed | tf_op | source)
XLA Modules:
  0.0 92.7 jit_solution(5126621356063804304)
XLA Ops:
  0.6 2.0 %shard_map.95 = f32[256,128]{1,0:T(8,128)} custom-call(f32[16,16,128]{2,1,0:T(8,128)} %table_ref.1, s32[256,128]{1,0:T(8,128)} %bitcast.73), custom_call_target="tpu_custom_call" | custom-call | tf_op jit(solution)/shard_map/pallas_call | solution.py:68
  2.7 20.6 %all-to-all-start = ((f32[128,2,128]{2,1,0:T(2,128)}), f32[128,2,128]{2,1,0:T(2,128)S(1)}, u32[]{:S(2)}, u32[]{:S(2)}) async-start(f32[128,2,128]{2,1,0:T(2,128)} %bitcast.75), calls=%async_computation | async-start | bytes 262144 | tf_op jit(solution)/shard_map/all_to_all | solution.py:164
  23.2 0.0 copy-start.5
  23.2 0.6 copy-done.5
  23.9 0.1 fusion.1
  24.0 0.2 reduce_window_sum.11
  24.1 0.2 select_reduce_fusion.1
  24.3 0.1 fusion
  24.5 0.1 select_reduce_fusion
  24.6 0.4 copy-done.4
  25.0 0.2 rev.10
  25.2 0.0 copy-start.6
  25.2 0.6 copy-done.6
  25.9 15.5 %all-to-all-done = f32[128,2,128]{2,1,0:T(2,128)S(1)} async-done(((f32[128,2,128]{2,1,0:T(2,128)}), f32[128,2,128]{2,1,0:T(2,128)S(1)}, u32[]{:S(2)}, u32[]{:S(2)}) %all-to-all-start) | async-done | bytes 131104 | tf_op jit(solution)/shard_map/all_to_all | solution.py:164
  41.3 0.6 gather_fusion
  42.0 0.2 rev.9
  42.2 0.1 add_divide_fusion.8
  42.3 0.1 add_divide_fusion.7
  42.4 0.1 add_divide_fusion.6
  42.5 0.1 add_divide_fusion.5
  42.6 0.1 add_divide_fusion.4
  42.8 0.1 add_divide_fusion.3
  42.9 0.1 add_divide_fusion.2
  43.0 0.1 add_divide_fusion.1
  43.1 0.1 multiply_subtract_fusion
  43.2 0.2 rev.11
  43.4 0.1 broadcast_select_fusion
  43.5 0.0 copy-start.2
  43.5 0.8 copy-done.2
  44.3 0.0 copy-start
  44.4 0.0 copy-start.3
  44.4 1.0 %gather_fusion.1 = f32[256,256]{1,0:T(8,128)S(1)} fusion(f32[129,256]{1,0:T(8,128)S(1)} %select_maximum_fusion, s32[1024]{0:T(1024)S(1)} %pad_clamp_fusion), kind=kCustom, calls=%fused_computation.1 | custom fusion | bytes 525312 | tf_op jit(solution)/shard_map/gather | solution.py:182
  45.4 0.0 copy-start.1
  45.4 0.9 copy-done.1
  46.3 0.5 while.24
  46.8 3.1 %collective-permute-start = (f32[2,16,128]{2,1,0:T(8,128)S(1)}, f32[2,16,128]{2,1,0:T(8,128)S(1)}, u32[]{:S(2)}, u32[]{:S(2)}) collective-permute-start(f32[2,16,128]{2,1,0:T(8,128)S(1)} %pad_maximum_fusion), channel_id=1, source_target_pairs={{0,1},{1,2},{2,3},{4,5},{5,6},{6,7},{8,9},{9,10},{10,11},{12,13},{... | collective-permute-start | bytes 49160 | tf_op jit(solution)/shard_map/ppermute | solution.py:15
  49.9 4.4 %collective-permute-start.1 = (f32[2,16,128]{2,1,0:T(8,128)S(1)}, f32[2,16,128]{2,1,0:T(8,128)S(1)}, u32[]{:S(2)}, u32[]{:S(2)}) collective-permute-start(f32[2,16,128]{2,1,0:T(8,128)S(1)} %pad_maximum_fusion), channel_id=1, source_target_pairs={{0,2},{1,3},{4,6},{5,7},{8,10},{9,11},{12,14},{13,15},{16,18},{17,... | collective-permute-start | bytes 49160 | tf_op jit(solution)/shard_map/ppermute | solution.py:15
  54.3 1.3 %collective-permute-start.2 = (f32[2,16,128]{2,1,0:T(8,128)S(1)}, f32[2,16,128]{2,1,0:T(8,128)S(1)}, u32[]{:S(2)}, u32[]{:S(2)}) collective-permute-start(f32[2,16,128]{2,1,0:T(8,128)S(1)} %pad_maximum_fusion), channel_id=1, source_target_pairs={{0,3},{4,7},{8,11},{12,15},{16,19},{20,23},{24,27},{28,31},{32,35}... | collective-permute-start | bytes 49160 | tf_op jit(solution)/shard_map/ppermute | solution.py:15
  55.6 0.8 all_to_all.18
  56.4 0.6 broadcast_in_dim_reshape.3
  57.1 5.6 %all-to-all-start.1 = ((f32[128,2,256]{2,1,0:T(2,128)}), f32[128,2,256]{2,1,0:T(2,128)S(1)}, u32[]{:S(2)}, u32[]{:S(2)}) async-start(f32[128,2,256]{2,1,0:T(2,128)} %all_to_all.18), calls=%async_computation.1 | async-start | bytes 524288 | tf_op jit(solution)/shard_map/all_to_all | solution.py:183
  62.7 0.0 collective-permute-done.1
  62.7 0.8 while.23
  63.6 22.6 %all-to-all-done.1 = f32[128,2,256]{2,1,0:T(2,128)S(1)} async-done(((f32[128,2,256]{2,1,0:T(2,128)}), f32[128,2,256]{2,1,0:T(2,128)S(1)}, u32[]{:S(2)}, u32[]{:S(2)}) %all-to-all-start.1) | async-done | bytes 262176 | tf_op jit(solution)/shard_map/all_to_all | solution.py:183
  86.1 0.9 all_to_all.20.both_ref
  87.0 4.3 %shard_map.96 = f32[16,128]{1,0:T(8,128)} custom-call(s32[256,128]{1,0:T(8,128)} %bitcast.74, f32[256,256]{1,0:T(8,128)} %all_to_all.20.both_ref), custom_call_target="tpu_custom_call" | custom-call | tf_op jit(solution)/shard_map/pallas_call | solution.py:127
  91.3 0.7 slice_bitcast_fusion.1
  92.0 0.7 add_subtract_fusion
  (72 shorter events, 0.7 us)
Async XLA Ops:
  2.7 38.7 %all-to-all-start = ((f32[128,2,128]{2,1,0:T(2,128)}), f32[128,2,128]{2,1,0:T(2,128)S(1)}, u32[]{:S(2)}, u32[]{:S(2)}) async-start(f32[128,2,128]{2,1,0:T(2,128)} %bitcast.75), calls=%async_computation | async-start | bytes 262144 | tf_op jit(solution)/shard_map/all_to_all | solution.py:164
  23.2 0.7 copy-start.5
  24.1 0.8 copy-start.4
  25.2 0.7 copy-start.6
  43.5 0.8 copy-start.2
  44.3 1.0 %copy-start = (f32[16,16,128]{2,1,0:T(8,128)S(1)}, f32[16,16,128]{2,1,0:T(8,128)}, u32[]{:S(2)}) copy-start(f32[16,16,128]{2,1,0:T(8,128)} %table_ref.1) | copy-start | bytes 393220
  44.4 1.0 %copy-start.3 = (f32[16,16,128]{2,1,0:T(8,128)S(1)}, f32[16,16,128]{2,1,0:T(8,128)}, u32[]{:S(2)}) copy-start(f32[16,16,128]{2,1,0:T(8,128)} %param.14) | copy-start | bytes 393220
  45.4 0.9 copy-start.1
  46.8 15.9 %collective-permute-start = (f32[2,16,128]{2,1,0:T(8,128)S(1)}, f32[2,16,128]{2,1,0:T(8,128)S(1)}, u32[]{:S(2)}, u32[]{:S(2)}) collective-permute-start(f32[2,16,128]{2,1,0:T(8,128)S(1)} %pad_maximum_fusion), channel_id=1, source_target_pairs={{0,1},{1,2},{2,3},{4,5},{5,6},{6,7},{8,9},{9,10},{10,11},{12,13},{... | collective-permute-start | bytes 49160 | tf_op jit(solution)/shard_map/ppermute | solution.py:15
  49.9 12.8 %collective-permute-start.1 = (f32[2,16,128]{2,1,0:T(8,128)S(1)}, f32[2,16,128]{2,1,0:T(8,128)S(1)}, u32[]{:S(2)}, u32[]{:S(2)}) collective-permute-start(f32[2,16,128]{2,1,0:T(8,128)S(1)} %pad_maximum_fusion), channel_id=1, source_target_pairs={{0,2},{1,3},{4,6},{5,7},{8,10},{9,11},{12,14},{13,15},{16,18},{17,... | collective-permute-start | bytes 49160 | tf_op jit(solution)/shard_map/ppermute | solution.py:15
  54.3 8.4 %collective-permute-start.2 = (f32[2,16,128]{2,1,0:T(8,128)S(1)}, f32[2,16,128]{2,1,0:T(8,128)S(1)}, u32[]{:S(2)}, u32[]{:S(2)}) collective-permute-start(f32[2,16,128]{2,1,0:T(8,128)S(1)} %pad_maximum_fusion), channel_id=1, source_target_pairs={{0,3},{4,7},{8,11},{12,15},{16,19},{20,23},{24,27},{28,31},{32,35}... | collective-permute-start | bytes 49160 | tf_op jit(solution)/shard_map/ppermute | solution.py:15
  57.1 29.0 %all-to-all-start.1 = ((f32[128,2,256]{2,1,0:T(2,128)}), f32[128,2,256]{2,1,0:T(2,128)S(1)}, u32[]{:S(2)}, u32[]{:S(2)}) async-start(f32[128,2,256]{2,1,0:T(2,128)} %all_to_all.18), calls=%async_computation.1 | async-start | bytes 524288 | tf_op jit(solution)/shard_map/all_to_all | solution.py:183

commit v4 on v3

--- a/solution.py
+++ b/solution.py
@@ -93,8 +93,8 @@
     def body(i, totals):
         start = pl.multiple_of(i * 8, 8)
         ids = ids_ref[pl.ds(start, 8), :]
-        upper = both_ref[pl.ds(start, 8), pl.ds(0, 128)]
-        lower = both_ref[pl.ds(start, 8), pl.ds(128, 128)]
+        upper = both_ref[pl.ds(2 * start, 8, stride=2), :]
+        lower = both_ref[pl.ds(2 * start + 1, 8, stride=2), :]
         hots, parts = [], []
         for j in range(8):
             cell = ids[j : j + 1, :]
@@ -177,9 +177,11 @@
     filled = rows[None, :] == jnp.arange(slots, dtype=jnp.int32)[:, None]
     source = jnp.sum(jnp.where(filled, jnp.arange(seg_dev, dtype=jnp.int32)[None, :], 0), axis=1)
     used = jnp.any(filled, axis=1)
-    joined = jnp.concatenate([weights * updated, weights], axis=1)
-    joined = jnp.concatenate([joined, jnp.zeros((1, 2 * seg_len), jnp.float32)], axis=0)
-    package = joined[jnp.where(used, source, seg_dev)]
+    joined = jnp.concatenate(
+        [weights * updated, weights, jnp.zeros((1, seg_len), jnp.float32)], axis=0
+    )
+    picks = jnp.stack([source, source + seg_dev], axis=1)
+    package = joined[jnp.where(used[:, None], picks, 2 * seg_dev).reshape(-1)]
     returned = lax.all_to_all(package, ("gx", "gy"), split_axis=0, concat_axis=0, tiled=True)
     package, retention, gravity = lax.optimization_barrier((package, retention, gravity))
     inflow, burden = segregation(saturation, retention, gravity)

time: 93.1 us -> 92.3 us (level)
    all_to_all x2 -> x0, local copies, waits for them, and re-layouts: 1.73 us -> none  [on_device(): lax.all_to_all(package, ('gx', 'gy'), split_axis=0, concat_axis=0, tiled=...]
    unnamed x14 -> x16, local copies, waits for them, and re-layouts: 3.38 us -> 4.1 us
where the time goes in v4:
time: 92.3 us; the launch traced here: 91.8 us
  waiting for transfers between devices  37.7 us (41%)
  starting transfers between devices  34.3 us (37%)
  local copies, waits for them, and re-layouts  8.59 us (9%)
  Pallas kernels  6.29 us (7%)
  other arithmetic  3.12 us (3%)
  between operations  0.96 us (1%)
    all_to_all x1, waiting for transfers between devices, on_device(): lax.all_to_all(package, ('gx', 'gy'), split_axis=0, concat_axis=0, tiled=...  22.6 us
    all_to_all x1, starting transfers between devices, on_device(): lax.all_to_all(offered, ('gx', 'gy'), split_axis=0, concat_axis=0, tiled=...  20.6 us
    all_to_all x1, waiting for transfers between devices, on_device(): lax.all_to_all(offered, ('gx', 'gy'), split_axis=0, concat_axis=0, tiled=...  15.1 us
    ppermute x3, starting transfers between devices, from_behind(): return lax.ppermute(block, axis, route)  8.16 us
    all_to_all x1, starting transfers between devices, on_device(): lax.all_to_all(package, ('gx', 'gy'), split_axis=0, concat_axis=0, tiled=...  5.61 us
    pallas_call x1, Pallas kernels, scatter_cells(): pl.pallas_call(scatter_kernel, out_shape=jax.ShapeDtypeStruct((2 * map_ro...  4.26 us
    unnamed x16, local copies, waits for them, and re-layouts  4.1 us
    pallas_call x1, Pallas kernels, gather_cells(): pl.pallas_call(gather_kernel, out_shape=jax.ShapeDtypeStruct(local_map.sh...  2.03 us
  transfers between devices with their start and end apart: 5, of which 2 were waited for; matrix products, arithmetic and copies ran while one was open for 2% of the time, Pallas kernels for 0%

profile of v4, /device:TPU:1, one launch (start us, length us, event | category | flops | bytes accessed | tf_op | source)
XLA Modules:
  0.0 91.8 jit_solution(4612500097858723434)
XLA Ops:
  0.6 2.0 %shard_map.95 = f32[256,128]{1,0:T(8,128)} custom-call(f32[16,16,128]{2,1,0:T(8,128)} %table_ref.1, s32[256,128]{1,0:T(8,128)} %bitcast.77), custom_call_target="tpu_custom_call" | custom-call | tf_op jit(solution)/shard_map/pallas_call | solution.py:68
  2.7 20.6 %all-to-all-start = ((f32[128,2,128]{2,1,0:T(2,128)}), f32[128,2,128]{2,1,0:T(2,128)S(1)}, u32[]{:S(2)}, u32[]{:S(2)}) async-start(f32[128,2,128]{2,1,0:T(2,128)} %bitcast.79), calls=%async_computation | async-start | bytes 262144 | tf_op jit(solution)/shard_map/all_to_all | solution.py:164
  23.2 0.0 copy-start.6
  23.2 0.6 copy-done.6
  23.9 0.1 fusion.1
  24.0 0.2 reduce_window_sum.11
  24.2 0.2 select_reduce_fusion.1
  24.4 0.1 fusion
  24.5 0.1 select_reduce_fusion
  24.6 0.4 copy-done.5
  25.0 0.2 rev.10
  25.2 0.1 copy.11
  25.4 0.1 select_n.55
  25.5 0.0 copy-start.7
  25.6 0.6 copy-done.7
  26.2 15.1 %all-to-all-done = f32[128,2,128]{2,1,0:T(2,128)S(1)} async-done(((f32[128,2,128]{2,1,0:T(2,128)}), f32[128,2,128]{2,1,0:T(2,128)S(1)}, u32[]{:S(2)}, u32[]{:S(2)}) %all-to-all-start) | async-done | bytes 131104 | tf_op jit(solution)/shard_map/all_to_all | solution.py:164
  41.3 0.6 gather_fusion
  42.0 0.2 rev.9
  42.2 0.1 add_divide_fusion.8
  42.3 0.1 add_divide_fusion.7
  42.4 0.1 add_divide_fusion.6
  42.5 0.1 add_divide_fusion.5
  42.6 0.1 add_divide_fusion.4
  42.8 0.1 add_divide_fusion.3
  42.9 0.1 add_divide_fusion.2
  43.0 0.1 add_divide_fusion.1
  43.1 0.1 multiply_subtract_fusion
  43.2 0.2 rev.11
  43.4 0.1 broadcast_select_fusion
  43.5 0.0 copy-start.3
  43.5 0.8 copy-done.3
  44.3 0.1 maximum_maximum_fusion
  44.4 0.0 copy-start
  44.4 0.0 copy-start.4
  44.5 1.7 %gather_fusion.1 = f32[512,128]{1,0:T(8,128)} fusion(f32[257,128]{1,0:T(8,128)S(1)} %maximum_maximum_fusion, s32[1024]{0:T(1024)S(1)} %pad_clamp_fusion), kind=kCustom, calls=%fused_computation.1 | custom fusion | bytes 526336 | tf_op jit(solution)/shard_map/gather | solution.py:184
  46.1 0.9 copy-done.2
  47.0 0.5 while.24
  47.6 4.4 %collective-permute-start.2 = (f32[2,16,128]{2,1,0:T(8,128)S(1)}, f32[2,16,128]{2,1,0:T(8,128)S(1)}, u32[]{:S(2)}, u32[]{:S(2)}) collective-permute-start(f32[2,16,128]{2,1,0:T(8,128)S(1)} %pad_maximum_fusion), channel_id=1, source_target_pairs={{0,3},{4,7},{8,11},{12,15},{16,19},{20,23},{24,27},{28,31},{32,35}... | collective-permute-start | bytes 49160 | tf_op jit(solution)/shard_map/ppermute | solution.py:15
  52.0 1.3 %collective-permute-start.1 = (f32[2,16,128]{2,1,0:T(8,128)S(1)}, f32[2,16,128]{2,1,0:T(8,128)S(1)}, u32[]{:S(2)}, u32[]{:S(2)}) collective-permute-start(f32[2,16,128]{2,1,0:T(8,128)S(1)} %pad_maximum_fusion), channel_id=1, source_target_pairs={{0,2},{1,3},{4,6},{5,7},{8,10},{9,11},{12,14},{13,15},{16,18},{17,... | collective-permute-start | bytes 49160 | tf_op jit(solution)/shard_map/ppermute | solution.py:15
  53.3 2.5 %collective-permute-start = (f32[2,16,128]{2,1,0:T(8,128)S(1)}, f32[2,16,128]{2,1,0:T(8,128)S(1)}, u32[]{:S(2)}, u32[]{:S(2)}) collective-permute-start(f32[2,16,128]{2,1,0:T(8,128)S(1)} %pad_maximum_fusion), channel_id=1, source_target_pairs={{0,1},{1,2},{2,3},{4,5},{5,6},{6,7},{8,9},{9,10},{10,11},{12,13},{... | collective-permute-start | bytes 49160 | tf_op jit(solution)/shard_map/ppermute | solution.py:15
  55.8 0.6 broadcast_in_dim_reshape.3
  56.4 5.6 %all-to-all-start.1 = ((f32[128,4,128]{2,1,0:T(4,128)}), f32[128,4,128]{2,1,0:T(4,128)S(1)}, u32[]{:S(2)}, u32[]{:S(2)}) async-start(f32[128,4,128]{2,1,0:T(4,128)} %bitcast.15), calls=%async_computation.1 | async-start | bytes 524288 | tf_op jit(solution)/shard_map/all_to_all | solution.py:185
  62.1 0.8 while.23
  62.9 22.6 %all-to-all-done.1 = f32[128,4,128]{2,1,0:T(4,128)S(1)} async-done(((f32[128,4,128]{2,1,0:T(4,128)}), f32[128,4,128]{2,1,0:T(4,128)S(1)}, u32[]{:S(2)}, u32[]{:S(2)}) %all-to-all-start.1) | async-done | bytes 262176 | tf_op jit(solution)/shard_map/all_to_all | solution.py:185
  85.5 0.7 copy-done.1
  86.2 4.3 %shard_map.96 = f32[16,128]{1,0:T(8,128)} custom-call(s32[256,128]{1,0:T(8,128)} %bitcast.78, f32[512,128]{1,0:T(8,128)} %bitcast.70), custom_call_target="tpu_custom_call" | custom-call | tf_op jit(solution)/shard_map/pallas_call | solution.py:127
  90.4 0.7 slice_bitcast_fusion.1
  91.1 0.7 add_subtract_fusion
  (76 shorter events, 0.7 us)
Async XLA Ops:
  2.7 38.7 %all-to-all-start = ((f32[128,2,128]{2,1,0:T(2,128)}), f32[128,2,128]{2,1,0:T(2,128)S(1)}, u32[]{:S(2)}, u32[]{:S(2)}) async-start(f32[128,2,128]{2,1,0:T(2,128)} %bitcast.79), calls=%async_computation | async-start | bytes 262144 | tf_op jit(solution)/shard_map/all_to_all | solution.py:164
  23.2 0.7 copy-start.6
  24.2 0.8 copy-start.5
  25.5 0.7 copy-start.7
  43.5 0.8 copy-start.3
  44.4 1.7 %copy-start = (f32[16,16,128]{2,1,0:T(8,128)S(1)}, f32[16,16,128]{2,1,0:T(8,128)}, u32[]{:S(2)}) copy-start(f32[16,16,128]{2,1,0:T(8,128)} %table_ref.1) | copy-start | bytes 393220
  44.4 1.7 %copy-start.4 = (f32[16,16,128]{2,1,0:T(8,128)S(1)}, f32[16,16,128]{2,1,0:T(8,128)}, u32[]{:S(2)}) copy-start(f32[16,16,128]{2,1,0:T(8,128)} %param.14) | copy-start | bytes 393220
  46.1 0.9 copy-start.2
  47.6 14.4 %collective-permute-start.2 = (f32[2,16,128]{2,1,0:T(8,128)S(1)}, f32[2,16,128]{2,1,0:T(8,128)S(1)}, u32[]{:S(2)}, u32[]{:S(2)}) collective-permute-start(f32[2,16,128]{2,1,0:T(8,128)S(1)} %pad_maximum_fusion), channel_id=1, source_target_pairs={{0,3},{4,7},{8,11},{12,15},{16,19},{20,23},{24,27},{28,31},{32,35}... | collective-permute-start | bytes 49160 | tf_op jit(solution)/shard_map/ppermute | solution.py:15
  52.0 10.1 %collective-permute-start.1 = (f32[2,16,128]{2,1,0:T(8,128)S(1)}, f32[2,16,128]{2,1,0:T(8,128)S(1)}, u32[]{:S(2)}, u32[]{:S(2)}) collective-permute-start(f32[2,16,128]{2,1,0:T(8,128)S(1)} %pad_maximum_fusion), channel_id=1, source_target_pairs={{0,2},{1,3},{4,6},{5,7},{8,10},{9,11},{12,14},{13,15},{16,18},{17,... | collective-permute-start | bytes 49160 | tf_op jit(solution)/shard_map/ppermute | solution.py:15
  53.3 8.8 %collective-permute-start = (f32[2,16,128]{2,1,0:T(8,128)S(1)}, f32[2,16,128]{2,1,0:T(8,128)S(1)}, u32[]{:S(2)}, u32[]{:S(2)}) collective-permute-start(f32[2,16,128]{2,1,0:T(8,128)S(1)} %pad_maximum_fusion), channel_id=1, source_target_pairs={{0,1},{1,2},{2,3},{4,5},{5,6},{6,7},{8,9},{9,10},{10,11},{12,13},{... | collective-permute-start | bytes 49160 | tf_op jit(solution)/shard_map/ppermute | solution.py:15
  56.4 29.0 %all-to-all-start.1 = ((f32[128,4,128]{2,1,0:T(4,128)}), f32[128,4,128]{2,1,0:T(4,128)S(1)}, u32[]{:S(2)}, u32[]{:S(2)}) async-start(f32[128,4,128]{2,1,0:T(4,128)} %bitcast.15), calls=%async_computation.1 | async-start | bytes 524288 | tf_op jit(solution)/shard_map/all_to_all | solution.py:185
  85.5 0.7 copy-start.1

commit v5 on v4

--- a/solution.py
+++ b/solution.py
@@ -78,7 +78,7 @@
 
 
 def scatter_kernel(ids_ref, both_ref, out_ref):
-    map_rows = out_ref.shape[0] // 2
+    map_rows = out_ref.shape[1]
     tiles = ids_ref.shape[0] // 8
     lanes = lax.broadcasted_iota(jnp.int32, (128, 128), 0)
     levels = lax.broadcasted_iota(jnp.int32, (map_rows, 128), 0)
@@ -120,13 +120,15 @@
         0, tiles, body, jnp.zeros((6 * map_rows, 128), jnp.float32), unroll=True
     )
     span = 2 * map_rows
-    out_ref[...] = (totals[:span] + totals[span : 2 * span]) + totals[2 * span :]
+    summed = (totals[:span] + totals[span : 2 * span]) + totals[2 * span :]
+    out_ref[0] = summed[:map_rows]
+    out_ref[1] = summed[map_rows:]
 
 
 def scatter_cells(local_map, both, map_rows):
     return pl.pallas_call(
         scatter_kernel,
-        out_shape=jax.ShapeDtypeStruct((2 * map_rows, 128), jnp.float32),
+        out_shape=jax.ShapeDtypeStruct((2, map_rows, 128), jnp.float32),
         in_specs=[pl.BlockSpec(memory_space=pltpu.VMEM)] * 2,
         out_specs=pl.BlockSpec(memory_space=pltpu.VMEM),
     )(local_map, both)
@@ -186,10 +188,11 @@
     package, retention, gravity = lax.optimization_barrier((package, retention, gravity))
     inflow, burden = segregation(saturation, retention, gravity)
     sums = scatter_cells(local_map, returned, map_rows)
-    padding = jnp.zeros((cell_count - map_rows * 128,), jnp.float32)
-    numerator = jnp.concatenate([sums[:map_rows].reshape(-1), padding])
-    denominator = jnp.concatenate([sums[map_rows:].reshape(-1), padding])
-    mixed = ((flat + numerator) / (1.0 + denominator)).reshape(layers, rows_x, rows_y)
+    head_rows = (map_rows * 128) // rows_y
+    cover = ((0, layers - 1), (0, rows_x - head_rows), (0, 0))
+    numerator = jnp.pad(sums[0].reshape(1, head_rows, rows_y), cover)
+    denominator = jnp.pad(sums[1].reshape(1, head_rows, rows_y), cover)
+    mixed = (saturation + numerator) / (1.0 + denominator)
     final_sat = mixed + inflow - burden
     return (final_sat, updated[None])
 

time: 92.3 us -> 92.3 us (level)
  no operation moved by 1% of the time
where the time goes in v5:
time: 92.3 us; the launch traced here: 91.8 us
  waiting for transfers between devices  37.7 us (41%)
  starting transfers between devices  34.3 us (37%)
  local copies, waits for them, and re-layouts  8.59 us (9%)
  Pallas kernels  6.29 us (7%)
  other arithmetic  3.11 us (3%)
  between operations  0.95 us (1%)
    all_to_all x1, waiting for transfers between devices, on_device(): lax.all_to_all(package, ('gx', 'gy'), split_axis=0, concat_axis=0, tiled=...  22.6 us
    all_to_all x1, starting transfers between devices, on_device(): lax.all_to_all(offered, ('gx', 'gy'), split_axis=0, concat_axis=0, tiled=...  20.6 us
    all_to_all x1, waiting for transfers between devices, on_device(): lax.all_to_all(offered, ('gx', 'gy'), split_axis=0, concat_axis=0, tiled=...  15.1 us
    ppermute x3, starting transfers between devices, from_behind(): return lax.ppermute(block, axis, route)  8.16 us
    all_to_all x1, starting transfers between devices, on_device(): lax.all_to_all(package, ('gx', 'gy'), split_axis=0, concat_axis=0, tiled=...  5.61 us
    pallas_call x1, Pallas kernels, scatter_cells(): pl.pallas_call(scatter_kernel, out_shape=jax.ShapeDtypeStruct((2, map_row...  4.26 us
    unnamed x16, local copies, waits for them, and re-layouts  4.1 us
    pallas_call x1, Pallas kernels, gather_cells(): pl.pallas_call(gather_kernel, out_shape=jax.ShapeDtypeStruct(local_map.sh...  2.03 us
  transfers between devices with their start and end apart: 5, of which 2 were waited for; matrix products, arithmetic and copies ran while one was open for 2% of the time, Pallas kernels for 0%

profile of v5, /device:TPU:1, one launch (start us, length us, event | category | flops | bytes accessed | tf_op | source)
XLA Modules:
  0.0 91.8 jit_solution(15357317729454999219)
XLA Ops:
  0.6 2.0 %shard_map.95 = f32[256,128]{1,0:T(8,128)} custom-call(f32[16,16,128]{2,1,0:T(8,128)} %table_ref.1, s32[256,128]{1,0:T(8,128)} %bitcast.70), custom_call_target="tpu_custom_call" | custom-call | tf_op jit(solution)/shard_map/pallas_call | solution.py:68
  2.7 20.6 %all-to-all-start = ((f32[128,2,128]{2,1,0:T(2,128)}), f32[128,2,128]{2,1,0:T(2,128)S(1)}, u32[]{:S(2)}, u32[]{:S(2)}) async-start(f32[128,2,128]{2,1,0:T(2,128)} %bitcast.72), calls=%async_computation | async-start | bytes 262144 | tf_op jit(solution)/shard_map/all_to_all | solution.py:166
  23.2 0.0 copy-start.6
  23.2 0.6 copy-done.6
  23.9 0.1 fusion.1
  24.0 0.2 reduce_window_sum.11
  24.2 0.2 select_reduce_fusion.1
  24.4 0.1 fusion
  24.5 0.1 select_reduce_fusion
  24.6 0.4 copy-done.5
  25.0 0.2 rev.10
  25.2 0.1 copy.11
  25.4 0.1 select_n.55
  25.5 0.0 copy-start.7
  25.6 0.6 copy-done.7
  26.2 15.1 %all-to-all-done = f32[128,2,128]{2,1,0:T(2,128)S(1)} async-done(((f32[128,2,128]{2,1,0:T(2,128)}), f32[128,2,128]{2,1,0:T(2,128)S(1)}, u32[]{:S(2)}, u32[]{:S(2)}) %all-to-all-start) | async-done | bytes 131104 | tf_op jit(solution)/shard_map/all_to_all | solution.py:166
  41.3 0.6 gather_fusion
  42.0 0.2 rev.9
  42.2 0.1 add_divide_fusion.7
  42.3 0.1 add_divide_fusion.6
  42.4 0.1 add_divide_fusion.5
  42.5 0.1 add_divide_fusion.4
  42.6 0.1 add_divide_fusion.3
  42.8 0.1 add_divide_fusion.2
  42.9 0.1 add_divide_fusion.1
  43.0 0.1 add_divide_fusion
  43.1 0.1 multiply_subtract_fusion
  43.2 0.2 rev.11
  43.4 0.1 broadcast_select_fusion
  43.5 0.0 copy-start.4
  43.5 0.8 copy-done.4
  44.3 0.1 maximum_maximum_fusion
  44.4 0.0 copy-start
  44.4 0.0 copy-start.2
  44.5 1.7 %gather_fusion.1 = f32[512,128]{1,0:T(8,128)} fusion(f32[257,128]{1,0:T(8,128)S(1)} %maximum_maximum_fusion, s32[1024]{0:T(1024)S(1)} %pad_clamp_fusion), kind=kCustom, calls=%fused_computation.1 | custom fusion | bytes 526336 | tf_op jit(solution)/shard_map/gather | solution.py:186
  46.1 0.9 copy-done.3
  47.0 0.5 while.24
  47.6 4.4 %collective-permute-start.2 = (f32[2,16,128]{2,1,0:T(8,128)S(1)}, f32[2,16,128]{2,1,0:T(8,128)S(1)}, u32[]{:S(2)}, u32[]{:S(2)}) collective-permute-start(f32[2,16,128]{2,1,0:T(8,128)S(1)} %pad_maximum_fusion), channel_id=1, source_target_pairs={{0,3},{4,7},{8,11},{12,15},{16,19},{20,23},{24,27},{28,31},{32,35}... | collective-permute-start | bytes 49160 | tf_op jit(solution)/shard_map/ppermute | solution.py:15
  52.0 1.3 %collective-permute-start.1 = (f32[2,16,128]{2,1,0:T(8,128)S(1)}, f32[2,16,128]{2,1,0:T(8,128)S(1)}, u32[]{:S(2)}, u32[]{:S(2)}) collective-permute-start(f32[2,16,128]{2,1,0:T(8,128)S(1)} %pad_maximum_fusion), channel_id=1, source_target_pairs={{0,2},{1,3},{4,6},{5,7},{8,10},{9,11},{12,14},{13,15},{16,18},{17,... | collective-permute-start | bytes 49160 | tf_op jit(solution)/shard_map/ppermute | solution.py:15
  53.3 2.5 %collective-permute-start = (f32[2,16,128]{2,1,0:T(8,128)S(1)}, f32[2,16,128]{2,1,0:T(8,128)S(1)}, u32[]{:S(2)}, u32[]{:S(2)}) collective-permute-start(f32[2,16,128]{2,1,0:T(8,128)S(1)} %pad_maximum_fusion), channel_id=1, source_target_pairs={{0,1},{1,2},{2,3},{4,5},{5,6},{6,7},{8,9},{9,10},{10,11},{12,13},{... | collective-permute-start | bytes 49160 | tf_op jit(solution)/shard_map/ppermute | solution.py:15
  55.8 0.6 broadcast_in_dim_reshape.3
  56.4 5.6 %all-to-all-start.1 = ((f32[128,4,128]{2,1,0:T(4,128)}), f32[128,4,128]{2,1,0:T(4,128)S(1)}, u32[]{:S(2)}, u32[]{:S(2)}) async-start(f32[128,4,128]{2,1,0:T(4,128)} %bitcast.14), calls=%async_computation.1 | async-start | bytes 524288 | tf_op jit(solution)/shard_map/all_to_all | solution.py:187
  62.1 0.8 while.23
  62.9 22.6 %all-to-all-done.1 = f32[128,4,128]{2,1,0:T(4,128)S(1)} async-done(((f32[128,4,128]{2,1,0:T(4,128)}), f32[128,4,128]{2,1,0:T(4,128)S(1)}, u32[]{:S(2)}, u32[]{:S(2)}) %all-to-all-start.1) | async-done | bytes 262176 | tf_op jit(solution)/shard_map/all_to_all | solution.py:187
  85.5 0.7 copy-done.1
  86.2 4.3 %shard_map.96 = f32[2,8,128]{2,1,0:T(8,128)} custom-call(s32[256,128]{1,0:T(8,128)} %bitcast.71, f32[512,128]{1,0:T(8,128)} %bitcast.63), custom_call_target="tpu_custom_call" | custom-call | tf_op jit(solution)/shard_map/pallas_call | solution.py:129
  90.4 0.7 fusion.6
  91.1 0.7 add_subtract_fusion
  (75 shorter events, 0.7 us)
Async XLA Ops:
  2.7 38.7 %all-to-all-start = ((f32[128,2,128]{2,1,0:T(2,128)}), f32[128,2,128]{2,1,0:T(2,128)S(1)}, u32[]{:S(2)}, u32[]{:S(2)}) async-start(f32[128,2,128]{2,1,0:T(2,128)} %bitcast.72), calls=%async_computation | async-start | bytes 262144 | tf_op jit(solution)/shard_map/all_to_all | solution.py:166
  23.2 0.7 copy-start.6
  24.2 0.8 copy-start.5
  25.5 0.7 copy-start.7
  43.5 0.8 copy-start.4
  44.4 1.7 %copy-start = (f32[16,16,128]{2,1,0:T(8,128)S(1)}, f32[16,16,128]{2,1,0:T(8,128)}, u32[]{:S(2)}) copy-start(f32[16,16,128]{2,1,0:T(8,128)} %table_ref.1) | copy-start | bytes 393220
  44.4 1.7 %copy-start.2 = (f32[16,16,128]{2,1,0:T(8,128)S(1)}, f32[16,16,128]{2,1,0:T(8,128)}, u32[]{:S(2)}) copy-start(f32[16,16,128]{2,1,0:T(8,128)} %param.14) | copy-start | bytes 393220
  46.1 0.9 copy-start.3
  47.6 14.4 %collective-permute-start.2 = (f32[2,16,128]{2,1,0:T(8,128)S(1)}, f32[2,16,128]{2,1,0:T(8,128)S(1)}, u32[]{:S(2)}, u32[]{:S(2)}) collective-permute-start(f32[2,16,128]{2,1,0:T(8,128)S(1)} %pad_maximum_fusion), channel_id=1, source_target_pairs={{0,3},{4,7},{8,11},{12,15},{16,19},{20,23},{24,27},{28,31},{32,35}... | collective-permute-start | bytes 49160 | tf_op jit(solution)/shard_map/ppermute | solution.py:15
  52.0 10.1 %collective-permute-start.1 = (f32[2,16,128]{2,1,0:T(8,128)S(1)}, f32[2,16,128]{2,1,0:T(8,128)S(1)}, u32[]{:S(2)}, u32[]{:S(2)}) collective-permute-start(f32[2,16,128]{2,1,0:T(8,128)S(1)} %pad_maximum_fusion), channel_id=1, source_target_pairs={{0,2},{1,3},{4,6},{5,7},{8,10},{9,11},{12,14},{13,15},{16,18},{17,... | collective-permute-start | bytes 49160 | tf_op jit(solution)/shard_map/ppermute | solution.py:15
  53.3 8.8 %collective-permute-start = (f32[2,16,128]{2,1,0:T(8,128)S(1)}, f32[2,16,128]{2,1,0:T(8,128)S(1)}, u32[]{:S(2)}, u32[]{:S(2)}) collective-permute-start(f32[2,16,128]{2,1,0:T(8,128)S(1)} %pad_maximum_fusion), channel_id=1, source_target_pairs={{0,1},{1,2},{2,3},{4,5},{5,6},{6,7},{8,9},{9,10},{10,11},{12,13},{... | collective-permute-start | bytes 49160 | tf_op jit(solution)/shard_map/ppermute | solution.py:15
  56.4 29.0 %all-to-all-start.1 = ((f32[128,4,128]{2,1,0:T(4,128)}), f32[128,4,128]{2,1,0:T(4,128)S(1)}, u32[]{:S(2)}, u32[]{:S(2)}) async-start(f32[128,4,128]{2,1,0:T(4,128)} %bitcast.14), calls=%async_computation.1 | async-start | bytes 524288 | tf_op jit(solution)/shard_map/all_to_all | solution.py:187
  85.5 0.7 copy-start.1

commit v6 on v5

--- a/solution.py
+++ b/solution.py
@@ -21,14 +21,15 @@
 
 def transport(node_sat, increments, reversed_flag):
     flipped = reversed_flag[..., None] == 1
-    state = jnp.where(flipped, node_sat[..., ::-1], node_sat)
-    ratio = jnp.where(flipped, increments[..., ::-1], increments)
+    state = node_sat
     inlet = jnp.ones(state.shape[:-1] + (1,), jnp.float32)
     for _ in range(BL_STEPS):
         flows = frac_flow(state)
-        upstream = jnp.concatenate([inlet, flows[..., :-1]], axis=-1)
-        state = state - ratio * (flows - upstream)
-    return jnp.where(flipped, state[..., ::-1], state)
+        from_left = jnp.concatenate([inlet, flows[..., :-1]], axis=-1)
+        from_right = jnp.concatenate([flows[..., 1:], inlet], axis=-1)
+        upstream = jnp.where(flipped, from_right, from_left)
+        state = state - increments * (flows - upstream)
+    return state
 
 
 def slot_rows(owners, groups, capacity):

time: 92.3 us -> 92.5 us (level)
  no operation moved by 1% of the time
where the time goes in v6:
time: 92.5 us; the launch traced here: 92 us
  waiting for transfers between devices  37.9 us (41%)
  starting transfers between devices  34.3 us (37%)
  local copies, waits for them, and re-layouts  8.7 us (9%)
  Pallas kernels  6.29 us (7%)
  other arithmetic  2.99 us (3%)
  between operations  0.98 us (1%)
    all_to_all x1, waiting for transfers between devices, on_device(): lax.all_to_all(package, ('gx', 'gy'), split_axis=0, concat_axis=0, tiled=...  22.6 us
    all_to_all x1, starting transfers between devices, on_device(): lax.all_to_all(offered, ('gx', 'gy'), split_axis=0, concat_axis=0, tiled=...  20.6 us
    all_to_all x1, waiting for transfers between devices, on_device(): lax.all_to_all(offered, ('gx', 'gy'), split_axis=0, concat_axis=0, tiled=...  15.3 us
    ppermute x3, starting transfers between devices, from_behind(): return lax.ppermute(block, axis, route)  8.16 us
    all_to_all x1, starting transfers between devices, on_device(): lax.all_to_all(package, ('gx', 'gy'), split_axis=0, concat_axis=0, tiled=...  5.61 us
    pallas_call x1, Pallas kernels, scatter_cells(): pl.pallas_call(scatter_kernel, out_shape=jax.ShapeDtypeStruct((2, map_row...  4.26 us
    unnamed x16, local copies, waits for them, and re-layouts  4.11 us
    pallas_call x1, Pallas kernels, gather_cells(): pl.pallas_call(gather_kernel, out_shape=jax.ShapeDtypeStruct(local_map.sh...  2.03 us
  transfers between devices with their start and end apart: 5, of which 2 were waited for; matrix products, arithmetic and copies ran while one was open for 2% of the time, Pallas kernels for 0%

profile of v6, /device:TPU:1, one launch (start us, length us, event | category | flops | bytes accessed | tf_op | source)
XLA Modules:
  0.0 92.0 jit_solution(11282317048598067500)
XLA Ops:
  0.6 2.0 %shard_map.95 = f32[256,128]{1,0:T(8,128)} custom-call(f32[16,16,128]{2,1,0:T(8,128)} %table_ref.1, s32[256,128]{1,0:T(8,128)} %bitcast.56), custom_call_target="tpu_custom_call" | custom-call | tf_op jit(solution)/shard_map/pallas_call | solution.py:69
  2.7 20.6 %all-to-all-start = ((f32[128,2,128]{2,1,0:T(2,128)}), f32[128,2,128]{2,1,0:T(2,128)S(1)}, u32[]{:S(2)}, u32[]{:S(2)}) async-start(f32[128,2,128]{2,1,0:T(2,128)} %bitcast.58), calls=%async_computation | async-start | bytes 262144 | tf_op jit(solution)/shard_map/all_to_all | solution.py:167
  23.2 0.6 copy-done.6
  23.9 0.1 fusion.1
  24.0 0.2 reduce_window_sum.11
  24.2 0.2 select_reduce_fusion.1
  24.4 0.1 fusion
  24.5 0.1 select_reduce_fusion
  24.6 0.4 copy-done.5
  25.1 0.1 copy.11
  25.2 0.1 select_n.75
  25.4 0.0 copy-start.7
  25.4 0.6 copy-done.7
  26.0 15.3 %all-to-all-done = f32[128,2,128]{2,1,0:T(2,128)S(1)} async-done(((f32[128,2,128]{2,1,0:T(2,128)}), f32[128,2,128]{2,1,0:T(2,128)S(1)}, u32[]{:S(2)}, u32[]{:S(2)}) %all-to-all-start) | async-done | bytes 131104 | tf_op jit(solution)/shard_map/all_to_all | solution.py:167
  41.3 0.6 gather_fusion
  42.0 0.1 fusion.13
  42.1 0.1 add_divide_fusion.6
  42.2 0.1 fusion.12
  42.3 0.1 add_divide_fusion.5
  42.5 0.1 fusion.11
  42.5 0.1 add_divide_fusion.4
  42.7 0.1 fusion.10
  42.7 0.1 add_divide_fusion.3
  42.9 0.1 fusion.9
  42.9 0.1 add_divide_fusion.2
  43.1 0.1 fusion.8
  43.1 0.1 add_divide_fusion.1
  43.3 0.1 fusion.7
  43.3 0.1 add_divide_fusion
  43.5 0.1 fusion.6
  43.5 0.1 multiply_subtract_fusion
  43.7 0.8 copy-done.4
  44.5 0.1 maximum_maximum_fusion
  44.6 0.0 copy-start.2
  44.6 1.6 %gather_fusion.1 = f32[512,128]{1,0:T(8,128)} fusion(f32[257,128]{1,0:T(8,128)S(1)} %maximum_maximum_fusion, s32[1024]{0:T(1024)S(1)} %pad_clamp_fusion), kind=kCustom, calls=%fused_computation.1 | custom fusion | bytes 526336 | tf_op jit(solution)/shard_map/gather | solution.py:187
  46.3 0.9 copy-done.3
  47.2 0.5 while.24
  47.8 4.4 %collective-permute-start.2 = (f32[2,16,128]{2,1,0:T(8,128)S(1)}, f32[2,16,128]{2,1,0:T(8,128)S(1)}, u32[]{:S(2)}, u32[]{:S(2)}) collective-permute-start(f32[2,16,128]{2,1,0:T(8,128)S(1)} %pad_maximum_fusion), channel_id=1, source_target_pairs={{0,3},{4,7},{8,11},{12,15},{16,19},{20,23},{24,27},{28,31},{32,35}... | collective-permute-start | bytes 49160 | tf_op jit(solution)/shard_map/ppermute | solution.py:15
  52.2 1.3 %collective-permute-start.1 = (f32[2,16,128]{2,1,0:T(8,128)S(1)}, f32[2,16,128]{2,1,0:T(8,128)S(1)}, u32[]{:S(2)}, u32[]{:S(2)}) collective-permute-start(f32[2,16,128]{2,1,0:T(8,128)S(1)} %pad_maximum_fusion), channel_id=1, source_target_pairs={{0,2},{1,3},{4,6},{5,7},{8,10},{9,11},{12,14},{13,15},{16,18},{17,... | collective-permute-start | bytes 49160 | tf_op jit(solution)/shard_map/ppermute | solution.py:15
  53.4 2.5 %collective-permute-start = (f32[2,16,128]{2,1,0:T(8,128)S(1)}, f32[2,16,128]{2,1,0:T(8,128)S(1)}, u32[]{:S(2)}, u32[]{:S(2)}) collective-permute-start(f32[2,16,128]{2,1,0:T(8,128)S(1)} %pad_maximum_fusion), channel_id=1, source_target_pairs={{0,1},{1,2},{2,3},{4,5},{5,6},{6,7},{8,9},{9,10},{10,11},{12,13},{... | collective-permute-start | bytes 49160 | tf_op jit(solution)/shard_map/ppermute | solution.py:15
  56.0 0.6 broadcast_in_dim_reshape.3
  56.6 5.6 %all-to-all-start.1 = ((f32[128,4,128]{2,1,0:T(4,128)}), f32[128,4,128]{2,1,0:T(4,128)S(1)}, u32[]{:S(2)}, u32[]{:S(2)}) async-start(f32[128,4,128]{2,1,0:T(4,128)} %bitcast.14), calls=%async_computation.1 | async-start | bytes 524288 | tf_op jit(solution)/shard_map/all_to_all | solution.py:188
  62.3 0.8 while.23
  63.1 22.6 %all-to-all-done.1 = f32[128,4,128]{2,1,0:T(4,128)S(1)} async-done(((f32[128,4,128]{2,1,0:T(4,128)}), f32[128,4,128]{2,1,0:T(4,128)S(1)}, u32[]{:S(2)}, u32[]{:S(2)}) %all-to-all-start.1) | async-done | bytes 262176 | tf_op jit(solution)/shard_map/all_to_all | solution.py:188
  85.6 0.7 copy-done.1
  86.3 4.3 %shard_map.96 = f32[2,8,128]{2,1,0:T(8,128)} custom-call(s32[256,128]{1,0:T(8,128)} %bitcast.57, f32[512,128]{1,0:T(8,128)} %bitcast.55), custom_call_target="tpu_custom_call" | custom-call | tf_op jit(solution)/shard_map/pallas_call | solution.py:130
  90.6 0.7 fusion.14
  91.3 0.7 add_subtract_fusion
  (79 shorter events, 0.7 us)
Async XLA Ops:
  2.7 38.7 %all-to-all-start = ((f32[128,2,128]{2,1,0:T(2,128)}), f32[128,2,128]{2,1,0:T(2,128)S(1)}, u32[]{:S(2)}, u32[]{:S(2)}) async-start(f32[128,2,128]{2,1,0:T(2,128)} %bitcast.58), calls=%async_computation | async-start | bytes 262144 | tf_op jit(solution)/shard_map/all_to_all | solution.py:167
  23.2 0.7 copy-start.6
  24.2 0.8 copy-start.5
  25.4 0.7 copy-start.7
  43.6 0.8 copy-start.4
  44.6 1.7 %copy-start = (f32[16,16,128]{2,1,0:T(8,128)S(1)}, f32[16,16,128]{2,1,0:T(8,128)}, u32[]{:S(2)}) copy-start(f32[16,16,128]{2,1,0:T(8,128)} %table_ref.1) | copy-start | bytes 393220
  44.6 1.7 %copy-start.2 = (f32[16,16,128]{2,1,0:T(8,128)S(1)}, f32[16,16,128]{2,1,0:T(8,128)}, u32[]{:S(2)}) copy-start(f32[16,16,128]{2,1,0:T(8,128)} %param.14) | copy-start | bytes 393220
  46.3 0.9 copy-start.3
  47.8 14.4 %collective-permute-start.2 = (f32[2,16,128]{2,1,0:T(8,128)S(1)}, f32[2,16,128]{2,1,0:T(8,128)S(1)}, u32[]{:S(2)}, u32[]{:S(2)}) collective-permute-start(f32[2,16,128]{2,1,0:T(8,128)S(1)} %pad_maximum_fusion), channel_id=1, source_target_pairs={{0,3},{4,7},{8,11},{12,15},{16,19},{20,23},{24,27},{28,31},{32,35}... | collective-permute-start | bytes 49160 | tf_op jit(solution)/shard_map/ppermute | solution.py:15
  52.2 10.1 %collective-permute-start.1 = (f32[2,16,128]{2,1,0:T(8,128)S(1)}, f32[2,16,128]{2,1,0:T(8,128)S(1)}, u32[]{:S(2)}, u32[]{:S(2)}) collective-permute-start(f32[2,16,128]{2,1,0:T(8,128)S(1)} %pad_maximum_fusion), channel_id=1, source_target_pairs={{0,2},{1,3},{4,6},{5,7},{8,10},{9,11},{12,14},{13,15},{16,18},{17,... | collective-permute-start | bytes 49160 | tf_op jit(solution)/shard_map/ppermute | solution.py:15
  53.4 8.8 %collective-permute-start = (f32[2,16,128]{2,1,0:T(8,128)S(1)}, f32[2,16,128]{2,1,0:T(8,128)S(1)}, u32[]{:S(2)}, u32[]{:S(2)}) collective-permute-start(f32[2,16,128]{2,1,0:T(8,128)S(1)} %pad_maximum_fusion), channel_id=1, source_target_pairs={{0,1},{1,2},{2,3},{4,5},{5,6},{6,7},{8,9},{9,10},{10,11},{12,13},{... | collective-permute-start | bytes 49160 | tf_op jit(solution)/shard_map/ppermute | solution.py:15
  56.6 29.0 %all-to-all-start.1 = ((f32[128,4,128]{2,1,0:T(4,128)}), f32[128,4,128]{2,1,0:T(4,128)S(1)}, u32[]{:S(2)}, u32[]{:S(2)}) async-start(f32[128,4,128]{2,1,0:T(4,128)} %bitcast.14), calls=%async_computation.1 | async-start | bytes 524288 | tf_op jit(solution)/shard_map/all_to_all | solution.py:188
  85.6 0.7 copy-start.1

commit v7 on v6

--- a/solution.py
+++ b/solution.py
@@ -167,7 +167,14 @@
     arrived = lax.all_to_all(offered, ("gx", "gy"), split_axis=0, concat_axis=0, tiled=True)
     owners = owner_id[0, :, 0]
     rows = slot_rows(owners, groups, capacity)
-    node_in = arrived[rows]
+    slots = groups * capacity
+    filled = rows[None, :] == jnp.arange(slots, dtype=jnp.int32)[:, None]
+    node_in = jnp.dot(
+        filled.T.astype(jnp.float32),
+        arrived,
+        precision=lax.Precision.HIGHEST,
+        preferred_element_type=jnp.float32,
+    )
     seg_dev = node_in.shape[0]
     updated = transport(
         node_in.reshape(seg_dev // 2, 2 * seg_len),
@@ -176,15 +183,15 @@
     )
     updated = updated.reshape(seg_dev, seg_len)
     weights = node_weight[0]
-    slots = groups * capacity
-    filled = rows[None, :] == jnp.arange(slots, dtype=jnp.int32)[:, None]
-    source = jnp.sum(jnp.where(filled, jnp.arange(seg_dev, dtype=jnp.int32)[None, :], 0), axis=1)
-    used = jnp.any(filled, axis=1)
-    joined = jnp.concatenate(
-        [weights * updated, weights, jnp.zeros((1, seg_len), jnp.float32)], axis=0
-    )
-    picks = jnp.stack([source, source + seg_dev], axis=1)
-    package = joined[jnp.where(used[:, None], picks, 2 * seg_dev).reshape(-1)]
+    joined = jnp.concatenate([weights * updated, weights], axis=0)
+    halves = jnp.arange(2, dtype=jnp.int32)
+    spread = (filled[:, None, None, :] & (halves[None, :, None, None] == halves[None, None, :, None]))
+    package = jnp.dot(
+        spread.reshape(2 * slots, 2 * seg_dev).astype(jnp.float32),
+        joined,
+        precision=lax.Precision.HIGHEST,
+        preferred_element_type=jnp.float32,
+    )
     returned = lax.all_to_all(package, ("gx", "gy"), split_axis=0, concat_axis=0, tiled=True)
     package, retention, gravity = lax.optimization_barrier((package, retention, gravity))
     inflow, burden = segregation(saturation, retention, gravity)

time: 92.5 us -> 92 us (level)
  local copies, waits for them, and re-layouts: 8.7 us -> 6.38 us
  matrix products: 0 us -> 1.38 us
    gather x2 -> x0, local copies, waits for them, and re-layouts: 2.29 us -> none  [the longest x1 1.65 us: on_device(): package = joined[jnp.where(used[:, None], picks, 2 * seg_dev).reshape(-1)]]
    dot_general x0 -> x2, matrix products: none -> 1.38 us  [the longest x1 1.09 us: on_device(): jnp.dot(spread.reshape(2 * slots, 2 * seg_dev).astype(jnp.float32), joine...]
where the time goes in v7:
time: 92 us; the launch traced here: 91.6 us
  waiting for transfers between devices  37.9 us (41%)
  starting transfers between devices  34.9 us (38%)
  local copies, waits for them, and re-layouts  6.38 us (7%)
  Pallas kernels  6.29 us (7%)
  other arithmetic  3 us (3%)
  matrix products  1.38 us (2%)
  between operations  0.92 us (1%)
    all_to_all x1, waiting for transfers between devices, on_device(): lax.all_to_all(package, ('gx', 'gy'), split_axis=0, concat_axis=0, tiled=...  22.6 us
    all_to_all x1, starting transfers between devices, on_device(): lax.all_to_all(offered, ('gx', 'gy'), split_axis=0, concat_axis=0, tiled=...  20.6 us
    all_to_all x1, waiting for transfers between devices, on_device(): lax.all_to_all(offered, ('gx', 'gy'), split_axis=0, concat_axis=0, tiled=...  15.3 us
    ppermute x3, starting transfers between devices, from_behind(): return lax.ppermute(block, axis, route)  8.77 us
    all_to_all x1, starting transfers between devices, on_device(): lax.all_to_all(package, ('gx', 'gy'), split_axis=0, concat_axis=0, tiled=...  5.61 us
    unnamed x16, local copies, waits for them, and re-layouts  4.36 us
    pallas_call x1, Pallas kernels, scatter_cells(): pl.pallas_call(scatter_kernel, out_shape=jax.ShapeDtypeStruct((2, map_row...  4.26 us
    pallas_call x1, Pallas kernels, gather_cells(): pl.pallas_call(gather_kernel, out_shape=jax.ShapeDtypeStruct(local_map.sh...  2.03 us
  transfers between devices with their start and end apart: 5, of which 2 were waited for; matrix products, arithmetic and copies ran while one was open for 2% of the time, Pallas kernels for 0%

profile of v7, /device:TPU:1, one launch (start us, length us, event | category | flops | bytes accessed | tf_op | source)
XLA Modules:
  0.0 91.6 jit_solution(12900373390384087092)
XLA Ops:
  0.6 2.0 %shard_map.95 = f32[256,128]{1,0:T(8,128)} custom-call(f32[16,16,128]{2,1,0:T(8,128)} %table_ref.1, s32[256,128]{1,0:T(8,128)} %bitcast.50), custom_call_target="tpu_custom_call" | custom-call | tf_op jit(solution)/shard_map/pallas_call | solution.py:69
  2.7 20.6 %all-to-all-start = ((f32[128,2,128]{2,1,0:T(2,128)}), f32[128,2,128]{2,1,0:T(2,128)S(1)}, u32[]{:S(2)}, u32[]{:S(2)}) async-start(f32[128,2,128]{2,1,0:T(2,128)} %bitcast.52), calls=%async_computation | async-start | bytes 262144 | tf_op jit(solution)/shard_map/all_to_all | solution.py:167
  23.2 0.0 copy-start.6
  23.2 0.6 copy-done.6
  23.9 0.1 fusion.6
  24.0 0.2 reduce_window_sum.11
  24.2 0.2 select_reduce_fusion
  24.3 0.7 copy-done.5
  25.0 0.6 copy-done.7
  25.7 0.3 broadcast_and_fusion
  26.0 15.3 %all-to-all-done = f32[128,2,128]{2,1,0:T(2,128)S(1)} async-done(((f32[128,2,128]{2,1,0:T(2,128)}), f32[128,2,128]{2,1,0:T(2,128)S(1)}, u32[]{:S(2)}, u32[]{:S(2)}) %all-to-all-start) | async-done | bytes 131104 | tf_op jit(solution)/shard_map/all_to_all | solution.py:167
  41.3 0.3 fusion.10
  41.7 0.1 fusion.19
  41.8 0.1 add_divide_fusion.6
  41.9 0.1 fusion.18
  42.0 0.1 add_divide_fusion.5
  42.1 0.1 fusion.17
  42.2 0.1 add_divide_fusion.4
  42.3 0.1 fusion.16
  42.4 0.1 add_divide_fusion.3
  42.5 0.1 fusion.15
  42.6 0.1 add_divide_fusion.2
  42.7 0.1 fusion.14
  42.8 0.1 add_divide_fusion.1
  42.9 0.1 fusion.13
  43.0 0.1 add_divide_fusion
  43.1 0.1 fusion.12
  43.2 0.1 multiply_subtract_fusion
  43.3 0.0 copy-start.4
  43.3 0.8 copy-done.4
  44.1 0.0 copy-start
  44.2 0.0 copy-start.2
  44.2 1.1 %fusion = f32[512,128]{1,0:T(8,128)} fusion(pred[64,8,2,128]{3,2,1,0:T(4,128)(4,1)S(1)} %bitcast.55, f32[128,128]{1,0:T(8,128)S(1)} %bitcast.56, f32[128,128]{1,0:T(8,128)S(1)} %bitcast_multiply_fusion.2), kind=kOutput, calls=%fused_computation.5 | convolution fusion | flops 201359360 | bytes 524288 | tf_op jit(solution)/shard_map/dot_general | solution.py:189
  45.3 0.9 copy-done.3
  46.2 0.5 while.24
  46.7 3.1 %collective-permute-start = (f32[2,16,128]{2,1,0:T(8,128)S(1)}, f32[2,16,128]{2,1,0:T(8,128)S(1)}, u32[]{:S(2)}, u32[]{:S(2)}) collective-permute-start(f32[2,16,128]{2,1,0:T(8,128)S(1)} %pad_maximum_fusion), channel_id=1, source_target_pairs={{0,1},{1,2},{2,3},{4,5},{5,6},{6,7},{8,9},{9,10},{10,11},{12,13},{... | collective-permute-start | bytes 49160 | tf_op jit(solution)/shard_map/ppermute | solution.py:15
  49.8 4.4 %collective-permute-start.1 = (f32[2,16,128]{2,1,0:T(8,128)S(1)}, f32[2,16,128]{2,1,0:T(8,128)S(1)}, u32[]{:S(2)}, u32[]{:S(2)}) collective-permute-start(f32[2,16,128]{2,1,0:T(8,128)S(1)} %pad_maximum_fusion), channel_id=1, source_target_pairs={{0,2},{1,3},{4,6},{5,7},{8,10},{9,11},{12,14},{13,15},{16,18},{17,... | collective-permute-start | bytes 49160 | tf_op jit(solution)/shard_map/ppermute | solution.py:15
  54.2 1.3 %collective-permute-start.2 = (f32[2,16,128]{2,1,0:T(8,128)S(1)}, f32[2,16,128]{2,1,0:T(8,128)S(1)}, u32[]{:S(2)}, u32[]{:S(2)}) collective-permute-start(f32[2,16,128]{2,1,0:T(8,128)S(1)} %pad_maximum_fusion), channel_id=1, source_target_pairs={{0,3},{4,7},{8,11},{12,15},{16,19},{20,23},{24,27},{28,31},{32,35}... | collective-permute-start | bytes 49160 | tf_op jit(solution)/shard_map/ppermute | solution.py:15
  55.5 0.6 broadcast_in_dim_reshape.3
  56.1 5.6 %all-to-all-start.1 = ((f32[128,4,128]{2,1,0:T(4,128)}), f32[128,4,128]{2,1,0:T(4,128)S(1)}, u32[]{:S(2)}, u32[]{:S(2)}) async-start(f32[128,4,128]{2,1,0:T(4,128)} %bitcast.9), calls=%async_computation.1 | async-start | bytes 524288 | tf_op jit(solution)/shard_map/all_to_all | solution.py:195
  61.8 0.0 collective-permute-done
  61.8 0.0 collective-permute-done.2
  61.8 0.8 while.23
  62.6 22.6 %all-to-all-done.1 = f32[128,4,128]{2,1,0:T(4,128)S(1)} async-done(((f32[128,4,128]{2,1,0:T(4,128)}), f32[128,4,128]{2,1,0:T(4,128)S(1)}, u32[]{:S(2)}, u32[]{:S(2)}) %all-to-all-start.1) | async-done | bytes 262176 | tf_op jit(solution)/shard_map/all_to_all | solution.py:195
  85.2 0.7 copy-done.1
  85.9 4.3 %shard_map.96 = f32[2,8,128]{2,1,0:T(8,128)} custom-call(s32[256,128]{1,0:T(8,128)} %bitcast.51, f32[512,128]{1,0:T(8,128)} %bitcast.49), custom_call_target="tpu_custom_call" | custom-call | tf_op jit(solution)/shard_map/pallas_call | solution.py:130
  90.2 0.7 fusion.20
  90.9 0.7 add_subtract_fusion
  (70 shorter events, 0.7 us)
Async XLA Ops:
  2.7 38.7 %all-to-all-start = ((f32[128,2,128]{2,1,0:T(2,128)}), f32[128,2,128]{2,1,0:T(2,128)S(1)}, u32[]{:S(2)}, u32[]{:S(2)}) async-start(f32[128,2,128]{2,1,0:T(2,128)} %bitcast.52), calls=%async_computation | async-start | bytes 262144 | tf_op jit(solution)/shard_map/all_to_all | solution.py:167
  23.2 0.7 copy-start.6
  24.2 0.8 copy-start.5
  25.0 0.7 copy-start.7
  43.3 0.8 copy-start.4
  44.1 1.1 %copy-start = (f32[16,16,128]{2,1,0:T(8,128)S(1)}, f32[16,16,128]{2,1,0:T(8,128)}, u32[]{:S(2)}) copy-start(f32[16,16,128]{2,1,0:T(8,128)} %table_ref.1) | copy-start | bytes 393220
  44.2 1.1 %copy-start.2 = (f32[16,16,128]{2,1,0:T(8,128)S(1)}, f32[16,16,128]{2,1,0:T(8,128)}, u32[]{:S(2)}) copy-start(f32[16,16,128]{2,1,0:T(8,128)} %param.14) | copy-start | bytes 393220
  45.3 0.9 copy-start.3
  46.7 15.1 %collective-permute-start = (f32[2,16,128]{2,1,0:T(8,128)S(1)}, f32[2,16,128]{2,1,0:T(8,128)S(1)}, u32[]{:S(2)}, u32[]{:S(2)}) collective-permute-start(f32[2,16,128]{2,1,0:T(8,128)S(1)} %pad_maximum_fusion), channel_id=1, source_target_pairs={{0,1},{1,2},{2,3},{4,5},{5,6},{6,7},{8,9},{9,10},{10,11},{12,13},{... | collective-permute-start | bytes 49160 | tf_op jit(solution)/shard_map/ppermute | solution.py:15
  49.8 11.9 %collective-permute-start.1 = (f32[2,16,128]{2,1,0:T(8,128)S(1)}, f32[2,16,128]{2,1,0:T(8,128)S(1)}, u32[]{:S(2)}, u32[]{:S(2)}) collective-permute-start(f32[2,16,128]{2,1,0:T(8,128)S(1)} %pad_maximum_fusion), channel_id=1, source_target_pairs={{0,2},{1,3},{4,6},{5,7},{8,10},{9,11},{12,14},{13,15},{16,18},{17,... | collective-permute-start | bytes 49160 | tf_op jit(solution)/shard_map/ppermute | solution.py:15
  54.2 7.6 %collective-permute-start.2 = (f32[2,16,128]{2,1,0:T(8,128)S(1)}, f32[2,16,128]{2,1,0:T(8,128)S(1)}, u32[]{:S(2)}, u32[]{:S(2)}) collective-permute-start(f32[2,16,128]{2,1,0:T(8,128)S(1)} %pad_maximum_fusion), channel_id=1, source_target_pairs={{0,3},{4,7},{8,11},{12,15},{16,19},{20,23},{24,27},{28,31},{32,35}... | collective-permute-start | bytes 49160 | tf_op jit(solution)/shard_map/ppermute | solution.py:15
  56.1 29.0 %all-to-all-start.1 = ((f32[128,4,128]{2,1,0:T(4,128)}), f32[128,4,128]{2,1,0:T(4,128)S(1)}, u32[]{:S(2)}, u32[]{:S(2)}) async-start(f32[128,4,128]{2,1,0:T(4,128)} %bitcast.9), calls=%async_computation.1 | async-start | bytes 524288 | tf_op jit(solution)/shard_map/all_to_all | solution.py:195
  85.2 0.7 copy-start.1

commit v8 on v7

--- a/solution.py
+++ b/solution.py
@@ -169,6 +169,18 @@
     rows = slot_rows(owners, groups, capacity)
     slots = groups * capacity
     filled = rows[None, :] == jnp.arange(slots, dtype=jnp.int32)[:, None]
+    segments = rows.shape[0]
+    weights = node_weight[0]
+    halves = lax.broadcasted_iota(jnp.int32, (slots, 2, segments), 1)
+    sat_rows = (filled[:, None, :] & (halves == 0)).reshape(2 * slots, segments)
+    weight_rows = (filled[:, None, :] & (halves == 1)).reshape(2 * slots, segments)
+    weight_part = jnp.dot(
+        weight_rows.astype(jnp.float32),
+        weights,
+        precision=lax.Precision.HIGHEST,
+        preferred_element_type=jnp.float32,
+    )
+    weight_part, arrived = lax.optimization_barrier((weight_part, arrived))
     node_in = jnp.dot(
         filled.T.astype(jnp.float32),
         arrived,
@@ -182,13 +194,9 @@
         stream_dir[0],
     )
     updated = updated.reshape(seg_dev, seg_len)
-    weights = node_weight[0]
-    joined = jnp.concatenate([weights * updated, weights], axis=0)
-    halves = jnp.arange(2, dtype=jnp.int32)
-    spread = (filled[:, None, None, :] & (halves[None, :, None, None] == halves[None, None, :, None]))
-    package = jnp.dot(
-        spread.reshape(2 * slots, 2 * seg_dev).astype(jnp.float32),
-        joined,
+    package = weight_part + jnp.dot(
+        sat_rows.astype(jnp.float32),
+        weights * updated,
         precision=lax.Precision.HIGHEST,
         preferred_element_type=jnp.float32,
     )

time: 92 us -> 90.4 us (0.983)
  local copies, waits for them, and re-layouts: 6.38 us -> 5.44 us
    unnamed x16 -> x18, local copies, waits for them, and re-layouts: 4.36 us -> 3.73 us
where the time goes in v8:
time: 90.4 us; the launch traced here: 90 us
  waiting for transfers between devices  37.1 us (41%)
  starting transfers between devices  34.9 us (39%)
  Pallas kernels  6.29 us (7%)
  local copies, waits for them, and re-layouts  5.44 us (6%)
  other arithmetic  2.97 us (3%)
  matrix products  1.5 us (2%)
  between operations  0.95 us (1%)
    all_to_all x1, waiting for transfers between devices, on_device(): lax.all_to_all(package, ('gx', 'gy'), split_axis=0, concat_axis=0, tiled=...  22.6 us
    all_to_all x1, starting transfers between devices, on_device(): lax.all_to_all(offered, ('gx', 'gy'), split_axis=0, concat_axis=0, tiled=...  20.6 us
    all_to_all x1, waiting for transfers between devices, on_device(): lax.all_to_all(offered, ('gx', 'gy'), split_axis=0, concat_axis=0, tiled=...  14.5 us
    ppermute x3, starting transfers between devices, from_behind(): return lax.ppermute(block, axis, route)  8.76 us
    all_to_all x1, starting transfers between devices, on_device(): lax.all_to_all(package, ('gx', 'gy'), split_axis=0, concat_axis=0, tiled=...  5.62 us
    pallas_call x1, Pallas kernels, scatter_cells(): pl.pallas_call(scatter_kernel, out_shape=jax.ShapeDtypeStruct((2, map_row...  4.26 us
    unnamed x18, local copies, waits for them, and re-layouts  3.73 us
    pallas_call x1, Pallas kernels, gather_cells(): pl.pallas_call(gather_kernel, out_shape=jax.ShapeDtypeStruct(local_map.sh...  2.03 us
  transfers between devices with their start and end apart: 5, of which 2 were waited for; matrix products, arithmetic and copies ran while one was open for 2% of the time, Pallas kernels for 0%

profile of v8, /device:TPU:1, one launch (start us, length us, event | category | flops | bytes accessed | tf_op | source)
XLA Modules:
  0.0 90.0 jit_solution(5378756394881126322)
XLA Ops:
  0.6 2.0 %shard_map.95 = f32[256,128]{1,0:T(8,128)} custom-call(f32[16,16,128]{2,1,0:T(8,128)} %table_ref.1, s32[256,128]{1,0:T(8,128)} %bitcast.51), custom_call_target="tpu_custom_call" | custom-call | tf_op jit(solution)/shard_map/pallas_call | solution.py:69
  2.7 20.6 %all-to-all-start = ((f32[128,2,128]{2,1,0:T(2,128)}), f32[128,2,128]{2,1,0:T(2,128)S(1)}, u32[]{:S(2)}, u32[]{:S(2)}) async-start(f32[128,2,128]{2,1,0:T(2,128)} %bitcast.53), calls=%async_computation | async-start | bytes 262144 | tf_op jit(solution)/shard_map/all_to_all | solution.py:167
  23.2 0.0 copy-start.7
  23.2 0.6 copy-done.7
  23.9 0.1 fusion.4
  24.0 0.2 reduce_window_sum.11
  24.2 0.2 select_reduce_fusion
  24.4 0.3 broadcast_and_fusion
  24.7 0.2 and.36
  24.9 0.0 copy-start.6
  24.9 0.2 and.38
  25.1 0.7 copy-done.6
  25.7 0.6 copy-done.8
  26.4 0.2 copy-done.5
  26.6 0.3 fusion.1
  26.8 14.5 %all-to-all-done = f32[128,2,128]{2,1,0:T(2,128)S(1)} async-done(((f32[128,2,128]{2,1,0:T(2,128)}), f32[128,2,128]{2,1,0:T(2,128)S(1)}, u32[]{:S(2)}, u32[]{:S(2)}) %all-to-all-start) | async-done | bytes 131104 | tf_op jit(solution)/shard_map/all_to_all | solution.py:167
  41.3 0.3 fusion.8
  41.7 0.1 fusion.16
  41.8 0.1 add_divide_fusion.6
  41.9 0.1 fusion.15
  42.0 0.1 add_divide_fusion.5
  42.1 0.1 fusion.14
  42.2 0.1 add_divide_fusion.4
  42.3 0.1 fusion.13
  42.4 0.1 add_divide_fusion.3
  42.5 0.1 fusion.12
  42.6 0.1 add_divide_fusion.2
  42.7 0.1 fusion.11
  42.8 0.1 add_divide_fusion.1
  42.9 0.1 fusion.10
  43.0 0.1 add_divide_fusion
  43.1 0.1 fusion.9
  43.2 0.1 multiply_subtract_fusion
  43.3 0.0 copy-start.4
  43.3 0.0 copy-start
  43.3 1.0 %convolution_add_fusion = f32[512,128]{1,0:T(8,128)} fusion(f32[512,128]{1,0:T(8,128)S(1)} %fusion.1, pred[512,128]{1,0:T(32,128)(4,1)S(1)} %and.38, f32[1,128,128]{2,1,0:T(8,128)S(1)} %copy-done.5, f32[1,128,128]{2,1,0:T(8,128)S(1)} %reshape.123), kind=kOutput, calls=%fused_computation.5 | convolution fusion | flops 100745216 | bytes 720896 | tf_op jit(solution)/shard_map/dot_general | solution.py:197
  44.3 0.9 copy-done.3
  45.2 0.5 while.24
  45.8 3.1 %collective-permute-start = (f32[2,16,128]{2,1,0:T(8,128)S(1)}, f32[2,16,128]{2,1,0:T(8,128)S(1)}, u32[]{:S(2)}, u32[]{:S(2)}) collective-permute-start(f32[2,16,128]{2,1,0:T(8,128)S(1)} %pad_maximum_fusion), channel_id=1, source_target_pairs={{0,1},{1,2},{2,3},{4,5},{5,6},{6,7},{8,9},{9,10},{10,11},{12,13},{... | collective-permute-start | bytes 49160 | tf_op jit(solution)/shard_map/ppermute | solution.py:15
  48.9 4.4 %collective-permute-start.1 = (f32[2,16,128]{2,1,0:T(8,128)S(1)}, f32[2,16,128]{2,1,0:T(8,128)S(1)}, u32[]{:S(2)}, u32[]{:S(2)}) collective-permute-start(f32[2,16,128]{2,1,0:T(8,128)S(1)} %pad_maximum_fusion), channel_id=1, source_target_pairs={{0,2},{1,3},{4,6},{5,7},{8,10},{9,11},{12,14},{13,15},{16,18},{17,... | collective-permute-start | bytes 49160 | tf_op jit(solution)/shard_map/ppermute | solution.py:15
  53.2 1.3 %collective-permute-start.2 = (f32[2,16,128]{2,1,0:T(8,128)S(1)}, f32[2,16,128]{2,1,0:T(8,128)S(1)}, u32[]{:S(2)}, u32[]{:S(2)}) collective-permute-start(f32[2,16,128]{2,1,0:T(8,128)S(1)} %pad_maximum_fusion), channel_id=1, source_target_pairs={{0,3},{4,7},{8,11},{12,15},{16,19},{20,23},{24,27},{28,31},{32,35}... | collective-permute-start | bytes 49160 | tf_op jit(solution)/shard_map/ppermute | solution.py:15
  54.5 5.6 %all-to-all-start.1 = ((f32[128,4,128]{2,1,0:T(4,128)}), f32[128,4,128]{2,1,0:T(4,128)S(1)}, u32[]{:S(2)}, u32[]{:S(2)}) async-start(f32[128,4,128]{2,1,0:T(4,128)} %bitcast.10), calls=%async_computation.1 | async-start | bytes 524288 | tf_op jit(solution)/shard_map/all_to_all | solution.py:203
  60.2 0.8 while.23
  61.0 22.6 %all-to-all-done.1 = f32[128,4,128]{2,1,0:T(4,128)S(1)} async-done(((f32[128,4,128]{2,1,0:T(4,128)}), f32[128,4,128]{2,1,0:T(4,128)S(1)}, u32[]{:S(2)}, u32[]{:S(2)}) %all-to-all-start.1) | async-done | bytes 262176 | tf_op jit(solution)/shard_map/all_to_all | solution.py:203
  83.6 0.7 copy-done.1
  84.3 4.3 %shard_map.96 = f32[2,8,128]{2,1,0:T(8,128)} custom-call(s32[256,128]{1,0:T(8,128)} %bitcast.52, f32[512,128]{1,0:T(8,128)} %bitcast.50), custom_call_target="tpu_custom_call" | custom-call | tf_op jit(solution)/shard_map/pallas_call | solution.py:130
  88.6 0.7 fusion.17
  89.3 0.7 add_subtract_fusion
  (73 shorter events, 0.7 us)
Async XLA Ops:
  2.7 38.7 %all-to-all-start = ((f32[128,2,128]{2,1,0:T(2,128)}), f32[128,2,128]{2,1,0:T(2,128)S(1)}, u32[]{:S(2)}, u32[]{:S(2)}) async-start(f32[128,2,128]{2,1,0:T(2,128)} %bitcast.53), calls=%async_computation | async-start | bytes 262144 | tf_op jit(solution)/shard_map/all_to_all | solution.py:167
  23.2 0.7 copy-start.7
  24.9 0.8 copy-start.6
  25.7 0.7 copy-start.8
  25.7 0.9 copy-start.5
  43.3 1.0 %copy-start.4 = (f32[1,128,128]{2,1,0:T(8,128)}, f32[1,128,128]{2,1,0:T(8,128)S(1)}, u32[]{:S(2)}) copy-start(f32[1,128,128]{2,1,0:T(8,128)S(1)} %reshape.123) | copy-start | bytes 196612
  43.3 1.0 %copy-start = (f32[16,16,128]{2,1,0:T(8,128)S(1)}, f32[16,16,128]{2,1,0:T(8,128)}, u32[]{:S(2)}) copy-start(f32[16,16,128]{2,1,0:T(8,128)} %table_ref.1) | copy-start | bytes 393220
  43.3 1.0 %copy-start.2 = (f32[16,16,128]{2,1,0:T(8,128)S(1)}, f32[16,16,128]{2,1,0:T(8,128)}, u32[]{:S(2)}) copy-start(f32[16,16,128]{2,1,0:T(8,128)} %param.14) | copy-start | bytes 393220
  44.3 0.9 %copy-start.3 = (f32[16,16,128]{2,1,0:T(8,128)S(1)}, f32[16,16,128]{2,1,0:T(8,128)}, u32[]{:S(2)}) copy-start(f32[16,16,128]{2,1,0:T(8,128)} %param.13) | copy-start | bytes 393220
  45.8 14.4 %collective-permute-start = (f32[2,16,128]{2,1,0:T(8,128)S(1)}, f32[2,16,128]{2,1,0:T(8,128)S(1)}, u32[]{:S(2)}, u32[]{:S(2)}) collective-permute-start(f32[2,16,128]{2,1,0:T(8,128)S(1)} %pad_maximum_fusion), channel_id=1, source_target_pairs={{0,1},{1,2},{2,3},{4,5},{5,6},{6,7},{8,9},{9,10},{10,11},{12,13},{... | collective-permute-start | bytes 49160 | tf_op jit(solution)/shard_map/ppermute | solution.py:15
  48.9 11.3 %collective-permute-start.1 = (f32[2,16,128]{2,1,0:T(8,128)S(1)}, f32[2,16,128]{2,1,0:T(8,128)S(1)}, u32[]{:S(2)}, u32[]{:S(2)}) collective-permute-start(f32[2,16,128]{2,1,0:T(8,128)S(1)} %pad_maximum_fusion), channel_id=1, source_target_pairs={{0,2},{1,3},{4,6},{5,7},{8,10},{9,11},{12,14},{13,15},{16,18},{17,... | collective-permute-start | bytes 49160 | tf_op jit(solution)/shard_map/ppermute | solution.py:15
  53.2 7.0 %collective-permute-start.2 = (f32[2,16,128]{2,1,0:T(8,128)S(1)}, f32[2,16,128]{2,1,0:T(8,128)S(1)}, u32[]{:S(2)}, u32[]{:S(2)}) collective-permute-start(f32[2,16,128]{2,1,0:T(8,128)S(1)} %pad_maximum_fusion), channel_id=1, source_target_pairs={{0,3},{4,7},{8,11},{12,15},{16,19},{20,23},{24,27},{28,31},{32,35}... | collective-permute-start | bytes 49160 | tf_op jit(solution)/shard_map/ppermute | solution.py:15
  54.5 29.1 %all-to-all-start.1 = ((f32[128,4,128]{2,1,0:T(4,128)}), f32[128,4,128]{2,1,0:T(4,128)S(1)}, u32[]{:S(2)}, u32[]{:S(2)}) async-start(f32[128,4,128]{2,1,0:T(4,128)} %bitcast.10), calls=%async_computation.1 | async-start | bytes 524288 | tf_op jit(solution)/shard_map/all_to_all | solution.py:203
  83.6 0.7 copy-start.1

commit v9 on v8

--- a/solution.py
+++ b/solution.py
@@ -19,19 +19,6 @@
     return values * values / (values * values + (1.0 - values) * (1.0 - values))
 
 
-def transport(node_sat, increments, reversed_flag):
-    flipped = reversed_flag[..., None] == 1
-    state = node_sat
-    inlet = jnp.ones(state.shape[:-1] + (1,), jnp.float32)
-    for _ in range(BL_STEPS):
-        flows = frac_flow(state)
-        from_left = jnp.concatenate([inlet, flows[..., :-1]], axis=-1)
-        from_right = jnp.concatenate([flows[..., 1:], inlet], axis=-1)
-        upstream = jnp.where(flipped, from_right, from_left)
-        state = state - increments * (flows - upstream)
-    return state
-
-
 def slot_rows(owners, groups, capacity):
     onehot = (owners[:, None] == jnp.arange(groups, dtype=jnp.int32)[None, :]).astype(jnp.int32)
     before = jnp.cumsum(onehot, axis=0) - onehot
@@ -42,6 +29,30 @@
     keep, drop = layer
     inflow = keep * carried
     return (inflow + drop, inflow)
+
+
+def transport_kernel(state_ref, ratio_ref, flag_ref, out_ref):
+    state = state_ref[...]
+    ratio = ratio_ref[...]
+    flipped = flag_ref[...] == 1
+    width = state.shape[1]
+    lane = lax.broadcasted_iota(jnp.int32, state.shape, 1)
+    for _ in range(BL_STEPS):
+        flows = frac_flow(state)
+        from_left = jnp.where(lane == 0, 1.0, pltpu.roll(flows, 1, axis=1))
+        from_right = jnp.where(lane == width - 1, 1.0, pltpu.roll(flows, width - 1, axis=1))
+        upstream = jnp.where(flipped, from_right, from_left)
+        state = state - ratio * (flows - upstream)
+    out_ref[...] = state
+
+
+def transport_lines(node_sat, increments, reversed_flag):
+    return pl.pallas_call(
+        transport_kernel,
+        out_shape=jax.ShapeDtypeStruct(node_sat.shape, jnp.float32),
+        in_specs=[pl.BlockSpec(memory_space=pltpu.VMEM)] * 3,
+        out_specs=pl.BlockSpec(memory_space=pltpu.VMEM),
+    )(node_sat, increments, reversed_flag[:, None])
 
 
 def gather_kernel(table_ref, ids_ref, out_ref):
@@ -188,7 +199,7 @@
         preferred_element_type=jnp.float32,
     )
     seg_dev = node_in.shape[0]
-    updated = transport(
+    updated = transport_lines(
         node_in.reshape(seg_dev // 2, 2 * seg_len),
         flight[0].reshape(seg_dev // 2, 2 * seg_len),
         stream_dir[0],

time: 90.4 us -> 92.8 us (1.027)
  local copies, waits for them, and re-layouts: 5.44 us -> 8.11 us
  Pallas kernels: 6.29 us -> 8.72 us
  waiting for transfers between devices: 37.1 us -> 35.2 us
  other arithmetic: 2.97 us -> 2.03 us
    pallas_call x0 -> x1, Pallas kernels: none -> 2.42 us  [transport_lines(): pl.pallas_call(transport_kernel, out_shape=jax.ShapeDtypeStruct(node_sat....]
    all_to_all x1, waiting for transfers between devices: 14.5 us -> 12.7 us  [on_device(): lax.all_to_all(offered, ('gx', 'gy'), split_axis=0, concat_axis=0, tiled=...]
  transfers between devices with their start and end apart: 5 -> 5, of which waited for: 2 -> 2; matrix products, arithmetic and copies ran while one was open for 2% -> 3% of each run, Pallas kernels for 0% -> 0%
where the time goes in v9:
time: 92.8 us; the launch traced here: 92.2 us
  waiting for transfers between devices  35.2 us (38%)
  starting transfers between devices  34.9 us (38%)
  Pallas kernels  8.72 us (9%)
  local copies, waits for them, and re-layouts  8.11 us (9%)
  other arithmetic  2.03 us (2%)
  matrix products  1.51 us (2%)
    all_to_all x1, waiting for transfers between devices, on_device(): lax.all_to_all(package, ('gx', 'gy'), split_axis=0, concat_axis=0, tiled=...  22.6 us
    all_to_all x1, starting transfers between devices, on_device(): lax.all_to_all(offered, ('gx', 'gy'), split_axis=0, concat_axis=0, tiled=...  20.6 us
    all_to_all x1, waiting for transfers between devices, on_device(): lax.all_to_all(offered, ('gx', 'gy'), split_axis=0, concat_axis=0, tiled=...  12.7 us
    ppermute x3, starting transfers between devices, from_behind(): return lax.ppermute(block, axis, route)  8.76 us
    all_to_all x1, starting transfers between devices, on_device(): lax.all_to_all(package, ('gx', 'gy'), split_axis=0, concat_axis=0, tiled=...  5.62 us
    pallas_call x1, Pallas kernels, scatter_cells(): pl.pallas_call(scatter_kernel, out_shape=jax.ShapeDtypeStruct((2, map_row...  4.27 us
    unnamed x18, local copies, waits for them, and re-layouts  4.24 us
    pallas_call x1, Pallas kernels, transport_lines(): pl.pallas_call(transport_kernel, out_shape=jax.ShapeDtypeStruct(node_sat....  2.42 us
  transfers between devices with their start and end apart: 5, of which 2 were waited for; matrix products, arithmetic and copies ran while one was open for 3% of the time, Pallas kernels for 0%

profile of v9, /device:TPU:1, one launch (start us, length us, event | category | flops | bytes accessed | tf_op | source)
XLA Modules:
  0.0 92.2 jit_solution(2975939210780250967)
XLA Ops:
  0.6 2.0 %shard_map.95 = f32[256,128]{1,0:T(8,128)} custom-call(f32[16,16,128]{2,1,0:T(8,128)} %table_ref.1, s32[256,128]{1,0:T(8,128)} %bitcast.50), custom_call_target="tpu_custom_call" | custom-call | tf_op jit(solution)/shard_map/pallas_call | solution.py:80
  2.7 20.6 %all-to-all-start = ((f32[128,2,128]{2,1,0:T(2,128)}), f32[128,2,128]{2,1,0:T(2,128)S(1)}, u32[]{:S(2)}, u32[]{:S(2)}) async-start(f32[128,2,128]{2,1,0:T(2,128)} %bitcast.52), calls=%async_computation | async-start | bytes 262144 | tf_op jit(solution)/shard_map/all_to_all | solution.py:178
  23.2 0.0 copy-start.7
  23.2 0.6 copy-done.7
  23.9 0.1 fusion.4
  24.0 0.2 reduce_window_sum.11
  24.1 0.2 select_reduce_fusion
  24.4 0.3 broadcast_and_fusion
  24.7 0.0 copy-start.6
  24.7 0.2 and.36
  24.9 0.7 copy-done.6
  25.6 0.7 reshape_squeeze.3.ratio_ref
  26.2 0.0 copy-start.8
  26.2 0.7 copy-done.8
  26.9 0.7 copy.11.flag_ref
  27.6 0.0 copy-start.5
  27.6 0.2 and.38
  27.7 0.7 copy-done.5
  28.4 0.3 fusion.1
  28.7 12.7 %all-to-all-done = f32[128,2,128]{2,1,0:T(2,128)S(1)} async-done(((f32[128,2,128]{2,1,0:T(2,128)}), f32[128,2,128]{2,1,0:T(2,128)S(1)}, u32[]{:S(2)}, u32[]{:S(2)}) %all-to-all-start) | async-done | bytes 131104 | tf_op jit(solution)/shard_map/all_to_all | solution.py:178
  41.3 0.3 fusion.8
  41.6 0.6 reshape.113.state_ref
  42.3 2.4 %shard_map.96 = f32[64,256]{1,0:T(8,128)} custom-call(f32[64,256]{1,0:T(8,128)} %reshape.113.state_ref, f32[64,256]{1,0:T(8,128)} %reshape_squeeze.3.ratio_ref, s32[64,1]{1,0:T(8,128)} %copy.11.flag_ref), custom_call_target="tpu_custom_call" | custom-call | tf_op jit(solution)/shard_map/pallas_call | solution.py:50
  44.7 0.8 reshape.114
  45.6 0.0 copy-start.4
  45.6 0.0 copy-start
  45.6 0.0 copy-start.2
  45.6 1.0 %convolution_add_fusion = f32[512,128]{1,0:T(8,128)} fusion(f32[512,128]{1,0:T(8,128)S(1)} %fusion.1, pred[512,128]{1,0:T(32,128)(4,1)S(1)} %and.38, f32[1,128,128]{2,1,0:T(8,128)S(1)} %copy-done.5, f32[1,128,128]{2,1,0:T(8,128)S(1)} %reshape.114), kind=kOutput, calls=%fused_computation.5 | convolution fusion | flops 100745216 | bytes 720896 | tf_op jit(solution)/shard_map/dot_general | solution.py:208
  46.5 0.0 copy-done.4
  46.5 0.0 copy-done
  46.5 0.0 copy-done.2
  46.5 0.0 copy-start.3
  46.6 0.9 copy-done.3
  47.5 0.5 while.24
  48.0 3.1 %collective-permute-start = (f32[2,16,128]{2,1,0:T(8,128)S(1)}, f32[2,16,128]{2,1,0:T(8,128)S(1)}, u32[]{:S(2)}, u32[]{:S(2)}) collective-permute-start(f32[2,16,128]{2,1,0:T(8,128)S(1)} %pad_maximum_fusion), channel_id=1, source_target_pairs={{0,1},{1,2},{2,3},{4,5},{5,6},{6,7},{8,9},{9,10},{10,11},{12,13},{... | collective-permute-start | bytes 49160 | tf_op jit(solution)/shard_map/ppermute | solution.py:15
  51.1 4.4 %collective-permute-start.1 = (f32[2,16,128]{2,1,0:T(8,128)S(1)}, f32[2,16,128]{2,1,0:T(8,128)S(1)}, u32[]{:S(2)}, u32[]{:S(2)}) collective-permute-start(f32[2,16,128]{2,1,0:T(8,128)S(1)} %pad_maximum_fusion), channel_id=1, source_target_pairs={{0,2},{1,3},{4,6},{5,7},{8,10},{9,11},{12,14},{13,15},{16,18},{17,... | collective-permute-start | bytes 49160 | tf_op jit(solution)/shard_map/ppermute | solution.py:15
  55.5 1.3 %collective-permute-start.2 = (f32[2,16,128]{2,1,0:T(8,128)S(1)}, f32[2,16,128]{2,1,0:T(8,128)S(1)}, u32[]{:S(2)}, u32[]{:S(2)}) collective-permute-start(f32[2,16,128]{2,1,0:T(8,128)S(1)} %pad_maximum_fusion), channel_id=1, source_target_pairs={{0,3},{4,7},{8,11},{12,15},{16,19},{20,23},{24,27},{28,31},{32,35}... | collective-permute-start | bytes 49160 | tf_op jit(solution)/shard_map/ppermute | solution.py:15
  56.8 5.6 %all-to-all-start.1 = ((f32[128,4,128]{2,1,0:T(4,128)}), f32[128,4,128]{2,1,0:T(4,128)S(1)}, u32[]{:S(2)}, u32[]{:S(2)}) async-start(f32[128,4,128]{2,1,0:T(4,128)} %bitcast.10), calls=%async_computation.1 | async-start | bytes 524288 | tf_op jit(solution)/shard_map/all_to_all | solution.py:214
  62.4 0.0 collective-permute-done
  62.4 0.0 collective-permute-done.1
  62.4 0.0 collective-permute-done.2
  62.5 0.8 while.23
  63.3 22.6 %all-to-all-done.1 = f32[128,4,128]{2,1,0:T(4,128)S(1)} async-done(((f32[128,4,128]{2,1,0:T(4,128)}), f32[128,4,128]{2,1,0:T(4,128)S(1)}, u32[]{:S(2)}, u32[]{:S(2)}) %all-to-all-start.1) | async-done | bytes 262176 | tf_op jit(solution)/shard_map/all_to_all | solution.py:214
  85.8 0.0 copy-start.1
  85.8 0.7 copy-done.1
  86.5 4.3 %shard_map.97 = f32[2,8,128]{2,1,0:T(8,128)} custom-call(s32[256,128]{1,0:T(8,128)} %bitcast.51, f32[512,128]{1,0:T(8,128)} %bitcast.49), custom_call_target="tpu_custom_call" | custom-call | tf_op jit(solution)/shard_map/pallas_call | solution.py:141
  90.8 0.7 fusion.9
  91.5 0.7 add_subtract_fusion
  (57 shorter events, 0.6 us)
Async XLA Ops:
  2.7 38.7 %all-to-all-start = ((f32[128,2,128]{2,1,0:T(2,128)}), f32[128,2,128]{2,1,0:T(2,128)S(1)}, u32[]{:S(2)}, u32[]{:S(2)}) async-start(f32[128,2,128]{2,1,0:T(2,128)} %bitcast.52), calls=%async_computation | async-start | bytes 262144 | tf_op jit(solution)/shard_map/all_to_all | solution.py:178
  23.2 0.7 copy-start.7
  24.7 0.8 copy-start.6
  26.2 0.7 copy-start.8
  27.6 0.8 copy-start.5
  45.6 1.0 %copy-start.4 = (f32[1,128,128]{2,1,0:T(8,128)}, f32[1,128,128]{2,1,0:T(8,128)S(1)}, u32[]{:S(2)}) copy-start(f32[1,128,128]{2,1,0:T(8,128)S(1)} %reshape.114) | copy-start | bytes 196612
  45.6 1.0 %copy-start = (f32[16,16,128]{2,1,0:T(8,128)S(1)}, f32[16,16,128]{2,1,0:T(8,128)}, u32[]{:S(2)}) copy-start(f32[16,16,128]{2,1,0:T(8,128)} %table_ref.1) | copy-start | bytes 393220
  45.6 1.0 %copy-start.2 = (f32[16,16,128]{2,1,0:T(8,128)S(1)}, f32[16,16,128]{2,1,0:T(8,128)}, u32[]{:S(2)}) copy-start(f32[16,16,128]{2,1,0:T(8,128)} %param.14) | copy-start | bytes 393220
  46.5 0.9 copy-start.3
  48.0 14.4 %collective-permute-start = (f32[2,16,128]{2,1,0:T(8,128)S(1)}, f32[2,16,128]{2,1,0:T(8,128)S(1)}, u32[]{:S(2)}, u32[]{:S(2)}) collective-permute-start(f32[2,16,128]{2,1,0:T(8,128)S(1)} %pad_maximum_fusion), channel_id=1, source_target_pairs={{0,1},{1,2},{2,3},{4,5},{5,6},{6,7},{8,9},{9,10},{10,11},{12,13},{... | collective-permute-start | bytes 49160 | tf_op jit(solution)/shard_map/ppermute | solution.py:15
  51.1 11.3 %collective-permute-start.1 = (f32[2,16,128]{2,1,0:T(8,128)S(1)}, f32[2,16,128]{2,1,0:T(8,128)S(1)}, u32[]{:S(2)}, u32[]{:S(2)}) collective-permute-start(f32[2,16,128]{2,1,0:T(8,128)S(1)} %pad_maximum_fusion), channel_id=1, source_target_pairs={{0,2},{1,3},{4,6},{5,7},{8,10},{9,11},{12,14},{13,15},{16,18},{17,... | collective-permute-start | bytes 49160 | tf_op jit(solution)/shard_map/ppermute | solution.py:15
  55.5 7.0 %collective-permute-start.2 = (f32[2,16,128]{2,1,0:T(8,128)S(1)}, f32[2,16,128]{2,1,0:T(8,128)S(1)}, u32[]{:S(2)}, u32[]{:S(2)}) collective-permute-start(f32[2,16,128]{2,1,0:T(8,128)S(1)} %pad_maximum_fusion), channel_id=1, source_target_pairs={{0,3},{4,7},{8,11},{12,15},{16,19},{20,23},{24,27},{28,31},{32,35}... | collective-permute-start | bytes 49160 | tf_op jit(solution)/shard_map/ppermute | solution.py:15
  56.8 29.1 %all-to-all-start.1 = ((f32[128,4,128]{2,1,0:T(4,128)}), f32[128,4,128]{2,1,0:T(4,128)S(1)}, u32[]{:S(2)}, u32[]{:S(2)}) async-start(f32[128,4,128]{2,1,0:T(4,128)} %bitcast.10), calls=%async_computation.1 | async-start | bytes 524288 | tf_op jit(solution)/shard_map/all_to_all | solution.py:214
  85.8 0.7 copy-start.1

commit v10 on v8

--- a/solution.py
+++ b/solution.py
@@ -1,3 +1,5 @@
+import functools
+
 import jax
 import jax.numpy as jnp
 from jax import lax
@@ -78,8 +80,7 @@
     )(saturation, local_map)
 
 
-def scatter_kernel(ids_ref, both_ref, out_ref):
-    map_rows = out_ref.shape[1]
+def scatter_kernel(map_rows, ids_ref, both_ref, sat_ref, inflow_ref, burden_ref, out_ref):
     tiles = ids_ref.shape[0] // 8
     lanes = lax.broadcasted_iota(jnp.int32, (128, 128), 0)
     levels = lax.broadcasted_iota(jnp.int32, (map_rows, 128), 0)
@@ -122,17 +123,18 @@
     )
     span = 2 * map_rows
     summed = (totals[:span] + totals[span : 2 * span]) + totals[2 * span :]
-    out_ref[0] = summed[:map_rows]
-    out_ref[1] = summed[map_rows:]
-
-
-def scatter_cells(local_map, both, map_rows):
+    out_ref[...] = (sat_ref[...] + inflow_ref[...]) - burden_ref[...]
+    mixed = (sat_ref[0, :map_rows, :] + summed[:map_rows]) / (1.0 + summed[map_rows:])
+    out_ref[0, :map_rows, :] = (mixed + inflow_ref[0, :map_rows, :]) - burden_ref[0, :map_rows, :]
+
+
+def scatter_cells(local_map, both, saturation, inflow, burden, map_rows):
     return pl.pallas_call(
-        scatter_kernel,
-        out_shape=jax.ShapeDtypeStruct((2, map_rows, 128), jnp.float32),
-        in_specs=[pl.BlockSpec(memory_space=pltpu.VMEM)] * 2,
+        functools.partial(scatter_kernel, map_rows),
+        out_shape=jax.ShapeDtypeStruct(saturation.shape, jnp.float32),
+        in_specs=[pl.BlockSpec(memory_space=pltpu.VMEM)] * 5,
         out_specs=pl.BlockSpec(memory_space=pltpu.VMEM),
-    )(local_map, both)
+    )(local_map, both, saturation, inflow, burden)
 
 
 def segregation(saturation, retention, gravity):
@@ -152,7 +154,6 @@
 
 
 def on_device(saturation, retention, gravity, cell_map, owner_id, stream_dir, node_weight, flight):
-    layers, rows_x, rows_y = saturation.shape
     size_x = lax.axis_size("gx")
     size_y = lax.axis_size("gy")
     groups = size_x * size_y
@@ -203,13 +204,7 @@
     returned = lax.all_to_all(package, ("gx", "gy"), split_axis=0, concat_axis=0, tiled=True)
     package, retention, gravity = lax.optimization_barrier((package, retention, gravity))
     inflow, burden = segregation(saturation, retention, gravity)
-    sums = scatter_cells(local_map, returned, map_rows)
-    head_rows = (map_rows * 128) // rows_y
-    cover = ((0, layers - 1), (0, rows_x - head_rows), (0, 0))
-    numerator = jnp.pad(sums[0].reshape(1, head_rows, rows_y), cover)
-    denominator = jnp.pad(sums[1].reshape(1, head_rows, rows_y), cover)
-    mixed = (saturation + numerator) / (1.0 + denominator)
-    final_sat = mixed + inflow - burden
+    final_sat = scatter_cells(local_map, returned, saturation, inflow, burden, map_rows)
     return (final_sat, updated[None])
 
 

time: 90.4 us -> 89.5 us (0.990)
  no operation moved by 1% of the time
where the time goes in v10:
time: 89.5 us; the launch traced here: 89 us
  waiting for transfers between devices  37.1 us (41%)
  starting transfers between devices  34.9 us (39%)
  Pallas kernels  6.77 us (8%)
  local copies, waits for them, and re-layouts  4.74 us (5%)
  other arithmetic  2.29 us (3%)
  matrix products  1.51 us (2%)
  between operations  0.95 us (1%)
    all_to_all x1, waiting for transfers between devices, on_device(): lax.all_to_all(package, ('gx', 'gy'), split_axis=0, concat_axis=0, tiled=...  22.6 us
    all_to_all x1, starting transfers between devices, on_device(): lax.all_to_all(offered, ('gx', 'gy'), split_axis=0, concat_axis=0, tiled=...  20.6 us
    all_to_all x1, waiting for transfers between devices, on_device(): lax.all_to_all(offered, ('gx', 'gy'), split_axis=0, concat_axis=0, tiled=...  14.5 us
    ppermute x3, starting transfers between devices, from_behind(): return lax.ppermute(block, axis, route)  8.77 us
    all_to_all x1, starting transfers between devices, on_device(): lax.all_to_all(package, ('gx', 'gy'), split_axis=0, concat_axis=0, tiled=...  5.62 us
    pallas_call x1, Pallas kernels, scatter_cells(): pl.pallas_call(functools.partial(scatter_kernel, map_rows), out_shape=jax...  4.73 us
    unnamed x18, local copies, waits for them, and re-layouts  3.74 us
    pallas_call x1, Pallas kernels, gather_cells(): pl.pallas_call(gather_kernel, out_shape=jax.ShapeDtypeStruct(local_map.sh...  2.03 us
  transfers between devices with their start and end apart: 5, of which 2 were waited for; matrix products, arithmetic and copies ran while one was open for 2% of the time, Pallas kernels for 0%

profile of v10, /device:TPU:1, one launch (start us, length us, event | category | flops | bytes accessed | tf_op | source)
XLA Modules:
  0.0 89.0 jit_solution(1347956269824350852)
XLA Ops:
  0.6 2.0 %shard_map.95 = f32[256,128]{1,0:T(8,128)} custom-call(f32[16,16,128]{2,1,0:T(8,128)} %sat_ref.1, s32[256,128]{1,0:T(8,128)} %bitcast.51), custom_call_target="tpu_custom_call" | custom-call | tf_op jit(solution)/shard_map/pallas_call | solution.py:71
  2.7 20.6 %all-to-all-start = ((f32[128,2,128]{2,1,0:T(2,128)}), f32[128,2,128]{2,1,0:T(2,128)S(1)}, u32[]{:S(2)}, u32[]{:S(2)}) async-start(f32[128,2,128]{2,1,0:T(2,128)} %bitcast.53), calls=%async_computation | async-start | bytes 262144 | tf_op jit(solution)/shard_map/all_to_all | solution.py:168
  23.2 0.0 copy-start.7
  23.2 0.6 copy-done.7
  23.9 0.1 fusion.4
  24.0 0.2 reduce_window_sum.11
  24.2 0.2 select_reduce_fusion
  24.4 0.3 broadcast_and_fusion
  24.7 0.2 and.36
  24.9 0.0 copy-start.6
  24.9 0.2 and.38
  25.1 0.7 copy-done.6
  25.7 0.6 copy-done.8
  26.4 0.2 copy-done.4
  26.6 0.3 fusion.1
  26.8 14.5 %all-to-all-done = f32[128,2,128]{2,1,0:T(2,128)S(1)} async-done(((f32[128,2,128]{2,1,0:T(2,128)}), f32[128,2,128]{2,1,0:T(2,128)S(1)}, u32[]{:S(2)}, u32[]{:S(2)}) %all-to-all-start) | async-done | bytes 131104 | tf_op jit(solution)/shard_map/all_to_all | solution.py:168
  41.3 0.3 fusion.8
  41.7 0.1 fusion.16
  41.8 0.1 add_divide_fusion.6
  41.9 0.1 fusion.15
  42.0 0.1 add_divide_fusion.5
  42.1 0.1 fusion.14
  42.2 0.1 add_divide_fusion.4
  42.3 0.1 fusion.13
  42.4 0.1 add_divide_fusion.3
  42.5 0.1 fusion.12
  42.6 0.1 add_divide_fusion.2
  42.7 0.1 fusion.11
  42.8 0.1 add_divide_fusion.1
  42.9 0.1 fusion.10
  43.0 0.1 add_divide_fusion
  43.1 0.1 fusion.9
  43.2 0.1 multiply_subtract_fusion
  43.3 0.0 copy-start.3
  43.3 0.0 copy-start
  43.3 0.0 copy-start.5
  43.3 1.0 %convolution_add_fusion = f32[512,128]{1,0:T(8,128)} fusion(f32[512,128]{1,0:T(8,128)S(1)} %fusion.1, pred[512,128]{1,0:T(32,128)(4,1)S(1)} %and.38, f32[1,128,128]{2,1,0:T(8,128)S(1)} %copy-done.4, f32[1,128,128]{2,1,0:T(8,128)S(1)} %reshape.123), kind=kOutput, calls=%fused_computation.5 | convolution fusion | flops 100745216 | bytes 720896 | tf_op jit(solution)/shard_map/dot_general | solution.py:198
  44.4 0.9 copy-done.2
  45.2 0.5 while.24
  45.8 3.1 %collective-permute-start = (f32[2,16,128]{2,1,0:T(8,128)S(1)}, f32[2,16,128]{2,1,0:T(8,128)S(1)}, u32[]{:S(2)}, u32[]{:S(2)}) collective-permute-start(f32[2,16,128]{2,1,0:T(8,128)S(1)} %pad_maximum_fusion), channel_id=1, source_target_pairs={{0,1},{1,2},{2,3},{4,5},{5,6},{6,7},{8,9},{9,10},{10,11},{12,13},{... | collective-permute-start | bytes 49160 | tf_op jit(solution)/shard_map/ppermute | solution.py:17
  48.9 4.4 %collective-permute-start.1 = (f32[2,16,128]{2,1,0:T(8,128)S(1)}, f32[2,16,128]{2,1,0:T(8,128)S(1)}, u32[]{:S(2)}, u32[]{:S(2)}) collective-permute-start(f32[2,16,128]{2,1,0:T(8,128)S(1)} %pad_maximum_fusion), channel_id=1, source_target_pairs={{0,2},{1,3},{4,6},{5,7},{8,10},{9,11},{12,14},{13,15},{16,18},{17,... | collective-permute-start | bytes 49160 | tf_op jit(solution)/shard_map/ppermute | solution.py:17
  53.2 1.3 %collective-permute-start.2 = (f32[2,16,128]{2,1,0:T(8,128)S(1)}, f32[2,16,128]{2,1,0:T(8,128)S(1)}, u32[]{:S(2)}, u32[]{:S(2)}) collective-permute-start(f32[2,16,128]{2,1,0:T(8,128)S(1)} %pad_maximum_fusion), channel_id=1, source_target_pairs={{0,3},{4,7},{8,11},{12,15},{16,19},{20,23},{24,27},{28,31},{32,35}... | collective-permute-start | bytes 49160 | tf_op jit(solution)/shard_map/ppermute | solution.py:17
  54.6 5.6 %all-to-all-start.1 = ((f32[128,4,128]{2,1,0:T(4,128)}), f32[128,4,128]{2,1,0:T(4,128)S(1)}, u32[]{:S(2)}, u32[]{:S(2)}) async-start(f32[128,4,128]{2,1,0:T(4,128)} %bitcast.10), calls=%async_computation.1 | async-start | bytes 524288 | tf_op jit(solution)/shard_map/all_to_all | solution.py:204
  60.2 0.0 collective-permute-done
  60.2 0.8 while.23
  61.1 22.6 %all-to-all-done.1 = f32[128,4,128]{2,1,0:T(4,128)S(1)} async-done(((f32[128,4,128]{2,1,0:T(4,128)}), f32[128,4,128]{2,1,0:T(4,128)S(1)}, u32[]{:S(2)}, u32[]{:S(2)}) %all-to-all-start.1) | async-done | bytes 262176 | tf_op jit(solution)/shard_map/all_to_all | solution.py:204
  83.6 0.7 copy-done.1
  84.3 4.7 %shard_map.96 = f32[16,16,128]{2,1,0:T(8,128)} custom-call(s32[256,128]{1,0:T(8,128)} %bitcast.52, f32[512,128]{1,0:T(8,128)} %bitcast.50, f32[16,16,128]{2,1,0:T(8,128)} %sat_ref.1, f32[16,16,128]{2,1,0:T(8,128)S(1)} %get-tuple-element.60.inflow_ref, f32[16,16,128]{2,1,0:T(8,128)S(1)} %get-tuple-element.222), custom_call_target="tpu_custom_call" | custom-call | tf_op jit(solution)/shard_map/pallas_call | solution.py:132
  (71 shorter events, 0.7 us)
Async XLA Ops:
  2.7 38.7 %all-to-all-start = ((f32[128,2,128]{2,1,0:T(2,128)}), f32[128,2,128]{2,1,0:T(2,128)S(1)}, u32[]{:S(2)}, u32[]{:S(2)}) async-start(f32[128,2,128]{2,1,0:T(2,128)} %bitcast.53), calls=%async_computation | async-start | bytes 262144 | tf_op jit(solution)/shard_map/all_to_all | solution.py:168
  23.2 0.7 copy-start.7
  24.9 0.8 copy-start.6
  25.7 0.7 copy-start.8
  25.7 0.9 copy-start.4
  43.3 1.0 %copy-start.3 = (f32[1,128,128]{2,1,0:T(8,128)}, f32[1,128,128]{2,1,0:T(8,128)S(1)}, u32[]{:S(2)}) copy-start(f32[1,128,128]{2,1,0:T(8,128)S(1)} %reshape.123) | copy-start | bytes 196612
  43.3 1.0 %copy-start = (f32[16,16,128]{2,1,0:T(8,128)S(1)}, f32[16,16,128]{2,1,0:T(8,128)}, u32[]{:S(2)}) copy-start(f32[16,16,128]{2,1,0:T(8,128)} %sat_ref.1) | copy-start | bytes 393220
  43.3 1.0 %copy-start.5 = (f32[16,16,128]{2,1,0:T(8,128)S(1)}, f32[16,16,128]{2,1,0:T(8,128)}, u32[]{:S(2)}) copy-start(f32[16,16,128]{2,1,0:T(8,128)} %param.14) | copy-start | bytes 393220
  44.3 0.9 %copy-start.2 = (f32[16,16,128]{2,1,0:T(8,128)S(1)}, f32[16,16,128]{2,1,0:T(8,128)}, u32[]{:S(2)}) copy-start(f32[16,16,128]{2,1,0:T(8,128)} %param.13) | copy-start | bytes 393220
  45.8 14.4 %collective-permute-start = (f32[2,16,128]{2,1,0:T(8,128)S(1)}, f32[2,16,128]{2,1,0:T(8,128)S(1)}, u32[]{:S(2)}, u32[]{:S(2)}) collective-permute-start(f32[2,16,128]{2,1,0:T(8,128)S(1)} %pad_maximum_fusion), channel_id=1, source_target_pairs={{0,1},{1,2},{2,3},{4,5},{5,6},{6,7},{8,9},{9,10},{10,11},{12,13},{... | collective-permute-start | bytes 49160 | tf_op jit(solution)/shard_map/ppermute | solution.py:17
  48.9 11.3 %collective-permute-start.1 = (f32[2,16,128]{2,1,0:T(8,128)S(1)}, f32[2,16,128]{2,1,0:T(8,128)S(1)}, u32[]{:S(2)}, u32[]{:S(2)}) collective-permute-start(f32[2,16,128]{2,1,0:T(8,128)S(1)} %pad_maximum_fusion), channel_id=1, source_target_pairs={{0,2},{1,3},{4,6},{5,7},{8,10},{9,11},{12,14},{13,15},{16,18},{17,... | collective-permute-start | bytes 49160 | tf_op jit(solution)/shard_map/ppermute | solution.py:17
  53.2 7.0 %collective-permute-start.2 = (f32[2,16,128]{2,1,0:T(8,128)S(1)}, f32[2,16,128]{2,1,0:T(8,128)S(1)}, u32[]{:S(2)}, u32[]{:S(2)}) collective-permute-start(f32[2,16,128]{2,1,0:T(8,128)S(1)} %pad_maximum_fusion), channel_id=1, source_target_pairs={{0,3},{4,7},{8,11},{12,15},{16,19},{20,23},{24,27},{28,31},{32,35}... | collective-permute-start | bytes 49160 | tf_op jit(solution)/shard_map/ppermute | solution.py:17
  54.6 29.1 %all-to-all-start.1 = ((f32[128,4,128]{2,1,0:T(4,128)}), f32[128,4,128]{2,1,0:T(4,128)S(1)}, u32[]{:S(2)}, u32[]{:S(2)}) async-start(f32[128,4,128]{2,1,0:T(4,128)} %bitcast.10), calls=%async_computation.1 | async-start | bytes 524288 | tf_op jit(solution)/shard_map/all_to_all | solution.py:204
  83.6 0.7 copy-start.1

commit v11 on v10

--- a/solution.py
+++ b/solution.py
@@ -25,11 +25,15 @@
     flipped = reversed_flag[..., None] == 1
     state = node_sat
     inlet = jnp.ones(state.shape[:-1] + (1,), jnp.float32)
+    lane = lax.broadcasted_iota(jnp.int32, state.shape, state.ndim - 1)
+    last = state.shape[-1] - 1
     for _ in range(BL_STEPS):
         flows = frac_flow(state)
-        from_left = jnp.concatenate([inlet, flows[..., :-1]], axis=-1)
-        from_right = jnp.concatenate([flows[..., 1:], inlet], axis=-1)
-        upstream = jnp.where(flipped, from_right, from_left)
+        left = jnp.concatenate([inlet, state[..., :-1]], axis=-1)
+        right = jnp.concatenate([state[..., 1:], inlet], axis=-1)
+        neighbour = jnp.where(flipped, right, left)
+        edge = jnp.where(flipped, lane == last, lane == 0)
+        upstream = jnp.where(edge, 1.0, frac_flow(neighbour))
         state = state - increments * (flows - upstream)
     return state
 

time: 89.5 us -> 89.5 us (level)
  no operation moved by 1% of the time
where the time goes in v11:
time: 89.5 us; the launch traced here: 89.1 us
  waiting for transfers between devices  37.1 us (41%)
  starting transfers between devices  34.9 us (39%)
  Pallas kernels  6.77 us (8%)
  local copies, waits for them, and re-layouts  4.7 us (5%)
  other arithmetic  2.32 us (3%)
  matrix products  1.5 us (2%)
  between operations  0.95 us (1%)
    all_to_all x1, waiting for transfers between devices, on_device(): lax.all_to_all(package, ('gx', 'gy'), split_axis=0, concat_axis=0, tiled=...  22.6 us
    all_to_all x1, starting transfers between devices, on_device(): lax.all_to_all(offered, ('gx', 'gy'), split_axis=0, concat_axis=0, tiled=...  20.6 us
    all_to_all x1, waiting for transfers between devices, on_device(): lax.all_to_all(offered, ('gx', 'gy'), split_axis=0, concat_axis=0, tiled=...  14.5 us
    ppermute x3, starting transfers between devices, from_behind(): return lax.ppermute(block, axis, route)  8.77 us
    all_to_all x1, starting transfers between devices, on_device(): lax.all_to_all(package, ('gx', 'gy'), split_axis=0, concat_axis=0, tiled=...  5.62 us
    pallas_call x1, Pallas kernels, scatter_cells(): pl.pallas_call(functools.partial(scatter_kernel, map_rows), out_shape=jax...  4.73 us
    unnamed x18, local copies, waits for them, and re-layouts  3.7 us
    pallas_call x1, Pallas kernels, gather_cells(): pl.pallas_call(gather_kernel, out_shape=jax.ShapeDtypeStruct(local_map.sh...  2.03 us
  transfers between devices with their start and end apart: 5, of which 2 were waited for; matrix products, arithmetic and copies ran while one was open for 2% of the time, Pallas kernels for 0%

profile of v11, /device:TPU:1, one launch (start us, length us, event | category | flops | bytes accessed | tf_op | source)
XLA Modules:
  0.0 89.1 jit_solution(9905116641500902833)
XLA Ops:
  0.6 2.0 %shard_map.95 = f32[256,128]{1,0:T(8,128)} custom-call(f32[16,16,128]{2,1,0:T(8,128)} %sat_ref.1, s32[256,128]{1,0:T(8,128)} %bitcast.51), custom_call_target="tpu_custom_call" | custom-call | tf_op jit(solution)/shard_map/pallas_call | solution.py:75
  2.7 20.6 %all-to-all-start = ((f32[128,2,128]{2,1,0:T(2,128)}), f32[128,2,128]{2,1,0:T(2,128)S(1)}, u32[]{:S(2)}, u32[]{:S(2)}) async-start(f32[128,2,128]{2,1,0:T(2,128)} %bitcast.53), calls=%async_computation | async-start | bytes 262144 | tf_op jit(solution)/shard_map/all_to_all | solution.py:172
  23.2 0.0 copy-start.7
  23.3 0.6 copy-done.7
  23.9 0.1 fusion.28
  24.0 0.2 reduce_window_sum.11
  24.2 0.2 select_reduce_fusion
  24.4 0.3 broadcast_and_fusion
  24.7 0.2 and.36
  24.9 0.0 copy-start.6
  24.9 0.2 and.38
  25.1 0.7 copy-done.6
  25.7 0.0 copy-start.8
  25.8 0.7 copy-done.8
  26.4 0.1 copy-done.4
  26.6 0.3 fusion.25
  26.8 14.5 %all-to-all-done = f32[128,2,128]{2,1,0:T(2,128)S(1)} async-done(((f32[128,2,128]{2,1,0:T(2,128)}), f32[128,2,128]{2,1,0:T(2,128)S(1)}, u32[]{:S(2)}, u32[]{:S(2)}) %all-to-all-start) | async-done | bytes 131104 | tf_op jit(solution)/shard_map/all_to_all | solution.py:172
  41.3 0.3 fusion.32
  41.7 0.1 fusion.40
  41.7 0.1 fusion.2
  41.9 0.1 fusion.39
  41.9 0.1 fusion.5
  42.1 0.1 fusion.38
  42.2 0.1 fusion.8
  42.3 0.1 fusion.37
  42.4 0.1 fusion.11
  42.5 0.1 fusion.36
  42.6 0.1 fusion.14
  42.7 0.1 fusion.35
  42.8 0.1 fusion.17
  42.9 0.1 fusion.34
  43.0 0.1 fusion.20
  43.1 0.1 fusion.33
  43.2 0.1 fusion.23
  43.3 0.0 copy-start.3
  43.3 0.0 copy-start
  43.3 0.0 copy-start.5
  43.4 1.0 %convolution_add_fusion = f32[512,128]{1,0:T(8,128)} fusion(f32[512,128]{1,0:T(8,128)S(1)} %fusion.25, pred[512,128]{1,0:T(32,128)(4,1)S(1)} %and.38, f32[1,128,128]{2,1,0:T(8,128)S(1)} %copy-done.4, f32[1,128,128]{2,1,0:T(8,128)S(1)} %reshape.123), kind=kOutput, calls=%fused_computation.5 | convolution fusion | flops 100745216 | bytes 720896 | tf_op jit(solution)/shard_map/dot_general | solution.py:202
  44.4 0.9 copy-done.2
  45.2 0.5 while.24
  45.8 3.1 %collective-permute-start = (f32[2,16,128]{2,1,0:T(8,128)S(1)}, f32[2,16,128]{2,1,0:T(8,128)S(1)}, u32[]{:S(2)}, u32[]{:S(2)}) collective-permute-start(f32[2,16,128]{2,1,0:T(8,128)S(1)} %pad_maximum_fusion), channel_id=1, source_target_pairs={{0,1},{1,2},{2,3},{4,5},{5,6},{6,7},{8,9},{9,10},{10,11},{12,13},{... | collective-permute-start | bytes 49160 | tf_op jit(solution)/shard_map/ppermute | solution.py:17
  48.9 4.4 %collective-permute-start.1 = (f32[2,16,128]{2,1,0:T(8,128)S(1)}, f32[2,16,128]{2,1,0:T(8,128)S(1)}, u32[]{:S(2)}, u32[]{:S(2)}) collective-permute-start(f32[2,16,128]{2,1,0:T(8,128)S(1)} %pad_maximum_fusion), channel_id=1, source_target_pairs={{0,2},{1,3},{4,6},{5,7},{8,10},{9,11},{12,14},{13,15},{16,18},{17,... | collective-permute-start | bytes 49160 | tf_op jit(solution)/shard_map/ppermute | solution.py:17
  53.3 1.3 %collective-permute-start.2 = (f32[2,16,128]{2,1,0:T(8,128)S(1)}, f32[2,16,128]{2,1,0:T(8,128)S(1)}, u32[]{:S(2)}, u32[]{:S(2)}) collective-permute-start(f32[2,16,128]{2,1,0:T(8,128)S(1)} %pad_maximum_fusion), channel_id=1, source_target_pairs={{0,3},{4,7},{8,11},{12,15},{16,19},{20,23},{24,27},{28,31},{32,35}... | collective-permute-start | bytes 49160 | tf_op jit(solution)/shard_map/ppermute | solution.py:17
  54.6 5.6 %all-to-all-start.1 = ((f32[128,4,128]{2,1,0:T(4,128)}), f32[128,4,128]{2,1,0:T(4,128)S(1)}, u32[]{:S(2)}, u32[]{:S(2)}) async-start(f32[128,4,128]{2,1,0:T(4,128)} %bitcast.10), calls=%async_computation.1 | async-start | bytes 524288 | tf_op jit(solution)/shard_map/all_to_all | solution.py:208
  60.2 0.8 while.23
  61.1 22.6 %all-to-all-done.1 = f32[128,4,128]{2,1,0:T(4,128)S(1)} async-done(((f32[128,4,128]{2,1,0:T(4,128)}), f32[128,4,128]{2,1,0:T(4,128)S(1)}, u32[]{:S(2)}, u32[]{:S(2)}) %all-to-all-start.1) | async-done | bytes 262176 | tf_op jit(solution)/shard_map/all_to_all | solution.py:208
  83.6 0.7 copy-done.1
  84.3 4.7 %shard_map.96 = f32[16,16,128]{2,1,0:T(8,128)} custom-call(s32[256,128]{1,0:T(8,128)} %bitcast.52, f32[512,128]{1,0:T(8,128)} %bitcast.50, f32[16,16,128]{2,1,0:T(8,128)} %sat_ref.1, f32[16,16,128]{2,1,0:T(8,128)S(1)} %get-tuple-element.60.inflow_ref, f32[16,16,128]{2,1,0:T(8,128)S(1)} %get-tuple-element.210), custom_call_target="tpu_custom_call" | custom-call | tf_op jit(solution)/shard_map/pallas_call | solution.py:136
  (71 shorter events, 0.7 us)
Async XLA Ops:
  2.7 38.7 %all-to-all-start = ((f32[128,2,128]{2,1,0:T(2,128)}), f32[128,2,128]{2,1,0:T(2,128)S(1)}, u32[]{:S(2)}, u32[]{:S(2)}) async-start(f32[128,2,128]{2,1,0:T(2,128)} %bitcast.53), calls=%async_computation | async-start | bytes 262144 | tf_op jit(solution)/shard_map/all_to_all | solution.py:172
  23.2 0.7 copy-start.7
  24.9 0.8 copy-start.6
  25.7 0.8 copy-start.4
  25.7 0.7 copy-start.8
  43.3 1.0 %copy-start.3 = (f32[1,128,128]{2,1,0:T(8,128)}, f32[1,128,128]{2,1,0:T(8,128)S(1)}, u32[]{:S(2)}) copy-start(f32[1,128,128]{2,1,0:T(8,128)S(1)} %reshape.123) | copy-start | bytes 196612
  43.3 1.0 %copy-start = (f32[16,16,128]{2,1,0:T(8,128)S(1)}, f32[16,16,128]{2,1,0:T(8,128)}, u32[]{:S(2)}) copy-start(f32[16,16,128]{2,1,0:T(8,128)} %sat_ref.1) | copy-start | bytes 393220
  43.3 1.0 %copy-start.5 = (f32[16,16,128]{2,1,0:T(8,128)S(1)}, f32[16,16,128]{2,1,0:T(8,128)}, u32[]{:S(2)}) copy-start(f32[16,16,128]{2,1,0:T(8,128)} %param.14) | copy-start | bytes 393220
  44.3 0.9 %copy-start.2 = (f32[16,16,128]{2,1,0:T(8,128)S(1)}, f32[16,16,128]{2,1,0:T(8,128)}, u32[]{:S(2)}) copy-start(f32[16,16,128]{2,1,0:T(8,128)} %param.13) | copy-start | bytes 393220
  45.8 14.4 %collective-permute-start = (f32[2,16,128]{2,1,0:T(8,128)S(1)}, f32[2,16,128]{2,1,0:T(8,128)S(1)}, u32[]{:S(2)}, u32[]{:S(2)}) collective-permute-start(f32[2,16,128]{2,1,0:T(8,128)S(1)} %pad_maximum_fusion), channel_id=1, source_target_pairs={{0,1},{1,2},{2,3},{4,5},{5,6},{6,7},{8,9},{9,10},{10,11},{12,13},{... | collective-permute-start | bytes 49160 | tf_op jit(solution)/shard_map/ppermute | solution.py:17
  48.9 11.3 %collective-permute-start.1 = (f32[2,16,128]{2,1,0:T(8,128)S(1)}, f32[2,16,128]{2,1,0:T(8,128)S(1)}, u32[]{:S(2)}, u32[]{:S(2)}) collective-permute-start(f32[2,16,128]{2,1,0:T(8,128)S(1)} %pad_maximum_fusion), channel_id=1, source_target_pairs={{0,2},{1,3},{4,6},{5,7},{8,10},{9,11},{12,14},{13,15},{16,18},{17,... | collective-permute-start | bytes 49160 | tf_op jit(solution)/shard_map/ppermute | solution.py:17
  53.3 7.0 %collective-permute-start.2 = (f32[2,16,128]{2,1,0:T(8,128)S(1)}, f32[2,16,128]{2,1,0:T(8,128)S(1)}, u32[]{:S(2)}, u32[]{:S(2)}) collective-permute-start(f32[2,16,128]{2,1,0:T(8,128)S(1)} %pad_maximum_fusion), channel_id=1, source_target_pairs={{0,3},{4,7},{8,11},{12,15},{16,19},{20,23},{24,27},{28,31},{32,35}... | collective-permute-start | bytes 49160 | tf_op jit(solution)/shard_map/ppermute | solution.py:17
  54.6 29.1 %all-to-all-start.1 = ((f32[128,4,128]{2,1,0:T(4,128)}), f32[128,4,128]{2,1,0:T(4,128)S(1)}, u32[]{:S(2)}, u32[]{:S(2)}) async-start(f32[128,4,128]{2,1,0:T(4,128)} %bitcast.10), calls=%async_computation.1 | async-start | bytes 524288 | tf_op jit(solution)/shard_map/all_to_all | solution.py:208
  83.6 0.7 copy-start.1

commit v12 on v10

--- a/solution.py
+++ b/solution.py
@@ -80,7 +80,7 @@
     )(saturation, local_map)
 
 
-def scatter_kernel(map_rows, ids_ref, both_ref, sat_ref, inflow_ref, burden_ref, out_ref):
+def scatter_kernel(map_rows, ids_ref, hots_ref, both_ref, sat_ref, inflow_ref, burden_ref, out_ref):
     tiles = ids_ref.shape[0] // 8
     lanes = lax.broadcasted_iota(jnp.int32, (128, 128), 0)
     levels = lax.broadcasted_iota(jnp.int32, (map_rows, 128), 0)
@@ -100,7 +100,7 @@
         hots, parts = [], []
         for j in range(8):
             cell = ids[j : j + 1, :]
-            hots.append((jnp.bitwise_and(cell, 127) == lanes).astype(jnp.bfloat16))
+            hots.append(hots_ref[start + j])
             on_level = jnp.right_shift(cell, 7) == levels
             rows = jnp.concatenate(
                 [
@@ -129,12 +129,15 @@
 
 
 def scatter_cells(local_map, both, saturation, inflow, burden, map_rows):
+    lanes = lax.broadcasted_iota(jnp.int32, (1, 128, 1), 1)
+    hots = (jnp.bitwise_and(local_map, 127)[:, None, :] == lanes).astype(jnp.bfloat16)
     return pl.pallas_call(
         functools.partial(scatter_kernel, map_rows),
         out_shape=jax.ShapeDtypeStruct(saturation.shape, jnp.float32),
-        in_specs=[pl.BlockSpec(memory_space=pltpu.VMEM)] * 5,
+        in_specs=[pl.BlockSpec(memory_space=pltpu.VMEM)] * 6,
         out_specs=pl.BlockSpec(memory_space=pltpu.VMEM),
-    )(local_map, both, saturation, inflow, burden)
+        compiler_params=pltpu.CompilerParams(vmem_limit_bytes=40 * 1024 * 1024),
+    )(local_map, hots, both, saturation, inflow, burden)
 
 
 def segregation(saturation, retention, gravity):

time: 89.5 us -> 96.4 us (1.077)
  other arithmetic: 2.29 us -> 11.5 us
  waiting for transfers between devices: 37.1 us -> 34 us
  matrix products: 1.51 us -> 3.22 us
  Pallas kernels: 6.77 us -> 5.76 us
    convert_element_type x0 -> x1, other arithmetic: none -> 5.7 us  [scatter_cells(): (jnp.bitwise_and(local_map, 127)[:, None, :] == lanes).astype(jnp.bfloat16)]
    all_to_all x1, waiting for transfers between devices: 14.5 us -> 11.5 us  [on_device(): lax.all_to_all(offered, ('gx', 'gy'), split_axis=0, concat_axis=0, tiled=...]
    pallas_call x1, Pallas kernels: 4.73 us -> 3.68 us  [scatter_cells(): pl.pallas_call(functools.partial(scatter_kernel, map_rows), out_shape=jax...]
    unnamed x18 -> x12, local copies, waits for them, and re-layouts: 3.74 us -> 3.41 us
  transfers between devices with their start and end apart: 5 -> 5, of which waited for: 2 -> 2; matrix products, arithmetic and copies ran while one was open for 2% -> 13% of each run, Pallas kernels for 0% -> 0%
where the time goes in v12:
time: 96.4 us; the launch traced here: 95.9 us
  starting transfers between devices  34.3 us (36%)
  waiting for transfers between devices  34 us (35%)
  other arithmetic  11.5 us (12%)
  Pallas kernels  5.76 us (6%)
  local copies, waits for them, and re-layouts  5.25 us (5%)
  matrix products  3.22 us (3%)
    all_to_all x1, waiting for transfers between devices, on_device(): lax.all_to_all(package, ('gx', 'gy'), split_axis=0, concat_axis=0, tiled=...  22.6 us
    all_to_all x1, starting transfers between devices, on_device(): lax.all_to_all(offered, ('gx', 'gy'), split_axis=0, concat_axis=0, tiled=...  20.6 us
    all_to_all x1, waiting for transfers between devices, on_device(): lax.all_to_all(offered, ('gx', 'gy'), split_axis=0, concat_axis=0, tiled=...  11.5 us
    ppermute x3, starting transfers between devices, from_behind(): return lax.ppermute(block, axis, route)  8.16 us
    convert_element_type x1, other arithmetic, scatter_cells(): (jnp.bitwise_and(local_map, 127)[:, None, :] == lanes).astype(jnp.bfloat16)  5.7 us
    all_to_all x1, starting transfers between devices, on_device(): lax.all_to_all(package, ('gx', 'gy'), split_axis=0, concat_axis=0, tiled=...  5.61 us
    pallas_call x1, Pallas kernels, scatter_cells(): pl.pallas_call(functools.partial(scatter_kernel, map_rows), out_shape=jax...  3.68 us
    unnamed x12, local copies, waits for them, and re-layouts  3.41 us
  transfers between devices with their start and end apart: 5, of which 2 were waited for; matrix products, arithmetic and copies ran while one was open for 13% of the time, Pallas kernels for 0%

profile of v12, /device:TPU:1, one launch (start us, length us, event | category | flops | bytes accessed | tf_op | source)
XLA Modules:
  0.0 95.9 jit_solution(8331782760759377715)
XLA Ops:
  0.6 0.0 copy-start.1
  0.7 2.1 %shard_map.95 = f32[256,128]{1,0:T(8,128)} custom-call(f32[16,16,128]{2,1,0:T(8,128)} %sat_ref.1, s32[256,128]{1,0:T(8,128)} %bitcast.51), custom_call_target="tpu_custom_call" | custom-call | tf_op jit(solution)/shard_map/pallas_call | solution.py:71
  2.7 20.6 %all-to-all-start = ((f32[128,2,128]{2,1,0:T(2,128)}), f32[128,2,128]{2,1,0:T(2,128)S(1)}, u32[]{:S(2)}, u32[]{:S(2)}) async-start(f32[128,2,128]{2,1,0:T(2,128)} %bitcast.54), calls=%async_computation | async-start | bytes 262144 | tf_op jit(solution)/shard_map/all_to_all | solution.py:171
  23.3 0.7 fusion.5
  24.1 0.2 reduce_window_sum.11
  24.2 0.8 select_reduce_fusion
  25.1 0.7 multiply_add_fusion
  25.8 0.3 broadcast_and_fusion
  26.1 0.7 compare_bitcast_fusion
  26.7 0.9 reshape_squeeze.3
  27.6 0.2 and.50
  27.8 0.2 and.48
  27.9 0.9 broadcast_and_fusion.2
  28.9 1.1 %fusion.2 = f32[512,128]{1,0:T(8,128)S(1)} fusion(pred[512,128]{1,0:T(32,128)(4,1)S(1)} %and.48, f32[1,128,128]{2,1,0:T(8,128)} %param.18), kind=kOutput, calls=%fused_computation.21 | convolution fusion | flops 100663296 | bytes 393216 | tf_op jit(solution)/shard_map/dot_general | solution.py:181
  30.0 11.5 %all-to-all-done = f32[128,2,128]{2,1,0:T(2,128)S(1)} async-done(((f32[128,2,128]{2,1,0:T(2,128)}), f32[128,2,128]{2,1,0:T(2,128)S(1)}, u32[]{:S(2)}, u32[]{:S(2)}) %all-to-all-start) | async-done | bytes 131104 | tf_op jit(solution)/shard_map/all_to_all | solution.py:171
  41.4 0.3 fusion.9
  41.7 0.0 copy-start.2
  41.8 0.1 fusion.17
  41.9 0.1 add_divide_fusion.6
  42.0 0.1 fusion.16
  42.1 0.1 add_divide_fusion.5
  42.2 0.1 fusion.15
  42.3 0.1 add_divide_fusion.4
  42.4 0.1 fusion.14
  42.5 0.1 add_divide_fusion.3
  42.6 0.1 fusion.13
  42.7 0.1 add_divide_fusion.2
  42.8 0.1 fusion.12
  42.9 0.1 add_divide_fusion.1
  43.0 0.1 fusion.11
  43.1 0.1 add_divide_fusion
  43.2 0.1 fusion.10
  43.3 0.1 multiply_subtract_fusion
  43.4 0.0 copy-start.4
  43.4 1.8 %convolution_add_fusion = f32[512,128]{1,0:T(8,128)} fusion(f32[512,128]{1,0:T(8,128)S(1)} %fusion.2, pred[512,128]{1,0:T(32,128)(4,1)S(1)} %and.50, f32[1,128,128]{2,1,0:T(8,128)} %param.18, f32[1,128,128]{2,1,0:T(8,128)S(1)} %reshape.128), kind=kOutput, calls=%fused_computation.7 | convolution fusion | flops 100745216 | bytes 720896 | tf_op jit(solution)/shard_map/dot_general | solution.py:201
  45.3 0.5 while.24
  45.9 4.4 %collective-permute-start.2 = (f32[2,16,128]{2,1,0:T(8,128)S(1)}, f32[2,16,128]{2,1,0:T(8,128)S(1)}, u32[]{:S(2)}, u32[]{:S(2)}) collective-permute-start(f32[2,16,128]{2,1,0:T(8,128)S(1)} %pad_maximum_fusion), channel_id=1, source_target_pairs={{0,3},{4,7},{8,11},{12,15},{16,19},{20,23},{24,27},{28,31},{32,35}... | collective-permute-start | bytes 49160 | tf_op jit(solution)/shard_map/ppermute | solution.py:17
  50.3 1.3 %collective-permute-start.1 = (f32[2,16,128]{2,1,0:T(8,128)S(1)}, f32[2,16,128]{2,1,0:T(8,128)S(1)}, u32[]{:S(2)}, u32[]{:S(2)}) collective-permute-start(f32[2,16,128]{2,1,0:T(8,128)S(1)} %pad_maximum_fusion), channel_id=1, source_target_pairs={{0,2},{1,3},{4,6},{5,7},{8,10},{9,11},{12,14},{13,15},{16,18},{17,... | collective-permute-start | bytes 49160 | tf_op jit(solution)/shard_map/ppermute | solution.py:17
  51.6 2.5 %collective-permute-start = (f32[2,16,128]{2,1,0:T(8,128)S(1)}, f32[2,16,128]{2,1,0:T(8,128)S(1)}, u32[]{:S(2)}, u32[]{:S(2)}) collective-permute-start(f32[2,16,128]{2,1,0:T(8,128)S(1)} %pad_maximum_fusion), channel_id=1, source_target_pairs={{0,1},{1,2},{2,3},{4,5},{5,6},{6,7},{8,9},{9,10},{10,11},{12,13},{... | collective-permute-start | bytes 49160 | tf_op jit(solution)/shard_map/ppermute | solution.py:17
  54.1 5.7 %fusion.hots_ref = bf16[256,128,128]{2,1,0:T(8,128)(2,1)} fusion(s32[256,128]{1,0:T(8,128)S(1)} %broadcast_and_fusion.2), kind=kLoop, calls=%fused_computation.6 | loop fusion | flops 8388608 | bytes 8519680 | tf_op jit(solution)/shard_map/convert_element_type | solution.py:133
  59.8 5.6 %all-to-all-start.1 = ((f32[128,4,128]{2,1,0:T(4,128)}), f32[128,4,128]{2,1,0:T(4,128)S(1)}, u32[]{:S(2)}, u32[]{:S(2)}) async-start(f32[128,4,128]{2,1,0:T(4,128)} %bitcast.10), calls=%async_computation.1 | async-start | bytes 524288 | tf_op jit(solution)/shard_map/all_to_all | solution.py:207
  65.4 0.0 collective-permute-done.2
  65.4 0.0 collective-permute-done.1
  65.4 0.0 collective-permute-done
  65.4 0.8 while.23
  66.2 22.6 %all-to-all-done.1 = f32[128,4,128]{2,1,0:T(4,128)S(1)} async-done(((f32[128,4,128]{2,1,0:T(4,128)}), f32[128,4,128]{2,1,0:T(4,128)S(1)}, u32[]{:S(2)}, u32[]{:S(2)}) %all-to-all-start.1) | async-done | bytes 262176 | tf_op jit(solution)/shard_map/all_to_all | solution.py:207
  88.8 3.4 %copy-done = bf16[256,128,128]{2,1,0:T(8,128)(2,1)S(1)} copy-done((bf16[256,128,128]{2,1,0:T(8,128)(2,1)S(1)}, bf16[256,128,128]{2,1,0:T(8,128)(2,1)}, u32[]{:S(2)}) %copy-start) | copy-done | bytes 8388632
  92.2 3.7 %shard_map.96 = f32[16,16,128]{2,1,0:T(8,128)} custom-call(s32[256,128]{1,0:T(8,128)S(1)} %bitcast.52, bf16[256,128,128]{2,1,0:T(8,128)(2,1)S(1)} %copy-done, f32[512,128]{1,0:T(8,128)S(1)} %bitcast.53, f32[16,16,128]{2,1,0:T(8,128)S(1)} %copy-done.1, f32[16,16,128]{2,1,0:T(8,128)S(1)} %get-tuple-element.60.inflow_ref, f32[16,16,128]{2,1,0:T(8,128)S(1)} %get-tuple-element.222), custom_call_target="tpu_custom_call" | custom-call | tf_op jit(solution)/shard_map/pallas_call | solution.py:134
  (67 shorter events, 0.7 us)
Async XLA Ops:
  0.6 44.6 %copy-start.1 = (f32[16,16,128]{2,1,0:T(8,128)S(1)}, f32[16,16,128]{2,1,0:T(8,128)}, u32[]{:S(2)}) copy-start(f32[16,16,128]{2,1,0:T(8,128)} %sat_ref.1) | copy-start | bytes 393220
  0.6 44.6 %copy-start.5 = (f32[16,16,128]{2,1,0:T(8,128)S(1)}, f32[16,16,128]{2,1,0:T(8,128)}, u32[]{:S(2)}) copy-start(f32[16,16,128]{2,1,0:T(8,128)} %param.14) | copy-start | bytes 393220
  0.6 44.6 %copy-start.3 = (f32[16,16,128]{2,1,0:T(8,128)S(1)}, f32[16,16,128]{2,1,0:T(8,128)}, u32[]{:S(2)}) copy-start(f32[16,16,128]{2,1,0:T(8,128)} %param.13) | copy-start | bytes 393220
  2.7 38.7 %all-to-all-start = ((f32[128,2,128]{2,1,0:T(2,128)}), f32[128,2,128]{2,1,0:T(2,128)S(1)}, u32[]{:S(2)}, u32[]{:S(2)}) async-start(f32[128,2,128]{2,1,0:T(2,128)} %bitcast.54), calls=%async_computation | async-start | bytes 262144 | tf_op jit(solution)/shard_map/all_to_all | solution.py:171
  41.7 47.1 %copy-start.2 = (s32[1,256,128]{2,1,0:T(8,128)S(1)}, s32[1,256,128]{2,1,0:T(8,128)}, u32[]{:S(2)}) copy-start(s32[1,256,128]{2,1,0:T(8,128)} %param.15) | copy-start | bytes 393220
  43.4 52.5 %copy-start.4 = (f32[1,128,128]{2,1,0:T(8,128)}, f32[1,128,128]{2,1,0:T(8,128)S(1)}, u32[]{:S(2)}) copy-start(f32[1,128,128]{2,1,0:T(8,128)S(1)} %reshape.128) | copy-start | bytes 196612
  45.9 19.5 %collective-permute-start.2 = (f32[2,16,128]{2,1,0:T(8,128)S(1)}, f32[2,16,128]{2,1,0:T(8,128)S(1)}, u32[]{:S(2)}, u32[]{:S(2)}) collective-permute-start(f32[2,16,128]{2,1,0:T(8,128)S(1)} %pad_maximum_fusion), channel_id=1, source_target_pairs={{0,3},{4,7},{8,11},{12,15},{16,19},{20,23},{24,27},{28,31},{32,35}... | collective-permute-start | bytes 49160 | tf_op jit(solution)/shard_map/ppermute | solution.py:17
  50.3 15.1 %collective-permute-start.1 = (f32[2,16,128]{2,1,0:T(8,128)S(1)}, f32[2,16,128]{2,1,0:T(8,128)S(1)}, u32[]{:S(2)}, u32[]{:S(2)}) collective-permute-start(f32[2,16,128]{2,1,0:T(8,128)S(1)} %pad_maximum_fusion), channel_id=1, source_target_pairs={{0,2},{1,3},{4,6},{5,7},{8,10},{9,11},{12,14},{13,15},{16,18},{17,... | collective-permute-start | bytes 49160 | tf_op jit(solution)/shard_map/ppermute | solution.py:17
  51.6 13.8 %collective-permute-start = (f32[2,16,128]{2,1,0:T(8,128)S(1)}, f32[2,16,128]{2,1,0:T(8,128)S(1)}, u32[]{:S(2)}, u32[]{:S(2)}) collective-permute-start(f32[2,16,128]{2,1,0:T(8,128)S(1)} %pad_maximum_fusion), channel_id=1, source_target_pairs={{0,1},{1,2},{2,3},{4,5},{5,6},{6,7},{8,9},{9,10},{10,11},{12,13},{... | collective-permute-start | bytes 49160 | tf_op jit(solution)/shard_map/ppermute | solution.py:17
  59.8 29.0 %all-to-all-start.1 = ((f32[128,4,128]{2,1,0:T(4,128)}), f32[128,4,128]{2,1,0:T(4,128)S(1)}, u32[]{:S(2)}, u32[]{:S(2)}) async-start(f32[128,4,128]{2,1,0:T(4,128)} %bitcast.10), calls=%async_computation.1 | async-start | bytes 524288 | tf_op jit(solution)/shard_map/all_to_all | solution.py:207
  88.8 3.4 %copy-start = (bf16[256,128,128]{2,1,0:T(8,128)(2,1)S(1)}, bf16[256,128,128]{2,1,0:T(8,128)(2,1)}, u32[]{:S(2)}) copy-start(bf16[256,128,128]{2,1,0:T(8,128)(2,1)} %fusion.hots_ref) | copy-start | bytes 25165828

commit v13 on v10

--- a/solution.py
+++ b/solution.py
@@ -71,12 +71,12 @@
     return pl.pallas_call(
         gather_kernel,
         out_shape=jax.ShapeDtypeStruct(local_map.shape, jnp.float32),
-        grid=(1,),
+        grid=(2,),
         in_specs=[
             pl.BlockSpec((1, map_rows, 128), lambda i: (0, 0, 0)),
-            pl.BlockSpec(local_map.shape, lambda i: (0, 0)),
+            pl.BlockSpec((local_map.shape[0] // 2, 128), lambda i: (i, 0)),
         ],
-        out_specs=pl.BlockSpec(local_map.shape, lambda i: (0, 0)),
+        out_specs=pl.BlockSpec((local_map.shape[0] // 2, 128), lambda i: (i, 0)),
     )(saturation, local_map)
 
 

time: 89.5 us -> 89.5 us (level)
  no operation moved by 1% of the time
where the time goes in v13:
time: 89.5 us; the launch traced here: 89 us
  waiting for transfers between devices  37.1 us (41%)
  starting transfers between devices  34.9 us (39%)
  Pallas kernels  6.76 us (8%)
  local copies, waits for them, and re-layouts  4.74 us (5%)
  other arithmetic  2.29 us (3%)
  matrix products  1.51 us (2%)
  between operations  0.95 us (1%)
    all_to_all x1, waiting for transfers between devices, on_device(): lax.all_to_all(package, ('gx', 'gy'), split_axis=0, concat_axis=0, tiled=...  22.6 us
    all_to_all x1, starting transfers between devices, on_device(): lax.all_to_all(offered, ('gx', 'gy'), split_axis=0, concat_axis=0, tiled=...  20.6 us
    all_to_all x1, waiting for transfers between devices, on_device(): lax.all_to_all(offered, ('gx', 'gy'), split_axis=0, concat_axis=0, tiled=...  14.5 us
    ppermute x3, starting transfers between devices, from_behind(): return lax.ppermute(block, axis, route)  8.76 us
    all_to_all x1, starting transfers between devices, on_device(): lax.all_to_all(package, ('gx', 'gy'), split_axis=0, concat_axis=0, tiled=...  5.62 us
    pallas_call x1, Pallas kernels, scatter_cells(): pl.pallas_call(functools.partial(scatter_kernel, map_rows), out_shape=jax...  4.73 us
    unnamed x18, local copies, waits for them, and re-layouts  3.74 us
    pallas_call x1, Pallas kernels, gather_cells(): pl.pallas_call(gather_kernel, out_shape=jax.ShapeDtypeStruct(local_map.sh...  2.03 us
  transfers between devices with their start and end apart: 5, of which 2 were waited for; matrix products, arithmetic and copies ran while one was open for 2% of the time, Pallas kernels for 0%

profile of v13, /device:TPU:1, one launch (start us, length us, event | category | flops | bytes accessed | tf_op | source)
XLA Modules:
  0.0 89.0 jit_solution(9671413015921395570)
XLA Ops:
  0.6 2.0 %shard_map.95 = f32[256,128]{1,0:T(8,128)} custom-call(f32[16,16,128]{2,1,0:T(8,128)} %sat_ref.1, s32[256,128]{1,0:T(8,128)} %bitcast.51), custom_call_target="tpu_custom_call" | custom-call | tf_op jit(solution)/shard_map/pallas_call | solution.py:71
  2.7 20.6 %all-to-all-start = ((f32[128,2,128]{2,1,0:T(2,128)}), f32[128,2,128]{2,1,0:T(2,128)S(1)}, u32[]{:S(2)}, u32[]{:S(2)}) async-start(f32[128,2,128]{2,1,0:T(2,128)} %bitcast.53), calls=%async_computation | async-start | bytes 262144 | tf_op jit(solution)/shard_map/all_to_all | solution.py:168
  23.2 0.0 copy-start.7
  23.2 0.6 copy-done.7
  23.9 0.1 fusion.4
  24.0 0.2 reduce_window_sum.11
  24.1 0.2 select_reduce_fusion
  24.4 0.3 broadcast_and_fusion
  24.7 0.2 and.36
  24.9 0.0 copy-start.6
  24.9 0.2 and.38
  25.1 0.7 copy-done.6
  25.7 0.6 copy-done.8
  26.4 0.2 copy-done.4
  26.6 0.3 fusion.1
  26.8 14.5 %all-to-all-done = f32[128,2,128]{2,1,0:T(2,128)S(1)} async-done(((f32[128,2,128]{2,1,0:T(2,128)}), f32[128,2,128]{2,1,0:T(2,128)S(1)}, u32[]{:S(2)}, u32[]{:S(2)}) %all-to-all-start) | async-done | bytes 131104 | tf_op jit(solution)/shard_map/all_to_all | solution.py:168
  41.3 0.3 fusion.8
  41.7 0.1 fusion.16
  41.8 0.1 add_divide_fusion.6
  41.9 0.1 fusion.15
  42.0 0.1 add_divide_fusion.5
  42.1 0.1 fusion.14
  42.2 0.1 add_divide_fusion.4
  42.3 0.1 fusion.13
  42.4 0.1 add_divide_fusion.3
  42.5 0.1 fusion.12
  42.6 0.1 add_divide_fusion.2
  42.7 0.1 fusion.11
  42.8 0.1 add_divide_fusion.1
  42.9 0.1 fusion.10
  43.0 0.1 add_divide_fusion
  43.1 0.1 fusion.9
  43.2 0.1 multiply_subtract_fusion
  43.3 0.0 copy-start.3
  43.3 0.0 copy-start
  43.3 0.0 copy-start.5
  43.3 1.0 %convolution_add_fusion = f32[512,128]{1,0:T(8,128)} fusion(f32[512,128]{1,0:T(8,128)S(1)} %fusion.1, pred[512,128]{1,0:T(32,128)(4,1)S(1)} %and.38, f32[1,128,128]{2,1,0:T(8,128)S(1)} %copy-done.4, f32[1,128,128]{2,1,0:T(8,128)S(1)} %reshape.123), kind=kOutput, calls=%fused_computation.5 | convolution fusion | flops 100745216 | bytes 720896 | tf_op jit(solution)/shard_map/dot_general | solution.py:198
  44.3 0.9 copy-done.2
  45.2 0.5 while.24
  45.7 3.1 %collective-permute-start = (f32[2,16,128]{2,1,0:T(8,128)S(1)}, f32[2,16,128]{2,1,0:T(8,128)S(1)}, u32[]{:S(2)}, u32[]{:S(2)}) collective-permute-start(f32[2,16,128]{2,1,0:T(8,128)S(1)} %pad_maximum_fusion), channel_id=1, source_target_pairs={{0,1},{1,2},{2,3},{4,5},{5,6},{6,7},{8,9},{9,10},{10,11},{12,13},{... | collective-permute-start | bytes 49160 | tf_op jit(solution)/shard_map/ppermute | solution.py:17
  48.9 4.4 %collective-permute-start.1 = (f32[2,16,128]{2,1,0:T(8,128)S(1)}, f32[2,16,128]{2,1,0:T(8,128)S(1)}, u32[]{:S(2)}, u32[]{:S(2)}) collective-permute-start(f32[2,16,128]{2,1,0:T(8,128)S(1)} %pad_maximum_fusion), channel_id=1, source_target_pairs={{0,2},{1,3},{4,6},{5,7},{8,10},{9,11},{12,14},{13,15},{16,18},{17,... | collective-permute-start | bytes 49160 | tf_op jit(solution)/shard_map/ppermute | solution.py:17
  53.2 1.3 %collective-permute-start.2 = (f32[2,16,128]{2,1,0:T(8,128)S(1)}, f32[2,16,128]{2,1,0:T(8,128)S(1)}, u32[]{:S(2)}, u32[]{:S(2)}) collective-permute-start(f32[2,16,128]{2,1,0:T(8,128)S(1)} %pad_maximum_fusion), channel_id=1, source_target_pairs={{0,3},{4,7},{8,11},{12,15},{16,19},{20,23},{24,27},{28,31},{32,35}... | collective-permute-start | bytes 49160 | tf_op jit(solution)/shard_map/ppermute | solution.py:17
  54.5 5.6 %all-to-all-start.1 = ((f32[128,4,128]{2,1,0:T(4,128)}), f32[128,4,128]{2,1,0:T(4,128)S(1)}, u32[]{:S(2)}, u32[]{:S(2)}) async-start(f32[128,4,128]{2,1,0:T(4,128)} %bitcast.10), calls=%async_computation.1 | async-start | bytes 524288 | tf_op jit(solution)/shard_map/all_to_all | solution.py:204
  60.2 0.0 collective-permute-done.2
  60.2 0.8 while.23
  61.0 22.6 %all-to-all-done.1 = f32[128,4,128]{2,1,0:T(4,128)S(1)} async-done(((f32[128,4,128]{2,1,0:T(4,128)}), f32[128,4,128]{2,1,0:T(4,128)S(1)}, u32[]{:S(2)}, u32[]{:S(2)}) %all-to-all-start.1) | async-done | bytes 262176 | tf_op jit(solution)/shard_map/all_to_all | solution.py:204
  83.6 0.7 copy-done.1
  84.3 4.7 %shard_map.96 = f32[16,16,128]{2,1,0:T(8,128)} custom-call(s32[256,128]{1,0:T(8,128)} %bitcast.52, f32[512,128]{1,0:T(8,128)} %bitcast.50, f32[16,16,128]{2,1,0:T(8,128)} %sat_ref.1, f32[16,16,128]{2,1,0:T(8,128)S(1)} %get-tuple-element.60.inflow_ref, f32[16,16,128]{2,1,0:T(8,128)S(1)} %get-tuple-element.222), custom_call_target="tpu_custom_call" | custom-call | tf_op jit(solution)/shard_map/pallas_call | solution.py:132
  (71 shorter events, 0.7 us)
Async XLA Ops:
  2.7 38.7 %all-to-all-start = ((f32[128,2,128]{2,1,0:T(2,128)}), f32[128,2,128]{2,1,0:T(2,128)S(1)}, u32[]{:S(2)}, u32[]{:S(2)}) async-start(f32[128,2,128]{2,1,0:T(2,128)} %bitcast.53), calls=%async_computation | async-start | bytes 262144 | tf_op jit(solution)/shard_map/all_to_all | solution.py:168
  23.2 0.7 copy-start.7
  24.9 0.8 copy-start.6
  25.7 0.7 copy-start.8
  25.7 0.9 copy-start.4
  43.3 1.0 %copy-start.3 = (f32[1,128,128]{2,1,0:T(8,128)}, f32[1,128,128]{2,1,0:T(8,128)S(1)}, u32[]{:S(2)}) copy-start(f32[1,128,128]{2,1,0:T(8,128)S(1)} %reshape.123) | copy-start | bytes 196612
  43.3 1.0 %copy-start = (f32[16,16,128]{2,1,0:T(8,128)S(1)}, f32[16,16,128]{2,1,0:T(8,128)}, u32[]{:S(2)}) copy-start(f32[16,16,128]{2,1,0:T(8,128)} %sat_ref.1) | copy-start | bytes 393220
  43.3 1.0 %copy-start.5 = (f32[16,16,128]{2,1,0:T(8,128)S(1)}, f32[16,16,128]{2,1,0:T(8,128)}, u32[]{:S(2)}) copy-start(f32[16,16,128]{2,1,0:T(8,128)} %param.14) | copy-start | bytes 393220
  44.3 0.9 %copy-start.2 = (f32[16,16,128]{2,1,0:T(8,128)S(1)}, f32[16,16,128]{2,1,0:T(8,128)}, u32[]{:S(2)}) copy-start(f32[16,16,128]{2,1,0:T(8,128)} %param.13) | copy-start | bytes 393220
  45.7 14.4 %collective-permute-start = (f32[2,16,128]{2,1,0:T(8,128)S(1)}, f32[2,16,128]{2,1,0:T(8,128)S(1)}, u32[]{:S(2)}, u32[]{:S(2)}) collective-permute-start(f32[2,16,128]{2,1,0:T(8,128)S(1)} %pad_maximum_fusion), channel_id=1, source_target_pairs={{0,1},{1,2},{2,3},{4,5},{5,6},{6,7},{8,9},{9,10},{10,11},{12,13},{... | collective-permute-start | bytes 49160 | tf_op jit(solution)/shard_map/ppermute | solution.py:17
  48.9 11.3 %collective-permute-start.1 = (f32[2,16,128]{2,1,0:T(8,128)S(1)}, f32[2,16,128]{2,1,0:T(8,128)S(1)}, u32[]{:S(2)}, u32[]{:S(2)}) collective-permute-start(f32[2,16,128]{2,1,0:T(8,128)S(1)} %pad_maximum_fusion), channel_id=1, source_target_pairs={{0,2},{1,3},{4,6},{5,7},{8,10},{9,11},{12,14},{13,15},{16,18},{17,... | collective-permute-start | bytes 49160 | tf_op jit(solution)/shard_map/ppermute | solution.py:17
  53.2 7.0 %collective-permute-start.2 = (f32[2,16,128]{2,1,0:T(8,128)S(1)}, f32[2,16,128]{2,1,0:T(8,128)S(1)}, u32[]{:S(2)}, u32[]{:S(2)}) collective-permute-start(f32[2,16,128]{2,1,0:T(8,128)S(1)} %pad_maximum_fusion), channel_id=1, source_target_pairs={{0,3},{4,7},{8,11},{12,15},{16,19},{20,23},{24,27},{28,31},{32,35}... | collective-permute-start | bytes 49160 | tf_op jit(solution)/shard_map/ppermute | solution.py:17
  54.5 29.1 %all-to-all-start.1 = ((f32[128,4,128]{2,1,0:T(4,128)}), f32[128,4,128]{2,1,0:T(4,128)S(1)}, u32[]{:S(2)}, u32[]{:S(2)}) async-start(f32[128,4,128]{2,1,0:T(4,128)} %bitcast.10), calls=%async_computation.1 | async-start | bytes 524288 | tf_op jit(solution)/shard_map/all_to_all | solution.py:204
  83.6 0.7 copy-start.1
